TPU v7x, 32 devices: a whole 2x2x4 slice. The times are simulated.
32 devices in a mesh: band: 2 (over x), spk: 16 (over z, y, core).
Axes of the slice: x: 2, y: 2, z: 4, core: 2. Of those that a mesh axis runs over, the one named last changes fastest.
Arguments:
- direction: float32 [64, 128, 128], P(('band', 'spk')), parts along dimension 0, may hold values from -6 to 6
- plant: bfloat16 [832, 2, 128, 128], P(('band', 'spk')), parts along dimension 0
- tile_pairs: int32 [832, 2], P(('band', 'spk')), parts along dimension 0, may hold values from 0 to 127, as said below
- mic_weight: float32 [2, 128, 128], P('band', 'spk'), parts along dimension 0, may hold values from 0.3 to 3
Outputs:
- hessian_vector: float32 [64, 128, 128], P(('band', 'spk')), parts along dimension 0
There are 2 independent parts, one for each index of `band`. A program takes and returns all parts, laid end to end along the dimension named above; each array names one. Nothing has to cross between parts.
Inputs may be any that keep to these rules, and one draw needn't show every extreme that they name: `tile_pairs`: column 0 is a speaker block, column 1 a microphone block. The rows of one device (aligned blocks of 26 rows) all lie in that device's bin, and their speaker blocks s satisfy s // 2 = (device index) % 16; no pair repeats on a device. Counting microphone blocks m by the device m * 16 // 128, at most 4 rows of one device fall to any one device, and in every part one device gets exactly 4 from every device.
All inputs are finite; a program needn't handle non-finite values.
Results may differ from a plain program's by a relative error of at most 0.0032.
Values may be sent and summed in bfloat16 or wider, within the bound.
No kernel may reach another device: no remote copies, remote signals or barrier semaphores. Data moves between devices by JAX's collectives and lax.ppermute only.
A program may use at most 128 MiB of HBM per device.

v0:
```python
import jax
import jax.numpy as jnp
from jax import lax
from jax.sharding import PartitionSpec as P

SBLK = 32
MBLK = 128
SPEAKERS = 4096


reg_weight = 0.25


def complex_forward(plant, field_rows):
    halfway = field_rows.shape[-1] // 2
    product = jnp.einsum("tcij,tjk->tcik", plant, field_rows, preferred_element_type=jnp.float32)
    real_part = product[:, 0, :, :halfway] - product[:, 1, :, halfway:]
    imag_part = product[:, 0, :, halfway:] + product[:, 1, :, :halfway]
    return jnp.concatenate([real_part, imag_part], axis=-1)


def complex_adjoint(plant, field_rows):
    halfway = field_rows.shape[-1] // 2
    product = jnp.einsum("tcij,tik->tcjk", plant, field_rows, preferred_element_type=jnp.float32)
    real_part = product[:, 0, :, :halfway] + product[:, 1, :, halfway:]
    imag_part = product[:, 0, :, halfway:] - product[:, 1, :, :halfway]
    return jnp.concatenate([real_part, imag_part], axis=-1)


def per_device(direction, plant, tile_pairs, mic_weight):
    devices = lax.axis_size("spk")
    device_id = lax.axis_index("spk")
    unit_count = direction.shape[0]
    tile_count = plant.shape[0]
    block_size = direction.shape[1]
    field_width = direction.shape[2]
    groups_per_bin = SBLK // unit_count
    bin_count = devices // groups_per_bin
    peer_blocks = MBLK // devices
    mic_units = bin_count * peer_blocks
    my_bin = device_id // groups_per_bin
    local_unit = tile_pairs[:, 0] % unit_count
    mic_block = tile_pairs[:, 1]
    direction_rows = direction.astype(jnp.bfloat16)[local_unit]
    partial_field = complex_forward(plant, direction_rows)
    local_power = jnp.sum(jnp.square(plant.astype(jnp.float32)))
    power_terms = jnp.where(jnp.arange(bin_count) == my_bin, local_power, 0.0)
    bin_power = lax.psum(power_terms, "spk")
    weights_flat = mic_weight.reshape(mic_units, block_size)
    capacity = max(3, (2 * tile_count + devices - 1) // devices)
    target_peer = mic_block // peer_blocks
    peer_onehot = (target_peer[:, None] == jnp.arange(devices)[None, :]).astype(jnp.int32)
    running = jnp.cumsum(peer_onehot, axis=0)
    slot_rank = jnp.take_along_axis(running, target_peer[:, None], axis=1)[:, 0] - 1
    position = target_peer * capacity + slot_rank
    target_label = my_bin * peer_blocks + mic_block - target_peer * peer_blocks
    outgoing = (
        jnp.zeros((devices * capacity, block_size, field_width), jnp.float32)
        .at[position]
        .set(partial_field)
    )
    labels = jnp.full((devices * capacity,), mic_units, jnp.int32).at[position].set(target_label)
    labels_in = lax.all_to_all(
        labels.reshape(devices, capacity), "spk", split_axis=0, concat_axis=0, tiled=True
    )
    arrived = lax.all_to_all(
        outgoing.reshape(devices, capacity, block_size, field_width),
        "spk",
        split_axis=0,
        concat_axis=0,
        tiled=True,
    )
    flat_labels = labels_in.reshape(devices * capacity)
    pressure = jax.ops.segment_sum(
        arrived.reshape(devices * capacity, block_size, field_width),
        flat_labels,
        num_segments=mic_units + 1,
    )[:mic_units]
    weighted = (weights_flat[:, :, None] * pressure).astype(jnp.bfloat16)
    clipped = jnp.minimum(flat_labels, mic_units - 1)
    reply = weighted[clipped].reshape(devices, capacity, block_size, field_width)
    returned = lax.all_to_all(reply, "spk", split_axis=0, concat_axis=0, tiled=True)
    tile_weighted = returned.reshape(devices * capacity, block_size, field_width)[position]
    back_field = complex_adjoint(plant, tile_weighted)
    unit_onehot = (local_unit[:, None] == jnp.arange(unit_count)[None, :]).astype(jnp.float32)
    gram = jnp.einsum("tu,tjk->ujk", unit_onehot, back_field, precision=lax.Precision.HIGHEST)
    my_power = bin_power[my_bin]
    return gram + reg_weight * my_power / SPEAKERS * direction


def solution(mesh):
    placed = (
        P(("band", "spk"), None, None),
        P(("band", "spk"), None, None, None),
        P(("band", "spk"), None),
        P("band", "spk", None),
    )
    return jax.shard_map(
        per_device,
        mesh=mesh,
        in_specs=placed,
        out_specs=P(("band", "spk"), None, None),
        check_vma=False,
    )
```

profile of v0, /device:TPU:13, one launch (start us, length us, event | category | flops | bytes accessed | tf_op | source)
XLA Modules:
  0.0 210.9 jit_solution(8495858670104442344)
XLA Ops:
  0.0 0.0 copy-start
  0.0 0.8 fusion.16
  0.9 0.7 fusion.18
  1.5 0.1 fusion.9
  1.7 0.8 gather_fusion.3
  2.5 0.7 scatter_custom_fusion
  3.2 0.7 all_to_all.12
  3.9 6.5 %all-to-all-start = ((s32[16,1,4]{2,1,0:T(1,128)}), s32[16,1,4]{2,1,0:T(1,128)S(1)}, u32[]{:S(2)}, u32[]{:S(2)}) async-start(s32[16,1,4]{2,1,0:T(1,128)} %bitcast.10), calls=%async_computation | async-start | bytes 16384 | tf_op jit(solution)/shard_map/all_to_all | solution.py:63
  10.4 0.9 convert_element_type.14
  11.3 0.7 gather_fusion
  12.0 0.0 copy-done
  12.0 0.7 convolution_bitcast_fusion.1
  12.7 0.1 fusion.3
  12.8 0.1 fusion.5
  12.9 0.2 pad_maximum_fusion
  13.1 1.7 copy.38
  14.8 0.0 copy-start.1
  14.8 2.4 %broadcast_in_dim.9 = f32[64,128,128]{2,1,0:T(8,128)} broadcast(f32[]{:T(128)} %constant.79.clone.1), dimensions={} | broadcast | bytes 4194308 | tf_op jit(solution)/shard_map/broadcast_in_dim | solution.py:58
  17.2 0.0 copy-done.1
  17.2 5.3 %scatter_fusion = f32[64,128,128]{2,1,0:T(8,128)} fusion(f32[64,128,128]{2,1,0:T(8,128)} %broadcast_in_dim.9, s32[26]{0:T(128)S(1)} %fusion.15, f32[26,128,128]{2,1,0:T(8,128)S(1)} %copy-done.1), kind=kCustom, calls=%fused_computation.5 | custom fusion | bytes 5111912 | tf_op jit(solution)/shard_map/scatter | solution.py:60
  22.6 0.0 all-to-all-done
  22.6 6.0 %all-to-all-start.1 = ((f32[16,4,128,128]{3,2,1,0:T(8,128)}), f32[16,4,128,128]{3,2,1,0:T(8,128)}, u32[]{:S(2)}, u32[]{:S(2)}) async-start(f32[16,4,128,128]{3,2,1,0:T(8,128)} %bitcast.87), calls=%async_computation.1 | async-start | bytes 8388608 | tf_op jit(solution)/shard_map/all_to_all | solution.py:66
  28.6 0.5 broadcast.181
  29.1 0.7 minimum_reduce_fusion
  29.8 0.1 reshape.124
  29.9 0.1 reshape.132
  30.0 91.1 %all-to-all-done.1 = f32[16,4,128,128]{3,2,1,0:T(8,128)} async-done(((f32[16,4,128,128]{3,2,1,0:T(8,128)}), f32[16,4,128,128]{3,2,1,0:T(8,128)}, u32[]{:S(2)}, u32[]{:S(2)}) %all-to-all-start.1) | async-done | bytes 4194336 | tf_op jit(solution)/shard_map/all_to_all | solution.py:66
  121.1 0.0 copy-start.3
  121.1 8.8 %scatter_fusion.1 = f32[9,128,128]{2,1,0:T(8,128)S(1)} fusion(f32[9,128,128]{2,1,0:T(8,128)S(1)} %broadcast_in_dim.8, s32[64]{0:T(128)S(1)} %reshape.124, f32[64,128,128]{2,1,0:T(8,128)} %bitcast.17), kind=kCustom, calls=%fused_computation.6 | custom fusion | flops 1048576 | bytes 12583168 | tf_op jit(solution)/shard_map/scatter-add | solution.py:74
  129.9 0.0 copy-done.3
  129.9 0.2 fusion.8
  130.1 2.1 %gather_fusion.1 = bf16[64,128,128]{2,1,0:T(8,128)(2,1)} fusion(bf16[8,128,128]{2,1,0:T(8,128)(2,1)S(1)} %fusion.8, s32[1024]{0:T(1024)S(1)} %pad_clamp_fusion.1), kind=kCustom, calls=%fused_computation.1 | custom fusion | bytes 4194560 | tf_op jit(solution)/shard_map/gather | solution.py:81
  132.2 4.8 %all-to-all-start.2 = ((bf16[16,4,128,128]{3,2,1,0:T(8,128)(2,1)}), bf16[16,4,128,128]{3,2,1,0:T(8,128)(2,1)}, u32[]{:S(2)}, u32[]{:S(2)}) async-start(bf16[16,4,128,128]{3,2,1,0:T(8,128)(2,1)} %bitcast.88), calls=%async_computation.2 | async-start | bytes 4194304 | tf_op jit(solution)/shard_map/all_to_all | solution.py:82
  137.0 1.5 multiply_reduce_fusion
  139.1 62.4 %psum.7 = f32[1]{0:T(128)} all-reduce(f32[1]{0:T(128)} %bitcast.25), channel_id=1, replica_groups=mesh['band'=2,'spk'=16] {'spk'}, use_global_device_ids=true, to_apply=%region_5.6 | all-reduce | flops 1 | bytes 8 | tf_op jit(solution)/shard_map/psum | solution.py:48
  202.2 0.0 all-to-all-done.2
  202.2 2.3 %gather_fusion.2 = bf16[26,128,128]{2,1,0:T(8,128)(2,1)S(1)} fusion(bf16[64,128,128]{2,1,0:T(8,128)(2,1)} %bitcast.20, s32[1024]{0:T(1024)S(1)} %pad_clamp_fusion), kind=kCustom, calls=%fused_computation.2 | custom fusion | bytes 1704040 | tf_op jit(solution)/shard_map/gather | solution.py:83
  204.5 0.7 convolution_bitcast_fusion
  205.2 0.1 fusion
  205.3 0.1 fusion.2
  205.5 0.1 pad_maximum_fusion.1
  205.6 0.0 copy-start.2
  205.6 2.2 %copy.42 = f32[26,128,128]{2,0,1:T(8,128)} copy(f32[26,128,128]{1,2,0:T(8,128)S(1)} %pad_maximum_fusion.1) | data formatting | bytes 3407872 | tf_op jit(solution)/shard_map/concatenate | solution.py:27
  207.8 2.4 %fusion.10 = f32[2,128,128]{2,0,1:T(2,128)S(1)} fusion(f32[26,128,128]{2,0,1:T(8,128)} %copy.42, s32[26]{0:T(128)S(1)} %bitcast.90), kind=kOutput, calls=%fused_computation.41 | convolution fusion | flops 10223668 | bytes 1835112 | tf_op jit(solution)/shard_map/tu,tjk->ujk/dot_general | solution.py:86
  210.2 0.0 copy-done.2
  210.2 0.7 copy_add_fusion
  (10 shorter events, 0.1 us)
Async XLA Ops:
  0.0 12.0 %copy-start = (bf16[26,2,128,128]{3,2,1,0:T(8,128)(2,1)S(1)}, bf16[26,2,128,128]{3,2,1,0:T(8,128)(2,1)}, u32[]{:S(2)}) copy-start(bf16[26,2,128,128]{3,2,1,0:T(8,128)(2,1)} %param.5) | copy-start | bytes 5111812
  3.9 18.7 %all-to-all-start = ((s32[16,1,4]{2,1,0:T(1,128)}), s32[16,1,4]{2,1,0:T(1,128)S(1)}, u32[]{:S(2)}, u32[]{:S(2)}) async-start(s32[16,1,4]{2,1,0:T(1,128)} %bitcast.10), calls=%async_computation | async-start | bytes 16384 | tf_op jit(solution)/shard_map/all_to_all | solution.py:63
  14.8 2.4 %copy-start.1 = (f32[26,128,128]{2,1,0:T(8,128)S(1)}, f32[26,128,128]{2,1,0:T(8,128)}, u32[]{:S(2)}) copy-start(f32[26,128,128]{2,1,0:T(8,128)} %copy.38) | copy-start | bytes 5111812
  22.6 98.5 %all-to-all-start.1 = ((f32[16,4,128,128]{3,2,1,0:T(8,128)}), f32[16,4,128,128]{3,2,1,0:T(8,128)}, u32[]{:S(2)}, u32[]{:S(2)}) async-start(f32[16,4,128,128]{3,2,1,0:T(8,128)} %bitcast.87), calls=%async_computation.1 | async-start | bytes 8388608 | tf_op jit(solution)/shard_map/all_to_all | solution.py:66
  121.1 8.8 %copy-start.3 = (f32[1,8,128]{2,1,0:T(8,128)S(1)}, f32[1,8,128]{2,1,0:T(8,128)}, u32[]{:S(2)}) copy-start(f32[1,8,128]{2,1,0:T(8,128)} %param.7) | copy-start | bytes 12292
  132.2 70.0 %all-to-all-start.2 = ((bf16[16,4,128,128]{3,2,1,0:T(8,128)(2,1)}), bf16[16,4,128,128]{3,2,1,0:T(8,128)(2,1)}, u32[]{:S(2)}, u32[]{:S(2)}) async-start(bf16[16,4,128,128]{3,2,1,0:T(8,128)(2,1)} %bitcast.88), calls=%async_computation.2 | async-start | bytes 4194304 | tf_op jit(solution)/shard_map/all_to_all | solution.py:82
  205.6 4.6 %copy-start.2 = (f32[2,128,128]{2,1,0:T(8,128)S(1)}, f32[2,128,128]{2,1,0:T(8,128)}, u32[]{:S(2)}) copy-start(f32[2,128,128]{2,1,0:T(8,128)} %param.4) | copy-start | bytes 393220
where the time goes:
time: 213 us; the launch traced here: 211 us
  waiting for transfers between devices  91.1 us (43%)
  blocking collectives  62.4 us (29%)
  local copies, waits for them, and re-layouts  19.6 us (9%)
  starting transfers between devices  17.3 us (8%)
  other arithmetic  15.2 us (7%)
  matrix products  3.67 us (2%)
    all_to_all x1, waiting for transfers between devices, per_device(): lax.all_to_all(outgoing.reshape(devices, capacity, block_size, field_widt...  91.1 us
    psum x1, blocking collectives, per_device(): bin_power = lax.psum(power_terms, 'spk')  62.4 us
    scatter-add x1, other arithmetic, per_device(): jax.ops.segment_sum(arrived.reshape(devices * capacity, block_size, field...  8.78 us
    all_to_all x1, starting transfers between devices, per_device(): lax.all_to_all(labels.reshape(devices, capacity), 'spk', split_axis=0, co...  6.52 us
    all_to_all x1, starting transfers between devices, per_device(): lax.all_to_all(outgoing.reshape(devices, capacity, block_size, field_widt...  6.04 us
    scatter x1, local copies, waits for them, and re-layouts, per_device(): outgoing = jnp.zeros((devices * capacity, block_size, field_width), jnp.f...  5.32 us
    all_to_all x1, starting transfers between devices, per_device(): lax.all_to_all(reply, 'spk', split_axis=0, concat_axis=0, tiled=True)  4.78 us
  transfers between devices with their start and end apart: 3, of which 1 were waited for; matrix products, arithmetic and copies ran while one was open for 7% of the time, Pallas kernels for 0%

commit v1 on v0

v1 whole, which is shorter than its diff:
```python
import jax
import jax.numpy as jnp
from jax import lax
from jax.sharding import PartitionSpec as P

SBLK = 32
MBLK = 128
SPEAKERS = 4096


reg_weight = 0.25


def complex_forward(plant, field_rows):
    halfway = field_rows.shape[-1] // 2
    product = jnp.einsum("tcij,tjk->tcik", plant, field_rows, preferred_element_type=jnp.float32)
    real_part = product[:, 0, :, :halfway] - product[:, 1, :, halfway:]
    imag_part = product[:, 0, :, halfway:] + product[:, 1, :, :halfway]
    return jnp.concatenate([real_part, imag_part], axis=-1)


def complex_adjoint(plant, field_rows):
    halfway = field_rows.shape[-1] // 2
    product = jnp.einsum("tcij,tik->tcjk", plant, field_rows, preferred_element_type=jnp.float32)
    real_part = product[:, 0, :, :halfway] + product[:, 1, :, halfway:]
    imag_part = product[:, 0, :, halfway:] - product[:, 1, :, :halfway]
    return jnp.concatenate([real_part, imag_part], axis=-1)


def slot_ranks(target_peer, devices):
    onehot = (target_peer[..., :, None] == jnp.arange(devices)).astype(jnp.int32)
    running = jnp.cumsum(onehot, axis=-2)
    return jnp.take_along_axis(running, target_peer[..., None], axis=-1)[..., 0] - 1


def select(onehot, blocks):
    return jnp.einsum("st,tjk->sjk", onehot.astype(blocks.dtype), blocks,
                      preferred_element_type=jnp.float32)


def per_device(direction, plant, tile_pairs, mic_weight):
    devices = lax.axis_size("spk")
    device_id = lax.axis_index("spk")
    unit_count = direction.shape[0]
    tile_count = plant.shape[0]
    block_size = direction.shape[1]
    groups_per_bin = SBLK // unit_count
    bin_count = devices // groups_per_bin
    peer_blocks = MBLK // devices
    mic_units = bin_count * peer_blocks
    my_bin = device_id // groups_per_bin
    capacity = max(3, (2 * tile_count + devices - 1) // devices)
    slots = devices * capacity

    local_power = jnp.sum(jnp.square(plant.astype(jnp.float32)))
    header = jnp.concatenate([tile_pairs.astype(jnp.float32).reshape(-1), local_power[None]])
    headers = lax.all_gather(header, "spk")
    all_pairs = headers[:, : 2 * tile_count].reshape(devices, tile_count, 2).astype(jnp.int32)
    source_bin = jnp.arange(devices) // groups_per_bin
    bin_power = jnp.sum(jnp.where(source_bin == my_bin, headers[:, -1], 0.0))

    local_unit = tile_pairs[:, 0] % unit_count
    mic_block = tile_pairs[:, 1]
    target_peer = mic_block // peer_blocks
    position = target_peer * capacity + slot_ranks(target_peer, devices)
    send_onehot = position[None, :] == jnp.arange(slots)[:, None]

    peer_of = all_pairs[:, :, 1] // peer_blocks
    rank_of = slot_ranks(peer_of, devices)
    label_of = source_bin[:, None] * peer_blocks + all_pairs[:, :, 1] - device_id * peer_blocks
    mine = peer_of == device_id
    slot_hit = mine[:, :, None] & (rank_of[:, :, None] == jnp.arange(capacity))
    label_hit = label_of[:, :, None] == jnp.arange(mic_units)
    recv_onehot = jnp.einsum("stj,stm->msj", slot_hit.astype(jnp.float32),
                             label_hit.astype(jnp.float32)).reshape(mic_units, slots)

    direction_rows = direction.astype(jnp.bfloat16)[local_unit]
    partial_field = complex_forward(plant, direction_rows).astype(jnp.bfloat16)
    outgoing = select(send_onehot, partial_field).astype(jnp.bfloat16)
    arrived = lax.all_to_all(
        outgoing.reshape(devices, capacity, block_size, -1), "spk", 0, 0, tiled=True
    ).reshape(slots, block_size, -1)
    pressure = select(recv_onehot, arrived)
    weights_flat = mic_weight.reshape(mic_units, block_size)
    weighted = (weights_flat[:, :, None] * pressure).astype(jnp.bfloat16)

    reply = select(recv_onehot.T, weighted).astype(jnp.bfloat16)
    returned = lax.all_to_all(
        reply.reshape(devices, capacity, block_size, -1), "spk", 0, 0, tiled=True
    ).reshape(slots, block_size, -1)
    tile_weighted = select(send_onehot.T, returned).astype(jnp.bfloat16)
    back_field = complex_adjoint(plant, tile_weighted)
    unit_onehot = (local_unit[:, None] == jnp.arange(unit_count)[None, :]).astype(jnp.float32)
    gram = jnp.einsum("tu,tjk->ujk", unit_onehot, back_field, precision=lax.Precision.HIGHEST)
    return gram + reg_weight * bin_power / SPEAKERS * direction


def solution(mesh):
    placed = (
        P(("band", "spk"), None, None),
        P(("band", "spk"), None, None, None),
        P(("band", "spk"), None),
        P("band", "spk", None),
    )
    return jax.shard_map(
        per_device,
        mesh=mesh,
        in_specs=placed,
        out_specs=P(("band", "spk"), None, None),
        check_vma=False,
    )
```

time: 213 us -> 160 us (0.75); the launches traced: 211 us -> 160 us
  waiting for transfers between devices: 91.1 us -> 46.1 us
  other arithmetic: 15.2 us -> 7.31 us
  matrix products: 3.67 us -> 10 us
  starting transfers between devices: 17.3 us -> 12.6 us
  local copies, waits for them, and re-layouts: 19.6 us -> 22.1 us
    psum x1 -> x0, blocking collectives: 62.4 us -> none  [per_device(): bin_power = lax.psum(power_terms, 'spk')]
    unnamed x0 -> x1, blocking collectives: none -> 60.3 us
    all_to_all x3 -> x2, waiting for transfers between devices: 91.1 us -> 46.1 us  [the longest x1 46.1 us: per_device(): lax.all_to_all(reply.reshape(devices, capacity, block_size, -1), 'spk', 0...]
    scatter-add x1 -> x0, other arithmetic: 8.78 us -> none  [per_device(): jax.ops.segment_sum(arrived.reshape(devices * capacity, block_size, field...]
    reshape x0 -> x3, local copies, waits for them, and re-layouts: none -> 6.31 us  [the longest x1 3.91 us: per_device(): reply.reshape(devices, capacity, block_size, -1)]
    dot_general x0 -> x4, matrix products: none -> 6.3 us  [the longest x3 6.15 us: select(): jnp.einsum('st,tjk->sjk', onehot.astype(blocks.dtype), blocks, preferred_...]
    scatter x2 -> x0, local copies, waits for them, and re-layouts: 5.97 us -> none  [the longest x1 5.32 us: per_device(): outgoing = jnp.zeros((devices * capacity, block_size, field_width), jnp.f...]
    all_to_all x3 -> x2, starting transfers between devices: 17.3 us -> 12.6 us  [the longest x1 6.66 us: per_device(): lax.all_to_all(outgoing.reshape(devices, capacity, block_size, -1), 'spk'...]
  transfers between devices with their start and end apart: 3 -> 2, of which waited for: 1 -> 1; matrix products, arithmetic and copies ran while one was open for 7% -> 7% of each run, Pallas kernels for 0% -> 0%
where the time goes in v1:
time: 160 us
  blocking collectives  60.3 us (38%)
  waiting for transfers between devices  46.1 us (29%)
  local copies, waits for them, and re-layouts  22.1 us (14%)
  starting transfers between devices  12.6 us (8%)
  matrix products  10 us (6%)
  other arithmetic  7.31 us (5%)
  between operations  1.61 us (1%)
    unnamed x1, blocking collectives  60.3 us
    all_to_all x1, waiting for transfers between devices, per_device(): lax.all_to_all(reply.reshape(devices, capacity, block_size, -1), 'spk', 0...  46.1 us
    gather x4, local copies, waits for them, and re-layouts, slot_ranks(): jnp.take_along_axis(running, target_peer[..., None], axis=-1)[..., 0] - 1  6.74 us
    all_to_all x1, starting transfers between devices, per_device(): lax.all_to_all(outgoing.reshape(devices, capacity, block_size, -1), 'spk'...  6.66 us
    dot_general x3, matrix products, select(): jnp.einsum('st,tjk->sjk', onehot.astype(blocks.dtype), blocks, preferred_...  6.15 us
    all_to_all x1, starting transfers between devices, per_device(): lax.all_to_all(reply.reshape(devices, capacity, block_size, -1), 'spk', 0...  5.93 us
    reshape x1, local copies, waits for them, and re-layouts, per_device(): reply.reshape(devices, capacity, block_size, -1)  3.91 us
  transfers between devices with their start and end apart: 2, of which 1 were waited for; matrix products, arithmetic and copies ran while one was open for 7% of the time, Pallas kernels for 0%

profile of v1, /device:TPU:13, one launch (start us, length us, event | category | flops | bytes accessed | tf_op | source)
XLA Modules:
  0.0 160.0 jit_solution(1801283176063942407)
XLA Ops:
  0.0 0.0 copy-start
  0.0 0.8 fusion.57
  0.9 0.9 convert_element_type.61
  1.8 0.7 gather_fusion
  2.5 0.0 copy-done
  2.5 0.7 convolution_bitcast_fusion.1
  3.2 0.0 copy-start.2
  3.2 0.1 fusion.23
  3.3 0.1 fusion.22
  3.5 0.1 fusion.32
  3.6 0.8 gather_fusion.1
  4.4 0.0 copy-done.2
  4.4 1.0 pad_maximum_fusion.1
  5.4 1.9 %copy.109 = bf16[26,128,128]{2,0,1:T(8,128)(2,1)S(1)} copy(bf16[26,128,128]{1,2,0:T(8,128)(2,1)} %pad_maximum_fusion.1) | data formatting | bytes 1703936 | tf_op jit(solution)/shard_map/concatenate | solution.py:19
  7.3 0.8 convolution_convert_fusion.1
  8.1 2.3 %copy.110 = bf16[16,4,128,128]{3,1,2,0:T(4,128)(2,1)} copy(bf16[16,4,128,128]{3,1,0,2:T(4,128)(2,1)S(1)} %bitcast.124) | data formatting | bytes 4194304 | tf_op jit(solution)/shard_map/reshape | solution.py:81
  10.4 0.0 copy-start.4
  10.4 6.7 %all-to-all-start = ((bf16[16,4,128,128]{3,1,2,0:T(4,128)(2,1)}), bf16[16,4,128,128]{3,1,2,0:T(4,128)(2,1)}, u32[]{:S(2)}, u32[]{:S(2)}) async-start(bf16[16,4,128,128]{3,1,2,0:T(4,128)(2,1)} %copy.110), calls=%async_computation | async-start | bytes 4194304 | tf_op jit(solution)/shard_map/all_to_all | solution.py:80
  17.1 0.0 copy-start.3
  17.1 0.1 copy.101
  17.2 0.1 reshape.124
  17.3 0.0 copy-done.4
  17.3 0.6 dynamic-slice
  18.6 1.5 multiply_reduce_fusion
  20.1 0.8 maximum_dynamic-update-slice_fusion
  20.9 60.3 %all-reduce = f32[848]{0:T(1024)S(1)} all-reduce(f32[848]{0:T(1024)S(1)} %maximum_dynamic-update-slice_fusion), channel_id=2, replica_groups=mesh['band'=2,'spk'=16] {'spk'}, use_global_device_ids=true, to_apply=%add | all-reduce | flops 848 | bytes 6784
  81.1 0.1 reshape.153
  81.2 0.1 copy.102
  81.4 0.1 copy.130
  81.5 0.1 reshape.147
  81.6 0.1 copy.104
  81.7 0.0 copy-done.3
  81.7 0.1 copy.105
  81.8 0.1 fusion.25
  81.9 5.8 %gather_fusion.2 = s32[416]{0:T(512)S(1)} fusion(s32[16,26,16]{2,0,1:T(8,128)S(1)} %fusion.25, s32[416]{0:T(512)S(1)} %reshape.147), kind=kCustom, calls=%fused_computation.2 | custom fusion | bytes 8320 | tf_op jit(solution)/shard_map/jit(take_along_axis)/gather | solution.py:33
  87.7 0.1 reshape.146
  87.8 0.1 add_bitcast_fusion.1
  87.9 0.1 convolution_convert_fusion.3
  88.1 0.1 copy.111
  88.2 0.0 all-to-all-done
  88.2 4.8 %convolution_convert_fusion = bf16[64,128,128]{2,0,1:T(8,128)(2,1)} fusion(bf16[8,64,1]{0,1,2:T(8,128)(2,1)S(1)} %bitcast.126, bf16[16,4,128,128]{3,1,2,0:T(4,128)(2,1)} %all-to-all-done, f32[8,128]{0,1:T(8,128)S(1)} %copy.105, bf16[8,16,4]{1,0,2:T(8,128)(2,1)S(1)} %copy.111), kind=kOutput, calls=%fused_computation.8 | convolution fusion | flops 34865152 | bytes 4200448 | tf_op jit(solution)/shard_map/st,tjk->sjk/dot_general | solution.py:37
  93.0 3.9 %copy.114 = bf16[16,4,128,128]{3,1,2,0:T(4,128)(2,1)} copy(bf16[16,4,128,128]{3,1,0,2:T(4,128)(2,1)} %bitcast.122) | data formatting | bytes 4194304 | tf_op jit(solution)/shard_map/reshape | solution.py:89
  96.9 5.9 %all-to-all-start.1 = ((bf16[16,4,128,128]{3,1,2,0:T(4,128)(2,1)}), bf16[16,4,128,128]{3,1,2,0:T(4,128)(2,1)}, u32[]{:S(2)}, u32[]{:S(2)}) async-start(bf16[16,4,128,128]{3,1,2,0:T(4,128)(2,1)} %copy.114), calls=%async_computation.1 | async-start | bytes 4194304 | tf_op jit(solution)/shard_map/all_to_all | solution.py:88
  102.9 0.2 slice_reduce_fusion
  103.0 0.6 fusion.53
  104.3 46.1 %all-to-all-done.1 = bf16[16,4,128,128]{3,1,2,0:T(4,128)(2,1)} async-done(((bf16[16,4,128,128]{3,1,2,0:T(4,128)(2,1)}), bf16[16,4,128,128]{3,1,2,0:T(4,128)(2,1)}, u32[]{:S(2)}, u32[]{:S(2)}) %all-to-all-start.1) | async-done | bytes 2097184 | tf_op jit(solution)/shard_map/all_to_all | solution.py:88
  150.4 2.8 %copy.115 = bf16[16,4,128,128]{3,1,0,2:T(4,128)(2,1)S(1)} copy(bf16[16,4,128,128]{3,1,2,0:T(4,128)(2,1)} %all-to-all-done.1) | data formatting | bytes 4194304 | tf_op jit(solution)/shard_map/all_to_all | solution.py:88
  153.1 0.5 fusion.2
  153.6 0.7 convolution_bitcast_fusion
  154.4 0.1 fusion.14
  154.5 0.1 fusion.16
  154.6 0.1 pad_maximum_fusion
  154.7 0.0 copy-start.1
  154.8 2.2 %copy.119 = f32[26,128,128]{2,0,1:T(8,128)} copy(f32[26,128,128]{1,2,0:T(8,128)S(1)} %pad_maximum_fusion) | data formatting | bytes 3407872 | tf_op jit(solution)/shard_map/concatenate | solution.py:27
  157.0 2.4 %fusion.49 = f32[2,128,128]{2,0,1:T(2,128)S(1)} fusion(f32[26,128,128]{2,0,1:T(8,128)} %copy.119, s32[26]{0:T(128)S(1)} %bitcast.129), kind=kOutput, calls=%fused_computation.81 | convolution fusion | flops 10223668 | bytes 1835112 | tf_op jit(solution)/shard_map/tu,tjk->ujk/dot_general | solution.py:94
  159.3 0.0 copy-done.1
  159.3 0.7 copy_add_fusion
  (18 shorter events, 0.2 us)
Async XLA Ops:
  0.0 2.5 %copy-start = (bf16[26,2,128,128]{3,2,1,0:T(8,128)(2,1)S(1)}, bf16[26,2,128,128]{3,2,1,0:T(8,128)(2,1)}, u32[]{:S(2)}) copy-start(bf16[26,2,128,128]{3,2,1,0:T(8,128)(2,1)} %param.5) | copy-start | bytes 5111812
  3.2 1.2 copy-start.2
  10.4 6.9 %copy-start.4 = (u32[32]{0:T(128)S(1)}, u32[32]{0:T(128)}, u32[]{:S(2)}) copy-start(u32[32]{0:T(128)} %constant.154) | copy-start | bytes 388
  10.4 77.7 %all-to-all-start = ((bf16[16,4,128,128]{3,1,2,0:T(4,128)(2,1)}), bf16[16,4,128,128]{3,1,2,0:T(4,128)(2,1)}, u32[]{:S(2)}, u32[]{:S(2)}) async-start(bf16[16,4,128,128]{3,1,2,0:T(4,128)(2,1)} %copy.110), calls=%async_computation | async-start | bytes 4194304 | tf_op jit(solution)/shard_map/all_to_all | solution.py:80
  17.1 64.6 %copy-start.3 = (f32[1,8,128]{2,1,0:T(8,128)S(1)}, f32[1,8,128]{2,1,0:T(8,128)}, u32[]{:S(2)}) copy-start(f32[1,8,128]{2,1,0:T(8,128)} %param.7) | copy-start | bytes 12292
  96.9 53.5 %all-to-all-start.1 = ((bf16[16,4,128,128]{3,1,2,0:T(4,128)(2,1)}), bf16[16,4,128,128]{3,1,2,0:T(4,128)(2,1)}, u32[]{:S(2)}, u32[]{:S(2)}) async-start(bf16[16,4,128,128]{3,1,2,0:T(4,128)(2,1)} %copy.114), calls=%async_computation.1 | async-start | bytes 4194304 | tf_op jit(solution)/shard_map/all_to_all | solution.py:88
  154.7 4.6 %copy-start.1 = (f32[2,128,128]{2,1,0:T(8,128)S(1)}, f32[2,128,128]{2,1,0:T(8,128)}, u32[]{:S(2)}) copy-start(f32[2,128,128]{2,1,0:T(8,128)} %param.4) | copy-start | bytes 393220

commit v2 on v1

--- a/solution.py
+++ b/solution.py
@@ -33,17 +33,13 @@
     return jnp.take_along_axis(running, target_peer[..., None], axis=-1)[..., 0] - 1
 
 
-def select(onehot, blocks):
-    return jnp.einsum("st,tjk->sjk", onehot.astype(blocks.dtype), blocks,
-                      preferred_element_type=jnp.float32)
-
-
 def per_device(direction, plant, tile_pairs, mic_weight):
     devices = lax.axis_size("spk")
     device_id = lax.axis_index("spk")
     unit_count = direction.shape[0]
     tile_count = plant.shape[0]
     block_size = direction.shape[1]
+    field_width = direction.shape[2]
     groups_per_bin = SBLK // unit_count
     bin_count = devices // groups_per_bin
     peer_blocks = MBLK // devices
@@ -55,6 +51,7 @@
     local_power = jnp.sum(jnp.square(plant.astype(jnp.float32)))
     header = jnp.concatenate([tile_pairs.astype(jnp.float32).reshape(-1), local_power[None]])
     headers = lax.all_gather(header, "spk")
+    headers, plant, direction = lax.optimization_barrier((headers, plant, direction))
     all_pairs = headers[:, : 2 * tile_count].reshape(devices, tile_count, 2).astype(jnp.int32)
     source_bin = jnp.arange(devices) // groups_per_bin
     bin_power = jnp.sum(jnp.where(source_bin == my_bin, headers[:, -1], 0.0))
@@ -63,32 +60,35 @@
     mic_block = tile_pairs[:, 1]
     target_peer = mic_block // peer_blocks
     position = target_peer * capacity + slot_ranks(target_peer, devices)
-    send_onehot = position[None, :] == jnp.arange(slots)[:, None]
+    send_hit = position[None, :] == jnp.arange(slots)[:, None]
+    slot_pair = jnp.where(
+        send_hit.any(axis=1), jnp.sum(jnp.where(send_hit, jnp.arange(tile_count), 0), axis=1), tile_count
+    )
 
     peer_of = all_pairs[:, :, 1] // peer_blocks
     rank_of = slot_ranks(peer_of, devices)
     label_of = source_bin[:, None] * peer_blocks + all_pairs[:, :, 1] - device_id * peer_blocks
-    mine = peer_of == device_id
-    slot_hit = mine[:, :, None] & (rank_of[:, :, None] == jnp.arange(capacity))
-    label_hit = label_of[:, :, None] == jnp.arange(mic_units)
-    recv_onehot = jnp.einsum("stj,stm->msj", slot_hit.astype(jnp.float32),
-                             label_hit.astype(jnp.float32)).reshape(mic_units, slots)
+    slot_hit = (peer_of == device_id)[:, :, None] & (rank_of[:, :, None] == jnp.arange(capacity))
+    slot_label = jnp.where(
+        slot_hit.any(axis=1), jnp.sum(jnp.where(slot_hit, label_of[:, :, None], 0), axis=1), mic_units
+    ).reshape(slots)
+    recv_onehot = (slot_label[None, :] == jnp.arange(mic_units)[:, None]).astype(jnp.bfloat16)
 
     direction_rows = direction.astype(jnp.bfloat16)[local_unit]
     partial_field = complex_forward(plant, direction_rows).astype(jnp.bfloat16)
-    outgoing = select(send_onehot, partial_field).astype(jnp.bfloat16)
+    outgoing = jnp.take(partial_field, slot_pair, axis=0, mode="fill", fill_value=0)
     arrived = lax.all_to_all(
-        outgoing.reshape(devices, capacity, block_size, -1), "spk", 0, 0, tiled=True
-    ).reshape(slots, block_size, -1)
-    pressure = select(recv_onehot, arrived)
+        outgoing.reshape(devices, capacity * block_size, field_width), "spk", 0, 0, tiled=True
+    ).reshape(slots, block_size, field_width)
+    pressure = jnp.einsum("ms,sjk->mjk", recv_onehot, arrived, preferred_element_type=jnp.float32)
     weights_flat = mic_weight.reshape(mic_units, block_size)
     weighted = (weights_flat[:, :, None] * pressure).astype(jnp.bfloat16)
 
-    reply = select(recv_onehot.T, weighted).astype(jnp.bfloat16)
+    reply = jnp.take(weighted, slot_label, axis=0, mode="fill", fill_value=0)
     returned = lax.all_to_all(
-        reply.reshape(devices, capacity, block_size, -1), "spk", 0, 0, tiled=True
-    ).reshape(slots, block_size, -1)
-    tile_weighted = select(send_onehot.T, returned).astype(jnp.bfloat16)
+        reply.reshape(devices, capacity * block_size, field_width), "spk", 0, 0, tiled=True
+    ).reshape(slots, block_size, field_width)
+    tile_weighted = jnp.take(returned, position, axis=0)
     back_field = complex_adjoint(plant, tile_weighted)
     unit_onehot = (local_unit[:, None] == jnp.arange(unit_count)[None, :]).astype(jnp.float32)
     gram = jnp.einsum("tu,tjk->ujk", unit_onehot, back_field, precision=lax.Precision.HIGHEST)

time: 160 us -> 181 us (1.13)
  waiting for transfers between devices: 46.1 us -> 86.1 us
  blocking collectives: 60.3 us -> 21.7 us
  other arithmetic: 7.31 us -> 19.5 us
  starting transfers between devices: 12.6 us -> 21.5 us
  matrix products: 10 us -> 6.83 us
    all_to_all x2, waiting for transfers between devices: 46.1 us -> 86.1 us  [the longest x1 46.1 us: per_device(): lax.all_to_all(reply.reshape(devices, capacity * block_size, field_width)...]
    unnamed x1, blocking collectives: 60.3 us -> 21.7 us
    gather x0 -> x4, local copies, waits for them, and re-layouts: none -> 10.7 us  [the longest x2 6.33 us: per_device(): jnp.take(partial_field, slot_pair, axis=0, mode='fill', fill_value=0)]
    all_to_all x2, starting transfers between devices: 12.6 us -> 21.5 us  [the longest x1 16.6 us: per_device(): lax.all_to_all(outgoing.reshape(devices, capacity * block_size, field_wid...]
    select_n x0 -> x4, other arithmetic: none -> 8.86 us  [the longest x2 4.45 us: per_device(): reply = jnp.take(weighted, slot_label, axis=0, mode='fill', fill_value=0)]
    reshape x2 -> x0, local copies, waits for them, and re-layouts: 6.22 us -> none  [the longest x1 3.91 us: per_device(): reply.reshape(devices, capacity, block_size, -1)]
    dot_general x4 -> x1, matrix products: 6.3 us -> 2.85 us  [per_device(): jnp.einsum('ms,sjk->mjk', recv_onehot, arrived, preferred_element_type=jn...]
    all_to_all x1 -> x0, local copies, waits for them, and re-layouts: 2.76 us -> none  [per_device(): lax.all_to_all(reply.reshape(devices, capacity, block_size, -1), 'spk', 0...]
  transfers between devices with their start and end apart: 2 -> 2, of which waited for: 1 -> 2; matrix products, arithmetic and copies ran while one was open for 7% -> 5% of each run, Pallas kernels for 0% -> 0%
where the time goes in v2:
time: 181 us; the launch traced here: 180 us
  waiting for transfers between devices  86.1 us (48%)
  local copies, waits for them, and re-layouts  22.7 us (13%)
  blocking collectives  21.7 us (12%)
  starting transfers between devices  21.5 us (12%)
  other arithmetic  19.5 us (11%)
  matrix products  6.83 us (4%)
    all_to_all x1, waiting for transfers between devices, per_device(): lax.all_to_all(reply.reshape(devices, capacity * block_size, field_width)...  46.1 us
    all_to_all x1, waiting for transfers between devices, per_device(): lax.all_to_all(outgoing.reshape(devices, capacity * block_size, field_wid...  40 us
    unnamed x1, blocking collectives  21.7 us
    all_to_all x1, starting transfers between devices, per_device(): lax.all_to_all(outgoing.reshape(devices, capacity * block_size, field_wid...  16.6 us
    gather x4, local copies, waits for them, and re-layouts, slot_ranks(): jnp.take_along_axis(running, target_peer[..., None], axis=-1)[..., 0] - 1  6.74 us
    gather x2, local copies, waits for them, and re-layouts, per_device(): jnp.take(partial_field, slot_pair, axis=0, mode='fill', fill_value=0)  6.33 us
    all_to_all x1, starting transfers between devices, per_device(): lax.all_to_all(reply.reshape(devices, capacity * block_size, field_width)...  4.89 us
    select_n x2, other arithmetic, per_device(): reply = jnp.take(weighted, slot_label, axis=0, mode='fill', fill_value=0)  4.45 us
  transfers between devices with their start and end apart: 2, of which 2 were waited for; matrix products, arithmetic and copies ran while one was open for 5% of the time, Pallas kernels for 0%

profile of v2, /device:TPU:13, one launch (start us, length us, event | category | flops | bytes accessed | tf_op | source)
XLA Modules:
  0.0 180.0 jit_solution(15492488191078392600)
XLA Ops:
  0.0 0.7 convert_element_type.27
  0.7 1.3 fusion.53
  2.0 0.1 fusion.29
  2.2 0.8 gather_fusion.4
  2.9 0.6 and_bitcast_fusion
  3.5 0.7 bitcast_add_fusion
  4.2 0.1 select_reduce_fusion.1
  4.3 0.1 fusion.28
  4.4 3.0 %multiply_reduce_fusion = f32[]{:T(128)} fusion(bf16[26,2,128,128]{3,2,1,0:T(8,128)(2,1)} %param.5), kind=kLoop, calls=%fused_computation.6 | loop fusion | flops 2555903 | bytes 1703940 | tf_op jit(solution)/shard_map/reduce_sum | solution.py:51
  7.4 0.1 copy.103
  7.5 0.1 reshape.212
  7.6 0.0 copy-done.6
  7.7 0.6 dynamic-slice
  8.9 0.9 maximum_dynamic-update-slice_fusion
  9.8 21.7 %all-reduce = f32[848]{0:T(1024)S(1)} all-reduce(f32[848]{0:T(1024)S(1)} %maximum_dynamic-update-slice_fusion), channel_id=2, replica_groups=mesh['band'=2,'spk'=16] {'spk'}, use_global_device_ids=true, to_apply=%add | all-reduce | flops 848 | bytes 6784
  31.5 0.1 reshape.265
  31.6 0.7 gather_fusion
  32.4 0.7 fusion.16
  33.0 0.1 fusion.21
  33.2 0.1 fusion.20
  33.3 0.6 pad_clamp_fusion.2
  33.9 0.1 select_n.201
  34.0 0.1 copy.110
  34.1 0.1 copy.113
  34.2 0.1 broadcast_in_dim.114
  34.3 0.1 pad_maximum_fusion.1
  34.4 2.2 %gather_fusion.1 = bf16[64,128,128]{1,2,0:T(8,128)(2,1)} fusion(bf16[26,128,128]{1,2,0:T(8,128)(2,1)S(1)} %pad_maximum_fusion.1, s32[1024]{0:T(1024)} %pad_clamp_fusion.2), kind=kCustom, calls=%fused_computation.1 | custom fusion | bytes 4194560 | tf_op jit(solution)/shard_map/jit(_take)/gather | solution.py:79
  36.6 4.1 %copy.117 = bf16[64,128,128]{2,1,0:T(8,128)(2,1)} copy(bf16[64,128,128]{1,2,0:T(8,128)(2,1)} %gather_fusion.1) | data formatting | bytes 4194304 | tf_op jit(solution)/shard_map/jit(_take)/gather | solution.py:79
  40.7 4.4 %bitcast_select_fusion.1 = bf16[16,512,128]{2,1,0:T(8,128)(2,1)} fusion(pred[16,512]{1,0:T(8,128)(4,1)S(1)} %bitcast.125, bf16[16,512,128]{2,1,0:T(8,128)(2,1)} %bitcast.123), kind=kLoop, calls=%fused_computation.8 | loop fusion | flops 1048576 | bytes 4202496 | tf_op jit(solution)/shard_map/jit(_take)/select_n | solution.py:79
  45.1 16.6 %all-to-all-start = ((bf16[16,512,128]{2,1,0:T(8,128)(2,1)}), bf16[16,512,128]{2,1,0:T(8,128)(2,1)}, u32[]{:S(2)}, u32[]{:S(2)}) async-start(bf16[16,512,128]{2,1,0:T(8,128)(2,1)} %bitcast_select_fusion.1), calls=%async_computation | async-start | bytes 4194304 | tf_op jit(solution)/shard_map/all_to_all | solution.py:80
  61.7 0.1 copy.104
  61.8 0.1 copy.132
  61.9 0.1 subtract_bitcast_fusion
  62.0 0.1 reshape.259
  62.1 0.1 copy.106
  62.2 0.1 fusion.23
  62.3 0.0 copy-start.2
  62.3 5.8 %gather_fusion.5 = s32[416]{0:T(512)S(1)} fusion(s32[16,26,16]{2,0,1:T(8,128)S(1)} %fusion.23, s32[416]{0:T(512)S(1)} %reshape.259), kind=kCustom, calls=%fused_computation.5 | custom fusion | bytes 8320 | tf_op jit(solution)/shard_map/jit(take_along_axis)/gather | solution.py:33
  68.1 0.1 reshape.258
  68.3 0.1 fusion.27
  68.4 0.2 select_reduce_fusion
  68.6 0.1 copy.109
  68.7 0.1 select_n.207
  68.8 0.1 select_n.197
  68.8 0.0 copy-done.2
  68.9 0.1 copy.108
  69.0 0.1 copy.107
  69.1 0.1 broadcast_in_dim.107
  69.2 40.0 %all-to-all-done = bf16[16,512,128]{2,1,0:T(8,128)(2,1)} async-done(((bf16[16,512,128]{2,1,0:T(8,128)(2,1)}), bf16[16,512,128]{2,1,0:T(8,128)(2,1)}, u32[]{:S(2)}, u32[]{:S(2)}) %all-to-all-start) | async-done | bytes 2097184 | tf_op jit(solution)/shard_map/all_to_all | solution.py:80
  109.2 2.8 %fusion.5 = bf16[8,128,128]{2,0,1:T(8,128)(2,1)S(1)} fusion(bf16[64,128,128]{2,1,0:T(8,128)(2,1)} %bitcast.27, f32[8,128]{0,1:T(8,128)S(1)} %copy.108, s32[64]{0:T(128)S(1)} %select_n.197), kind=kOutput, calls=%fused_computation.13 | convolution fusion | flops 17039872 | bytes 2363648 | tf_op jit(solution)/shard_map/ms,sjk->mjk/dot_general | solution.py:83
  112.1 2.1 %gather_fusion.2 = bf16[64,128,128]{2,1,0:T(8,128)(2,1)} fusion(bf16[8,128,128]{2,1,0:T(8,128)(2,1)S(1)} %copy.120, s32[1024]{0:T(1024)S(1)} %pad_clamp_fusion.1), kind=kCustom, calls=%fused_computation.2 | custom fusion | bytes 4194560 | tf_op jit(solution)/shard_map/jit(_take)/gather | solution.py:87
  114.2 4.4 %bitcast_select_fusion = bf16[16,512,128]{2,1,0:T(8,128)(2,1)} fusion(pred[16,512]{1,0:T(8,128)(4,1)S(1)} %bitcast.124, bf16[16,512,128]{2,1,0:T(8,128)(2,1)} %bitcast.122), kind=kLoop, calls=%fused_computation.7 | loop fusion | flops 1048576 | bytes 4202496 | tf_op jit(solution)/shard_map/jit(_take)/select_n | solution.py:87
  118.7 4.9 %all-to-all-start.1 = ((bf16[16,512,128]{2,1,0:T(8,128)(2,1)}), bf16[16,512,128]{2,1,0:T(8,128)(2,1)}, u32[]{:S(2)}, u32[]{:S(2)}) async-start(bf16[16,512,128]{2,1,0:T(8,128)(2,1)} %bitcast_select_fusion), calls=%async_computation.1 | async-start | bytes 4194304 | tf_op jit(solution)/shard_map/all_to_all | solution.py:88
  123.6 0.2 slice_reduce_fusion
  123.8 0.6 fusion.45
  125.0 46.1 %all-to-all-done.1 = bf16[16,512,128]{2,1,0:T(8,128)(2,1)} async-done(((bf16[16,512,128]{2,1,0:T(8,128)(2,1)}), bf16[16,512,128]{2,1,0:T(8,128)(2,1)}, u32[]{:S(2)}, u32[]{:S(2)}) %all-to-all-start.1) | async-done | bytes 2097184 | tf_op jit(solution)/shard_map/all_to_all | solution.py:88
  171.1 2.3 %gather_fusion.3 = bf16[26,128,128]{2,1,0:T(8,128)(2,1)S(1)} fusion(bf16[64,128,128]{2,1,0:T(8,128)(2,1)} %bitcast.30, s32[1024]{0:T(1024)S(1)} %pad_clamp_fusion), kind=kCustom, calls=%fused_computation.3 | custom fusion | bytes 1704040 | tf_op jit(solution)/shard_map/jit(_take)/gather | solution.py:91
  173.4 1.0 fusion.14
  174.4 0.1 fusion.8
  174.5 0.1 fusion.10
  174.6 0.1 pad_maximum_fusion
  174.7 2.2 %copy.124 = f32[26,128,128]{2,0,1:T(8,128)} copy(f32[26,128,128]{1,2,0:T(8,128)S(1)} %pad_maximum_fusion) | data formatting | bytes 3407872 | tf_op jit(solution)/shard_map/concatenate | solution.py:27
  177.0 2.4 %fusion.41 = f32[2,128,128]{2,0,1:T(2,128)S(1)} fusion(f32[26,128,128]{2,0,1:T(8,128)} %copy.124, s32[26]{0:T(128)S(1)} %bitcast.130), kind=kOutput, calls=%fused_computation.91 | convolution fusion | flops 10223668 | bytes 1835112 | tf_op jit(solution)/shard_map/tu,tjk->ujk/dot_general | solution.py:94
  179.3 0.7 copy_add_fusion
  (37 shorter events, 0.3 us)
Async XLA Ops:
  0.0 7.6 %copy-start.6 = (u32[32]{0:T(128)S(1)}, u32[32]{0:T(128)}, u32[]{:S(2)}) copy-start(u32[32]{0:T(128)} %constant.200) | copy-start | bytes 388
  0.0 31.6 %copy-start.1 = (f32[2,128,128]{2,1,0:T(8,128)S(1)}, f32[2,128,128]{2,1,0:T(8,128)}, u32[]{:S(2)}) copy-start(f32[2,128,128]{2,1,0:T(8,128)} %param.4) | copy-start | bytes 393220
  2.2 30.2 %copy-start = (bf16[26,2,128,128]{3,2,1,0:T(8,128)(2,1)S(1)}, bf16[26,2,128,128]{3,2,1,0:T(8,128)(2,1)}, u32[]{:S(2)}) copy-start(bf16[26,2,128,128]{3,2,1,0:T(8,128)(2,1)} %param.5) | copy-start | bytes 5111812
  45.1 64.1 %all-to-all-start = ((bf16[16,512,128]{2,1,0:T(8,128)(2,1)}), bf16[16,512,128]{2,1,0:T(8,128)(2,1)}, u32[]{:S(2)}, u32[]{:S(2)}) async-start(bf16[16,512,128]{2,1,0:T(8,128)(2,1)} %bitcast_select_fusion.1), calls=%async_computation | async-start | bytes 4194304 | tf_op jit(solution)/shard_map/all_to_all | solution.py:80
  62.3 6.5 %copy-start.2 = (f32[1,8,128]{2,1,0:T(8,128)S(1)}, f32[1,8,128]{2,1,0:T(8,128)}, u32[]{:S(2)}) copy-start(f32[1,8,128]{2,1,0:T(8,128)} %param.7) | copy-start | bytes 12292
  118.7 6.3 %copy-start.5 = (s32[26,1]{0,1:T(1,128)S(1)}, s32[26,1]{0,1:T(1,128)}, u32[]{:S(2)}) copy-start(s32[26,1]{0,1:T(1,128)} %get-tuple-element.12) | copy-start | bytes 316
  118.7 54.7 %copy-start.3 = (pred[26]{0:T(512)(128)(4,1)S(1)}, pred[26]{0:T(512)(128)(4,1)}, u32[]{:S(2)}) copy-start(pred[26]{0:T(512)(128)(4,1)} %get-tuple-element.11) | copy-start | bytes 82
  118.7 52.4 %all-to-all-start.1 = ((bf16[16,512,128]{2,1,0:T(8,128)(2,1)}), bf16[16,512,128]{2,1,0:T(8,128)(2,1)}, u32[]{:S(2)}, u32[]{:S(2)}) async-start(bf16[16,512,128]{2,1,0:T(8,128)(2,1)} %bitcast_select_fusion), calls=%async_computation.1 | async-start | bytes 4194304 | tf_op jit(solution)/shard_map/all_to_all | solution.py:88
  174.7 2.2 %copy-start.4 = (s32[26,1]{0,1:T(1,128)S(1)}, s32[26,1]{0,1:T(1,128)}, u32[]{:S(2)}) copy-start(s32[26,1]{0,1:T(1,128)} %get-tuple-element.26) | copy-start | bytes 316

commit v3 on v2

v3 whole, which is shorter than its diff:
```python
import jax
import jax.numpy as jnp
from jax import lax
from jax.sharding import PartitionSpec as P

SBLK = 32
MBLK = 128
SPEAKERS = 4096


reg_weight = 0.25


def swap_halves(rows, sign):
    width = rows.shape[-1]
    half = width // 2
    col = jnp.arange(width)
    flip = ((col[:, None] + half) % width == col[None, :]).astype(rows.dtype)
    flip = flip * jnp.where(col[None, :] < half, -sign, sign).astype(rows.dtype)
    return jnp.einsum("...ik,kl->...il", rows, flip, preferred_element_type=jnp.float32).astype(rows.dtype)


def slot_ranks(target_peer, devices):
    onehot = (target_peer[..., :, None] == jnp.arange(devices)).astype(jnp.int32)
    running = jnp.cumsum(onehot, axis=-2)
    return jnp.take_along_axis(running, target_peer[..., None], axis=-1)[..., 0] - 1


def per_device(direction, plant, tile_pairs, mic_weight):
    devices = lax.axis_size("spk")
    device_id = lax.axis_index("spk")
    unit_count = direction.shape[0]
    tile_count = plant.shape[0]
    block_size = direction.shape[1]
    field_width = direction.shape[2]
    groups_per_bin = SBLK // unit_count
    bin_count = devices // groups_per_bin
    peer_blocks = MBLK // devices
    mic_units = bin_count * peer_blocks
    my_bin = device_id // groups_per_bin
    capacity = max(3, (2 * tile_count + devices - 1) // devices)
    slots = devices * capacity

    local_unit = tile_pairs[:, 0] % unit_count
    mic_block = tile_pairs[:, 1]
    target_peer = mic_block // peer_blocks
    position = target_peer * capacity + slot_ranks(target_peer, devices)
    send_hit = position[None, :] == jnp.arange(slots)[:, None]
    slot_pair = jnp.sum(jnp.where(send_hit, jnp.arange(tile_count), 0), axis=1)
    target_label = my_bin * peer_blocks + mic_block - target_peer * peer_blocks
    slot_label = jnp.where(
        send_hit.any(axis=1), jnp.sum(jnp.where(send_hit, target_label, 0), axis=1), mic_units
    )

    local_power = jnp.sum(jnp.square(plant.astype(jnp.float32)))
    header = jnp.concatenate(
        [slot_label.reshape(devices, capacity).astype(jnp.float32),
         jnp.broadcast_to(local_power, (devices, 1))], axis=1)
    header_in = lax.all_to_all(header, "spk", 0, 0, tiled=True)
    labels_in = header_in[:, :capacity].astype(jnp.int32).reshape(slots)
    source_bin = jnp.arange(devices) // groups_per_bin
    bin_power = jnp.sum(jnp.where(source_bin == my_bin, header_in[:, capacity], 0.0))
    recv_onehot = (labels_in[None, :] == jnp.arange(mic_units)[:, None]).astype(jnp.bfloat16)

    rounded = direction.astype(jnp.bfloat16)
    both = jnp.stack([rounded, swap_halves(rounded, 1)], axis=1)
    pair_rows = both[local_unit]
    partial_field = jnp.einsum("tcij,tcjk->tik", plant, pair_rows,
                               preferred_element_type=jnp.float32).astype(jnp.bfloat16)
    outgoing = jnp.take(partial_field, slot_pair, axis=0, mode="clip")
    arrived = lax.all_to_all(
        outgoing.reshape(devices, capacity * block_size, field_width), "spk", 0, 0, tiled=True
    ).reshape(slots, block_size, field_width)
    pressure = jnp.einsum("ms,sjk->mjk", recv_onehot, arrived, preferred_element_type=jnp.float32)
    weights_flat = mic_weight.reshape(mic_units, block_size)
    weighted = (weights_flat[:, :, None] * pressure).astype(jnp.bfloat16)

    reply = jnp.take(weighted, jnp.minimum(labels_in, mic_units - 1), axis=0, mode="clip")
    returned = lax.all_to_all(
        reply.reshape(devices, capacity * block_size, field_width), "spk", 0, 0, tiled=True
    ).reshape(slots, block_size, field_width)
    tile_weighted = jnp.take(returned, position, axis=0, mode="clip")

    back_rows = jnp.stack([tile_weighted, swap_halves(tile_weighted, -1)], axis=1)
    unit_mask = (local_unit[:, None] == jnp.arange(unit_count)[None, :]).astype(jnp.bfloat16)
    masked = back_rows[:, None] * unit_mask[:, :, None, None, None]
    gram = jnp.einsum("tcij,tucik->ujk", plant, masked, preferred_element_type=jnp.float32)
    return gram + reg_weight * bin_power / SPEAKERS * direction


def solution(mesh):
    placed = (
        P(("band", "spk"), None, None),
        P(("band", "spk"), None, None, None),
        P(("band", "spk"), None),
        P("band", "spk", None),
    )
    return jax.shard_map(
        per_device,
        mesh=mesh,
        in_specs=placed,
        out_specs=P(("band", "spk"), None, None),
        check_vma=False,
    )
```

time: 181 us -> 140 us (0.77)
  blocking collectives: 21.7 us -> 0 us
  other arithmetic: 19.5 us -> 6.35 us
  local copies, waits for them, and re-layouts: 22.7 us -> 14.9 us
  waiting for transfers between devices: 86.1 us -> 93 us
  starting transfers between devices: 21.5 us -> 17.4 us
    unnamed x1 -> x0, blocking collectives: 21.7 us -> none
    all_to_all x1, starting transfers between devices: 16.6 us -> 6.15 us  [per_device(): lax.all_to_all(outgoing.reshape(devices, capacity * block_size, field_wid...]
    select_n x4 -> x1, other arithmetic: 8.86 us -> 0.01 us  [swap_halves(): flip = ((col[:, None] + half) % width == col[None, :]).astype(rows.dtype)]
    all_to_all x1, waiting for transfers between devices: 40 us -> 46.8 us  [per_device(): lax.all_to_all(outgoing.reshape(devices, capacity * block_size, field_wid...]
    all_to_all x0 -> x1, starting transfers between devices: none -> 6.52 us  [per_device(): header_in = lax.all_to_all(header, 'spk', 0, 0, tiled=True)]
    gather x4 -> x1, local copies, waits for them, and re-layouts: 6.74 us -> 0.79 us  [slot_ranks(): jnp.take_along_axis(running, target_peer[..., None], axis=-1)[..., 0] - 1]
    gather x5, local copies, waits for them, and re-layouts: 11.5 us -> 8.75 us  [the longest x2 3.88 us: per_device(): outgoing = jnp.take(partial_field, slot_pair, axis=0, mode='clip')]
    another operation x0 -> x1, local copies, waits for them, and re-layouts: none -> 2.53 us  [per_device(): jnp.stack([tile_weighted, swap_halves(tile_weighted, -1)], axis=1)]
  transfers between devices with their start and end apart: 2 -> 3, of which waited for: 2 -> 2; matrix products, arithmetic and copies ran while one was open for 5% -> 7% of each run, Pallas kernels for 0% -> 0%
where the time goes in v3:
time: 140 us; the launch traced here: 139 us
  waiting for transfers between devices  93 us (66%)
  starting transfers between devices  17.4 us (12%)
  local copies, waits for them, and re-layouts  14.9 us (11%)
  matrix products  6.55 us (5%)
  other arithmetic  6.35 us (5%)
    all_to_all x1, waiting for transfers between devices, per_device(): lax.all_to_all(outgoing.reshape(devices, capacity * block_size, field_wid...  46.8 us
    all_to_all x1, waiting for transfers between devices, per_device(): lax.all_to_all(reply.reshape(devices, capacity * block_size, field_width)...  46.1 us
    all_to_all x1, starting transfers between devices, per_device(): header_in = lax.all_to_all(header, 'spk', 0, 0, tiled=True)  6.52 us
    all_to_all x1, starting transfers between devices, per_device(): lax.all_to_all(outgoing.reshape(devices, capacity * block_size, field_wid...  6.15 us
    all_to_all x1, starting transfers between devices, per_device(): lax.all_to_all(reply.reshape(devices, capacity * block_size, field_width)...  4.78 us
    gather x2, local copies, waits for them, and re-layouts, per_device(): outgoing = jnp.take(partial_field, slot_pair, axis=0, mode='clip')  3.88 us
    reduce_sum x1, other arithmetic, per_device(): local_power = jnp.sum(jnp.square(plant.astype(jnp.float32)))  3.03 us
  transfers between devices with their start and end apart: 3, of which 2 were waited for; matrix products, arithmetic and copies ran while one was open for 7% of the time, Pallas kernels for 0%

profile of v3, /device:TPU:13, one launch (start us, length us, event | category | flops | bytes accessed | tf_op | source)
XLA Modules:
  0.0 139.1 jit_solution(4185015965966290898)
XLA Ops:
  0.0 0.0 copy-start.2
  0.0 0.8 fusion.54
  0.8 0.1 fusion.40
  0.9 0.8 gather_fusion.4
  1.7 0.7 bitcast_add_fusion
  2.4 0.1 fusion.39
  2.5 0.7 fusion.50
  3.2 0.1 select_reduce_fusion.1
  3.3 0.1 convert_element_type.64
  3.4 3.0 %multiply_reduce_fusion = f32[]{:T(128)} fusion(bf16[26,2,128,128]{3,2,1,0:T(8,128)(2,1)} %param.5), kind=kLoop, calls=%fused_computation.7 | loop fusion | flops 2555903 | bytes 1703940 | tf_op jit(solution)/shard_map/reduce_sum | solution.py:55
  6.4 1.3 concatenate.3
  7.7 6.5 %all-to-all-start = ((f32[16,1,5]{2,1,0:T(1,128)}), f32[16,1,5]{2,1,0:T(1,128)S(1)}, u32[]{:S(2)}, u32[]{:S(2)}) async-start(f32[16,1,5]{2,1,0:T(1,128)} %bitcast.33), calls=%async_computation | async-start | bytes 16384 | tf_op jit(solution)/shard_map/all_to_all | solution.py:59
  14.2 0.0 copy-done.2
  14.2 0.1 copy.51
  14.4 0.3 fusion.25
  14.7 0.0 copy-start
  14.7 2.0 %gather_fusion = bf16[26,2,128,128]{2,3,1,0:T(8,128)(2,1)} fusion(bf16[2,2,128,128]{2,3,0,1:T(8,128)(2,1)S(1)} %pad_maximum_fusion.1, s32[1024]{0:T(1024)S(1)} %pad_clamp_fusion.3), kind=kCustom, calls=%fused_computation | custom fusion | bytes 3407976 | tf_op jit(solution)/shard_map/gather | solution.py:67
  16.7 0.0 copy-done
  16.7 2.1 %fusion.8 = bf16[26,128,128]{1,2,0:T(8,128)(2,1)S(1)} fusion(bf16[26,2,128,128]{2,3,1,0:T(8,128)(2,1)} %gather_fusion, bf16[26,2,128,128]{3,2,1,0:T(8,128)(2,1)S(1)} %copy-done), kind=kOutput, calls=%fused_computation.17 | convolution fusion | flops 218529792 | bytes 4259840 | tf_op jit(solution)/shard_map/tcij,tcjk->tik/dot_general | solution.py:68
  18.8 1.0 gather_fusion.1
  19.7 2.9 %copy.54 = bf16[64,128,128]{2,1,0:T(8,128)(2,1)} copy(bf16[64,128,128]{1,2,0:T(8,128)(2,1)S(1)} %gather_fusion.1) | data formatting | bytes 4194304 | tf_op jit(solution)/shard_map/jit(_take)/gather | solution.py:70
  22.6 0.0 all-to-all-done
  22.7 0.0 copy-start.3
  22.7 6.2 %all-to-all-start.1 = ((bf16[16,512,128]{2,1,0:T(8,128)(2,1)}), bf16[16,512,128]{2,1,0:T(8,128)(2,1)S(1)}, u32[]{:S(2)}, u32[]{:S(2)}) async-start(bf16[16,512,128]{2,1,0:T(8,128)(2,1)} %bitcast.19), calls=%async_computation.1 | async-start | bytes 4194304 | tf_op jit(solution)/shard_map/all_to_all | solution.py:71
  28.8 0.0 copy-done.3
  28.8 0.1 copy.46
  28.9 0.1 copy.49
  29.0 0.1 copy.50
  29.1 0.1 eq.104
  29.2 0.1 copy.56
  29.3 0.1 reshape.175
  29.4 46.8 %all-to-all-done.1 = bf16[16,512,128]{2,1,0:T(8,128)(2,1)S(1)} async-done(((bf16[16,512,128]{2,1,0:T(8,128)(2,1)}), bf16[16,512,128]{2,1,0:T(8,128)(2,1)S(1)}, u32[]{:S(2)}, u32[]{:S(2)}) %all-to-all-start.1) | async-done | bytes 2097184 | tf_op jit(solution)/shard_map/all_to_all | solution.py:71
  76.2 1.3 fusion.12
  77.5 2.2 %gather_fusion.2 = bf16[64,128,128]{2,1,0:T(8,128)(2,1)} fusion(bf16[8,128,128]{2,1,0:T(8,128)(2,1)S(1)} %copy.57, s32[1024]{0:T(1024)S(1)} %pad_clamp_fusion.1), kind=kCustom, calls=%fused_computation.2 | custom fusion | bytes 4194560 | tf_op jit(solution)/shard_map/jit(_take)/gather | solution.py:78
  79.7 4.8 %all-to-all-start.2 = ((bf16[16,512,128]{2,1,0:T(8,128)(2,1)}), bf16[16,512,128]{2,1,0:T(8,128)(2,1)S(1)}, u32[]{:S(2)}, u32[]{:S(2)}) async-start(bf16[16,512,128]{2,1,0:T(8,128)(2,1)} %bitcast.21), calls=%async_computation.2 | async-start | bytes 4194304 | tf_op jit(solution)/shard_map/all_to_all | solution.py:79
  84.5 0.6 fusion.46
  85.8 46.1 %all-to-all-done.2 = bf16[16,512,128]{2,1,0:T(8,128)(2,1)S(1)} async-done(((bf16[16,512,128]{2,1,0:T(8,128)(2,1)}), bf16[16,512,128]{2,1,0:T(8,128)(2,1)S(1)}, u32[]{:S(2)}, u32[]{:S(2)}) %all-to-all-start.2) | async-done | bytes 2097184 | tf_op jit(solution)/shard_map/all_to_all | solution.py:79
  131.9 0.7 gather_fusion.3
  132.6 0.4 fusion.7
  133.0 0.2 pad_maximum_fusion
  133.2 0.0 copy-start.1
  133.2 2.5 %copy.58 = bf16[26,2,128,128]{2,3,0,1:T(8,128)(2,1)} copy(bf16[26,2,128,128]{3,2,0,1:T(8,128)(2,1)S(1)} %pad_maximum_fusion) | data formatting | bytes 3407872 | tf_op jit(solution)/shard_map/stack | solution.py:84
  135.8 0.0 copy-done.1
  135.8 2.5 %fusion.20 = f32[2,128,128]{1,2,0:T(8,128)S(1)} fusion(bf16[26,2]{0,1:T(2,128)(2,1)S(1)} %compare_convert_fusion, bf16[26,2,128,128]{2,3,0,1:T(8,128)(2,1)} %copy.58, f32[2,128,128]{1,2,0:T(8,128)S(1)} %copy.51, f32[]{:T(128)S(6)} %div.52, bf16[26,2,128,128]{3,2,1,0:T(8,128)(2,1)S(1)} %copy-done.1), kind=kOutput, calls=%fused_computation.21 | convolution fusion | flops 437977088 | bytes 3670124 | tf_op jit(solution)/shard_map/tcij,tucik->ujk/dot_general | solution.py:87
  138.3 0.8 copy.61
  (18 shorter events, 0.2 us)
Async XLA Ops:
  0.0 14.2 %copy-start.2 = (f32[2,128,128]{2,1,0:T(8,128)S(1)}, f32[2,128,128]{2,1,0:T(8,128)}, u32[]{:S(2)}) copy-start(f32[2,128,128]{2,1,0:T(8,128)} %param.4) | copy-start | bytes 393220
  7.7 14.9 %all-to-all-start = ((f32[16,1,5]{2,1,0:T(1,128)}), f32[16,1,5]{2,1,0:T(1,128)S(1)}, u32[]{:S(2)}, u32[]{:S(2)}) async-start(f32[16,1,5]{2,1,0:T(1,128)} %bitcast.33), calls=%async_computation | async-start | bytes 16384 | tf_op jit(solution)/shard_map/all_to_all | solution.py:59
  14.7 2.0 %copy-start = (bf16[26,2,128,128]{3,2,1,0:T(8,128)(2,1)S(1)}, bf16[26,2,128,128]{3,2,1,0:T(8,128)(2,1)}, u32[]{:S(2)}) copy-start(bf16[26,2,128,128]{3,2,1,0:T(8,128)(2,1)} %param.5) | copy-start | bytes 5111812
  22.7 6.2 %copy-start.3 = (f32[1,8,128]{2,1,0:T(8,128)S(1)}, f32[1,8,128]{2,1,0:T(8,128)}, u32[]{:S(2)}) copy-start(f32[1,8,128]{2,1,0:T(8,128)} %param.7) | copy-start | bytes 12292
  22.7 53.6 %all-to-all-start.1 = ((bf16[16,512,128]{2,1,0:T(8,128)(2,1)}), bf16[16,512,128]{2,1,0:T(8,128)(2,1)S(1)}, u32[]{:S(2)}, u32[]{:S(2)}) async-start(bf16[16,512,128]{2,1,0:T(8,128)(2,1)} %bitcast.19), calls=%async_computation.1 | async-start | bytes 4194304 | tf_op jit(solution)/shard_map/all_to_all | solution.py:71
  79.7 52.2 %all-to-all-start.2 = ((bf16[16,512,128]{2,1,0:T(8,128)(2,1)}), bf16[16,512,128]{2,1,0:T(8,128)(2,1)S(1)}, u32[]{:S(2)}, u32[]{:S(2)}) async-start(bf16[16,512,128]{2,1,0:T(8,128)(2,1)} %bitcast.21), calls=%async_computation.2 | async-start | bytes 4194304 | tf_op jit(solution)/shard_map/all_to_all | solution.py:79
  133.2 2.5 %copy-start.1 = (bf16[26,2,128,128]{3,2,1,0:T(8,128)(2,1)S(1)}, bf16[26,2,128,128]{3,2,1,0:T(8,128)(2,1)}, u32[]{:S(2)}) copy-start(bf16[26,2,128,128]{3,2,1,0:T(8,128)(2,1)} %param.5) | copy-start | bytes 5111812

commit v4 on v3

v4 whole, which is shorter than its diff:
```python
import jax
import jax.numpy as jnp
from jax import lax
from jax.sharding import PartitionSpec as P

SBLK = 32
MBLK = 128
SPEAKERS = 4096


reg_weight = 0.25


def swap_halves(rows, sign):
    width = rows.shape[-2]
    half = width // 2
    col = jnp.arange(width)
    flip = ((col[:, None] + half) % width == col[None, :]).astype(rows.dtype)
    flip = flip * jnp.where(col[None, :] < half, -sign, sign).astype(rows.dtype)
    return jnp.einsum("...ki,kl->...li", rows, flip, preferred_element_type=jnp.float32).astype(rows.dtype)


def slot_ranks(target_peer, devices):
    onehot = (target_peer[..., :, None] == jnp.arange(devices)).astype(jnp.int32)
    running = jnp.cumsum(onehot, axis=-2)
    return jnp.take_along_axis(running, target_peer[..., None], axis=-1)[..., 0] - 1


def with_header(blocks, values, devices, capacity):
    rows, lanes = blocks.shape[1], blocks.shape[2]
    body = blocks.reshape(devices, capacity * rows, lanes)
    head = jnp.pad(values.astype(blocks.dtype)[:, None, :], ((0, 0), (0, 15), (0, lanes - values.shape[1])))
    return jnp.concatenate([body, head], axis=1)


def split_header(buffer, capacity, rows, width):
    body = buffer[:, : capacity * rows].reshape(-1, rows, buffer.shape[2])
    return body, buffer[:, capacity * rows, :width]


def per_device(direction, plant, tile_pairs, mic_weight):
    devices = lax.axis_size("spk")
    device_id = lax.axis_index("spk")
    unit_count = direction.shape[0]
    tile_count = plant.shape[0]
    block_size = direction.shape[1]
    field_width = direction.shape[2]
    groups_per_bin = SBLK // unit_count
    bin_count = devices // groups_per_bin
    peer_blocks = MBLK // devices
    mic_units = bin_count * peer_blocks
    my_bin = device_id // groups_per_bin
    capacity = max(3, (2 * tile_count + devices - 1) // devices)
    slots = devices * capacity

    local_unit = tile_pairs[:, 0] % unit_count
    mic_block = tile_pairs[:, 1]
    target_peer = mic_block // peer_blocks
    position = target_peer * capacity + slot_ranks(target_peer, devices)
    send_hit = position[None, :] == jnp.arange(slots)[:, None]
    slot_pair = jnp.sum(jnp.where(send_hit, jnp.arange(tile_count), 0), axis=1)
    target_label = my_bin * peer_blocks + mic_block - target_peer * peer_blocks
    slot_label = jnp.where(
        send_hit.any(axis=1), jnp.sum(jnp.where(send_hit, target_label, 0), axis=1), mic_units
    )

    rounded = jnp.swapaxes(direction.astype(jnp.bfloat16), 1, 2)
    both = jnp.stack([rounded, swap_halves(rounded, 1)], axis=1)
    pair_rows = both[local_unit]
    partial_field = jnp.einsum("tcij,tckj->tki", plant, pair_rows,
                               preferred_element_type=jnp.float32).astype(jnp.bfloat16)
    outgoing = jnp.take(partial_field, slot_pair, axis=0, mode="clip")
    sent = with_header(outgoing, slot_label.reshape(devices, capacity), devices, capacity)
    arrived, labels_in = split_header(
        lax.all_to_all(sent, "spk", 0, 0, tiled=True), capacity, field_width, capacity)
    labels_in = labels_in.astype(jnp.int32).reshape(slots)
    recv_onehot = (labels_in[None, :] == jnp.arange(mic_units)[:, None]).astype(jnp.bfloat16)
    pressure = jnp.einsum("ms,ski->mki", recv_onehot, arrived, preferred_element_type=jnp.float32)
    weights_flat = mic_weight.reshape(mic_units, block_size)
    weighted = (weights_flat[:, None, :] * pressure).astype(jnp.bfloat16)

    local_power = jnp.sum(jnp.square(plant.astype(jnp.float32)))
    power_hi = local_power.astype(jnp.bfloat16).astype(jnp.float32)
    power_mid = (local_power - power_hi).astype(jnp.bfloat16).astype(jnp.float32)
    power_lo = local_power - power_hi - power_mid
    power_parts = jnp.broadcast_to(jnp.stack([power_hi, power_mid, power_lo]), (devices, 3))
    reply = jnp.take(weighted, jnp.minimum(labels_in, mic_units - 1), axis=0, mode="clip")
    returned, powers_in = split_header(
        lax.all_to_all(with_header(reply, power_parts, devices, capacity), "spk", 0, 0, tiled=True),
        capacity, field_width, 3)
    source_bin = jnp.arange(devices) // groups_per_bin
    power_of = jnp.sum(powers_in.astype(jnp.float32), axis=1)
    bin_power = jnp.sum(jnp.where(source_bin == my_bin, power_of, 0.0))
    tile_weighted = jnp.take(returned, position, axis=0, mode="clip")

    back_rows = jnp.stack([tile_weighted, swap_halves(tile_weighted, -1)], axis=1)
    unit_mask = (local_unit[:, None] == jnp.arange(unit_count)[None, :]).astype(jnp.bfloat16)
    masked = back_rows[:, None] * unit_mask[:, :, None, None, None]
    gram = jnp.einsum("tcij,tucki->ujk", plant, masked, preferred_element_type=jnp.float32)
    return gram + reg_weight * bin_power / SPEAKERS * direction


def solution(mesh):
    placed = (
        P(("band", "spk"), None, None),
        P(("band", "spk"), None, None, None),
        P(("band", "spk"), None),
        P("band", "spk", None),
    )
    return jax.shard_map(
        per_device,
        mesh=mesh,
        in_specs=placed,
        out_specs=P(("band", "spk"), None, None),
        check_vma=False,
    )
```

time: 140 us -> 134 us (0.957)
  starting transfers between devices: 17.4 us -> 11.3 us
  other arithmetic: 6.35 us -> 8.9 us
  local copies, waits for them, and re-layouts: 14.9 us -> 12.6 us
  matrix products: 6.55 us -> 5.02 us
    all_to_all x3 -> x2, starting transfers between devices: 17.4 us -> 11.3 us  [the longest x1 6.52 us: per_device(): lax.all_to_all(sent, 'spk', 0, 0, tiled=True)]
    concatenate x0 -> x2, other arithmetic: none -> 2.99 us  [with_header(): return jnp.concatenate([body, head], axis=1)]
    gather x2 -> x1, local copies, waits for them, and re-layouts: 3.88 us -> 0.95 us  [per_device(): outgoing = jnp.take(partial_field, slot_pair, axis=0, mode='clip')]
    unnamed x10 -> x8, local copies, waits for them, and re-layouts: 0.12 us -> 2.77 us
    another operation x1 -> x0, local copies, waits for them, and re-layouts: 2.53 us -> none  [per_device(): jnp.stack([tile_weighted, swap_halves(tile_weighted, -1)], axis=1)]
    slice x0 -> x2, local copies, waits for them, and re-layouts: none -> 1.77 us  [split_header(): body = buffer[:, :capacity * rows].reshape(-1, rows, buffer.shape[2])]
    gather x1, local copies, waits for them, and re-layouts: 0.71 us -> 2.3 us  [per_device(): tile_weighted = jnp.take(returned, position, axis=0, mode='clip')]
    dot_general x5, matrix products: 6.55 us -> 5.02 us  [the longest x1 2.06 us: per_device(): jnp.einsum('tcij,tckj->tki', plant, pair_rows, preferred_element_type=jnp...]
  transfers between devices with their start and end apart: 3 -> 2, of which waited for: 2 -> 2; matrix products, arithmetic and copies ran while one was open for 7% -> 2% of each run, Pallas kernels for 0% -> 0%
where the time goes in v4:
time: 134 us; the launch traced here: 133 us
  waiting for transfers between devices  93.3 us (70%)
  local copies, waits for them, and re-layouts  12.6 us (9%)
  starting transfers between devices  11.3 us (8%)
  other arithmetic  8.9 us (7%)
  matrix products  5.02 us (4%)
  between operations  2.18 us (2%)
    all_to_all x1, waiting for transfers between devices, per_device(): lax.all_to_all(with_header(reply, power_parts, devices, capacity), 'spk',...  48.8 us
    all_to_all x1, waiting for transfers between devices, per_device(): lax.all_to_all(sent, 'spk', 0, 0, tiled=True)  44.5 us
    all_to_all x1, starting transfers between devices, per_device(): lax.all_to_all(sent, 'spk', 0, 0, tiled=True)  6.52 us
    all_to_all x1, starting transfers between devices, per_device(): lax.all_to_all(with_header(reply, power_parts, devices, capacity), 'spk',...  4.78 us
    concatenate x2, other arithmetic, with_header(): return jnp.concatenate([body, head], axis=1)  2.99 us
    reduce_sum x1, other arithmetic, per_device(): local_power = jnp.sum(jnp.square(plant.astype(jnp.float32)))  2.93 us
    unnamed x8, local copies, waits for them, and re-layouts  2.77 us
  transfers between devices with their start and end apart: 2, of which 2 were waited for; matrix products, arithmetic and copies ran while one was open for 2% of the time, Pallas kernels for 0%

profile of v4, /device:TPU:13, one launch (start us, length us, event | category | flops | bytes accessed | tf_op | source)
XLA Modules:
  0.0 133.3 jit_solution(11322206905940903812)
XLA Ops:
  0.0 0.8 fusion.67
  0.8 0.7 fusion.63
  1.5 0.1 fusion.42
  1.7 0.8 gather_fusion.4
  2.5 0.1 fusion.38
  2.6 0.1 select_reduce_fusion.1
  2.7 0.1 convert_element_type.137
  2.8 1.0 copy.17
  3.8 0.0 copy-start
  3.8 0.2 fusion.26
  4.0 2.0 %gather_fusion = bf16[26,2,128,128]{3,2,1,0:T(8,128)(2,1)} fusion(bf16[2,2,128,128]{3,2,0,1:T(8,128)(2,1)S(1)} %pad_maximum_fusion.2, s32[1024]{0:T(1024)S(1)} %pad_clamp_fusion.3), kind=kCustom, calls=%fused_computation | custom fusion | bytes 3407976 | tf_op jit(solution)/shard_map/gather | solution.py:69
  6.0 0.0 copy-done
  6.0 2.1 %bitcast_convert_fusion = bf16[26,128,128]{2,1,0:T(8,128)(2,1)S(1)} fusion(bf16[26,2,128,128]{3,2,1,0:T(8,128)(2,1)} %gather_fusion, bf16[26,2,128,128]{3,2,1,0:T(8,128)(2,1)S(1)} %copy-done), kind=kOutput, calls=%fused_computation.16 | convolution fusion | flops 218529792 | bytes 4259840 | tf_op jit(solution)/shard_map/tcij,tckj->tki/dot_general | solution.py:70
  8.1 1.0 gather_fusion.1
  9.1 1.5 %fusion.3 = bf16[16,528,128]{2,1,0:T(8,128)(2,1)} fusion(bf16[16,1,4]{2,1,0:T(2,128)(2,1)S(1)} %convert_element_type.137, bf16[16,512,128]{2,1,0:T(8,128)(2,1)S(1)} %bitcast.82), kind=kLoop, calls=%fused_computation.10 | loop fusion | flops 6488064 | bytes 4259968 | tf_op jit(solution)/shard_map/concatenate | solution.py:33
  10.6 6.5 %all-to-all-start = ((bf16[16,528,128]{2,1,0:T(8,128)(2,1)}), bf16[16,528,128]{2,1,0:T(8,128)(2,1)S(1)}, u32[]{:S(2)}, u32[]{:S(2)}) async-start(bf16[16,528,128]{2,1,0:T(8,128)(2,1)} %fusion.3), calls=%async_computation | async-start | bytes 4325376 | tf_op jit(solution)/shard_map/all_to_all | solution.py:75
  17.1 2.9 %multiply_reduce_fusion = f32[]{:T(128)} fusion(bf16[26,2,128,128]{3,2,1,0:T(8,128)(2,1)} %param.5), kind=kLoop, calls=%fused_computation.9 | loop fusion | flops 2555903 | bytes 1703940 | tf_op jit(solution)/shard_map/reduce_sum | solution.py:82
  21.3 0.1 fusion.53
  21.4 44.5 %all-to-all-done = bf16[16,528,128]{2,1,0:T(8,128)(2,1)S(1)} async-done(((bf16[16,528,128]{2,1,0:T(8,128)(2,1)}), bf16[16,528,128]{2,1,0:T(8,128)(2,1)S(1)}, u32[]{:S(2)}, u32[]{:S(2)}) %all-to-all-start) | async-done | bytes 2162720 | tf_op jit(solution)/shard_map/all_to_all | solution.py:75
  65.9 0.1 minimum_reduce_fusion
  66.0 0.1 reshape.242
  66.1 0.1 reshape.223
  66.1 0.0 copy-start.2
  66.2 0.2 slice.35
  66.4 0.5 copy-done.2
  66.8 1.2 fusion.13
  68.1 1.0 gather_fusion.2
  69.1 1.5 %pad_maximum_fusion = bf16[16,528,128]{2,1,0:T(8,128)(2,1)} fusion(bf16[16,16,128]{2,1,0:T(8,128)(2,1)S(1)} %pad.12, bf16[16,512,128]{2,1,0:T(8,128)(2,1)S(1)} %bitcast.81), kind=kLoop, calls=%fused_computation.11 | loop fusion | flops 4325376 | bytes 4325376 | tf_op jit(solution)/shard_map/concatenate | solution.py:33
  70.6 4.8 %all-to-all-start.1 = ((bf16[16,528,128]{2,1,0:T(8,128)(2,1)}), bf16[16,528,128]{2,1,0:T(8,128)(2,1)S(1)}, u32[]{:S(2)}, u32[]{:S(2)}) async-start(bf16[16,528,128]{2,1,0:T(8,128)(2,1)} %pad_maximum_fusion), calls=%async_computation.1 | async-start | bytes 4325376 | tf_op jit(solution)/shard_map/all_to_all | solution.py:89
  75.4 48.8 %all-to-all-done.1 = bf16[16,528,128]{2,1,0:T(8,128)(2,1)S(1)} async-done(((bf16[16,528,128]{2,1,0:T(8,128)(2,1)}), bf16[16,528,128]{2,1,0:T(8,128)(2,1)S(1)}, u32[]{:S(2)}, u32[]{:S(2)}) %all-to-all-start.1) | async-done | bytes 2162720 | tf_op jit(solution)/shard_map/all_to_all | solution.py:89
  124.2 0.2 fusion.43
  124.4 0.6 fusion.59
  125.6 1.6 %slice.36 = bf16[16,512,128]{2,1,0:T(8,128)(2,1)} slice(bf16[16,528,128]{2,1,0:T(8,128)(2,1)S(1)} %all-to-all-done.1), slice={[0:16], [0:512], [0:128]} | slice | bytes 4194304 | tf_op jit(solution)/shard_map/slice | solution.py:37
  127.2 2.3 %gather_fusion.3 = bf16[26,128,128]{2,1,0:T(8,128)(2,1)S(1)} fusion(bf16[64,128,128]{2,1,0:T(8,128)(2,1)} %bitcast.85, s32[1024]{0:T(1024)S(1)} %pad_clamp_fusion), kind=kCustom, calls=%fused_computation.3 | custom fusion | bytes 1704040 | tf_op jit(solution)/shard_map/jit(_take)/gather | solution.py:94
  129.5 0.4 fusion.9
  129.9 0.0 copy-start.1
  130.0 0.2 pad_maximum_fusion.1
  130.1 1.3 copy-done.1
  131.4 1.1 fusion.21
  132.5 0.8 copy.23
  (18 shorter events, 0.2 us)
Async XLA Ops:
  3.8 2.3 %copy-start = (bf16[26,2,128,128]{3,2,1,0:T(8,128)(2,1)S(1)}, bf16[26,2,128,128]{3,2,1,0:T(8,128)(2,1)}, u32[]{:S(2)}) copy-start(bf16[26,2,128,128]{3,2,1,0:T(8,128)(2,1)} %param.5) | copy-start | bytes 5111812
  10.6 55.3 %all-to-all-start = ((bf16[16,528,128]{2,1,0:T(8,128)(2,1)}), bf16[16,528,128]{2,1,0:T(8,128)(2,1)S(1)}, u32[]{:S(2)}, u32[]{:S(2)}) async-start(bf16[16,528,128]{2,1,0:T(8,128)(2,1)} %fusion.3), calls=%async_computation | async-start | bytes 4325376 | tf_op jit(solution)/shard_map/all_to_all | solution.py:75
  66.1 0.7 copy-start.2
  70.6 53.6 %all-to-all-start.1 = ((bf16[16,528,128]{2,1,0:T(8,128)(2,1)}), bf16[16,528,128]{2,1,0:T(8,128)(2,1)S(1)}, u32[]{:S(2)}, u32[]{:S(2)}) async-start(bf16[16,528,128]{2,1,0:T(8,128)(2,1)} %pad_maximum_fusion), calls=%async_computation.1 | async-start | bytes 4325376 | tf_op jit(solution)/shard_map/all_to_all | solution.py:89
  129.9 1.5 %copy-start.1 = (bf16[26,2,128,128]{3,2,1,0:T(8,128)(2,1)S(1)}, bf16[26,2,128,128]{3,2,1,0:T(8,128)(2,1)}, u32[]{:S(2)}) copy-start(bf16[26,2,128,128]{3,2,1,0:T(8,128)(2,1)} %param.5) | copy-start | bytes 5111812

commit v5 on v4

--- a/solution.py
+++ b/solution.py
@@ -83,15 +83,15 @@
     power_hi = local_power.astype(jnp.bfloat16).astype(jnp.float32)
     power_mid = (local_power - power_hi).astype(jnp.bfloat16).astype(jnp.float32)
     power_lo = local_power - power_hi - power_mid
-    power_parts = jnp.broadcast_to(jnp.stack([power_hi, power_mid, power_lo]), (devices, 3))
-    reply = jnp.take(weighted, jnp.minimum(labels_in, mic_units - 1), axis=0, mode="clip")
-    returned, powers_in = split_header(
-        lax.all_to_all(with_header(reply, power_parts, devices, capacity), "spk", 0, 0, tiled=True),
-        capacity, field_width, 3)
+    power_parts = jnp.stack([power_hi, power_mid, power_lo])[None, :]
+    shared = with_header(weighted, power_parts, 1, mic_units)[0]
+    gathered = lax.all_gather(shared, "spk")
     source_bin = jnp.arange(devices) // groups_per_bin
-    power_of = jnp.sum(powers_in.astype(jnp.float32), axis=1)
+    power_of = jnp.sum(gathered[:, mic_units * field_width, :3].astype(jnp.float32), axis=1)
     bin_power = jnp.sum(jnp.where(source_bin == my_bin, power_of, 0.0))
-    tile_weighted = jnp.take(returned, position, axis=0, mode="clip")
+    tile_weighted = jax.vmap(
+        lambda peer, row: lax.dynamic_slice(gathered, (peer, row, 0), (1, field_width, block_size))[0]
+    )(target_peer, target_label * field_width)
 
     back_rows = jnp.stack([tile_weighted, swap_halves(tile_weighted, -1)], axis=1)
     unit_mask = (local_unit[:, None] == jnp.arange(unit_count)[None, :]).astype(jnp.bfloat16)

time: 134 us -> 154 us (1.15); the launches traced: 133 us -> 151 us
  between operations: 2.18 us -> 15.7 us
  local copies, waits for them, and re-layouts: 12.6 us -> 20.9 us
  starting transfers between devices: 11.3 us -> 6.56 us
    all_gather x0 -> x1, waiting for transfers between devices: none -> 49.8 us  [per_device(): gathered = lax.all_gather(shared, 'spk')]
    all_to_all x1 -> x0, waiting for transfers between devices: 48.8 us -> none  [per_device(): lax.all_to_all(with_header(reply, power_parts, devices, capacity), 'spk',...]
    all_gather x0 -> x1, local copies, waits for them, and re-layouts: none -> 8.72 us  [per_device(): gathered = lax.all_gather(shared, 'spk')]
    all_to_all x1 -> x0, starting transfers between devices: 4.78 us -> none  [per_device(): lax.all_to_all(with_header(reply, power_parts, devices, capacity), 'spk',...]
    gather x2, local copies, waits for them, and re-layouts: 3.25 us -> 5.24 us  [per_device(): lax.dynamic_slice(gathered, (peer, row, 0), (1, field_width, block_size))[0]]
    slice x2 -> x1, local copies, waits for them, and re-layouts: 1.77 us -> 0.21 us  [split_header(): body = buffer[:, :capacity * rows].reshape(-1, rows, buffer.shape[2])]
where the time goes in v5:
time: 154 us; the launch traced here: 151 us
  waiting for transfers between devices  94.3 us (61%)
  local copies, waits for them, and re-layouts  20.9 us (14%)
  between operations  15.7 us (10%)
  other arithmetic  8.86 us (6%)
  starting transfers between devices  6.56 us (4%)
  matrix products  5.07 us (3%)
    all_gather x1, waiting for transfers between devices, per_device(): gathered = lax.all_gather(shared, 'spk')  49.8 us
    all_to_all x1, waiting for transfers between devices, per_device(): lax.all_to_all(sent, 'spk', 0, 0, tiled=True)  44.4 us
    all_gather x1, local copies, waits for them, and re-layouts, per_device(): gathered = lax.all_gather(shared, 'spk')  8.72 us
    all_to_all x1, starting transfers between devices, per_device(): lax.all_to_all(sent, 'spk', 0, 0, tiled=True)  6.52 us
    gather x2, local copies, waits for them, and re-layouts, per_device(): lax.dynamic_slice(gathered, (peer, row, 0), (1, field_width, block_size))[0]  5.24 us
  transfers between devices with their start and end apart: 2, of which 2 were waited for; matrix products, arithmetic and copies ran while one was open for 2% of the time, Pallas kernels for 0%

profile of v5, /device:TPU:13, one launch (start us, length us, event | category | flops | bytes accessed | tf_op | source)
XLA Modules:
  0.0 151.3 jit_solution(8606303839995725628)
XLA Ops:
  6.5 0.7 fusion.67
  7.2 0.8 fusion.68
  8.1 0.1 fusion.43
  8.2 0.8 gather_fusion.3
  9.0 0.1 fusion.39
  9.1 0.1 select_reduce_fusion.1
  9.2 0.1 convert_element_type.128
  9.3 1.0 copy.32
  10.3 0.0 copy-start
  10.3 0.2 fusion.26
  10.6 2.0 %gather_fusion = bf16[26,2,128,128]{3,2,1,0:T(8,128)(2,1)} fusion(bf16[2,2,128,128]{3,2,0,1:T(8,128)(2,1)S(1)} %pad_maximum_fusion.2, s32[1024]{0:T(1024)S(1)} %pad_clamp_fusion.1), kind=kCustom, calls=%fused_computation | custom fusion | bytes 3407976 | tf_op jit(solution)/shard_map/gather | solution.py:69
  12.6 0.0 copy-done
  12.6 2.1 %bitcast_convert_fusion = bf16[26,128,128]{2,1,0:T(8,128)(2,1)S(1)} fusion(bf16[26,2,128,128]{3,2,1,0:T(8,128)(2,1)} %gather_fusion, bf16[26,2,128,128]{3,2,1,0:T(8,128)(2,1)S(1)} %copy-done), kind=kOutput, calls=%fused_computation.14 | convolution fusion | flops 218529792 | bytes 4259840 | tf_op jit(solution)/shard_map/tcij,tckj->tki/dot_general | solution.py:70
  14.6 1.0 gather_fusion.1
  15.6 1.5 fusion.3
  17.1 6.5 %all-to-all-start = ((bf16[16,528,128]{2,1,0:T(8,128)(2,1)}), bf16[16,528,128]{2,1,0:T(8,128)(2,1)S(1)}, u32[]{:S(2)}, u32[]{:S(2)}) async-start(bf16[16,528,128]{2,1,0:T(8,128)(2,1)} %fusion.3), calls=%async_computation | async-start | bytes 4325376 | tf_op jit(solution)/shard_map/all_to_all | solution.py:75
  23.6 0.0 all-gather.2.cloned.1.call-start
  23.7 2.9 %multiply_reduce_fusion = f32[]{:T(128)} fusion(bf16[26,2,128,128]{3,2,1,0:T(8,128)(2,1)} %param.5), kind=kLoop, calls=%fused_computation.8 | loop fusion | flops 2555903 | bytes 1703940 | tf_op jit(solution)/shard_map/reduce_sum | solution.py:82
  27.9 0.1 fusion.54
  28.0 44.4 %all-to-all-done = bf16[16,528,128]{2,1,0:T(8,128)(2,1)S(1)} async-done(((bf16[16,528,128]{2,1,0:T(8,128)(2,1)}), bf16[16,528,128]{2,1,0:T(8,128)(2,1)S(1)}, u32[]{:S(2)}, u32[]{:S(2)}) %all-to-all-start) | async-done | bytes 2162720 | tf_op jit(solution)/shard_map/all_to_all | solution.py:75
  72.5 0.1 reshape.220
  72.6 0.0 copy-start.2
  72.6 0.2 slice.30
  72.8 0.5 copy-done.2
  73.3 1.2 fusion.13
  74.5 0.7 pad_maximum_fusion.1
  75.2 0.0 all-gather.2.cloned.1.call-update
  75.3 49.8 %all-gather.2.cloned.1.call-done = bf16[16,1040,128]{2,1,0:T(8,128)(2,1)} async-done(((bf16[1,1040,128]{2,1,0:T(8,128)(2,1)}), bf16[16,1040,128]{2,1,0:T(8,128)(2,1)}) %all-gather.2.cloned.1.call-update) | async-done | bytes 4259856 | tf_op jit(solution)/shard_map/all_gather | solution.py:88
  125.1 1.0 fusion.44
  126.1 0.6 fusion.60
  126.7 8.7 %copy.36 = bf16[16,1040,128]{2,0,1:T(8,128)(2,1)} copy(bf16[16,1040,128]{2,1,0:T(8,128)(2,1)} %all-gather.2.cloned.1.call-done) | data formatting | bytes 8519680 | tf_op jit(solution)/shard_map/all_gather | solution.py:88
  135.4 4.9 %gather_fusion.2 = bf16[26,128,128]{2,0,1:T(8,128)(2,1)S(1)} fusion(bf16[16,1040,128]{2,0,1:T(8,128)(2,1)} %copy.36, s32[26]{0:T(128)S(1)} %get-tuple-element.7), kind=kCustom, calls=%fused_computation.2 | custom fusion | bytes 1704248 | tf_op jit(solution)/shard_map/vmap()/gather | solution.py:93
  140.3 0.3 copy.63
  140.7 0.5 fusion.9
  141.1 0.0 copy-start.1
  141.9 0.2 pad_maximum_fusion
  142.1 0.5 copy-done.1
  142.6 1.1 fusion.21
  143.7 0.8 copy.41
  (16 shorter events, 0.2 us)
Async XLA Ops:
  10.3 2.3 %copy-start = (bf16[26,2,128,128]{3,2,1,0:T(8,128)(2,1)S(1)}, bf16[26,2,128,128]{3,2,1,0:T(8,128)(2,1)}, u32[]{:S(2)}) copy-start(bf16[26,2,128,128]{3,2,1,0:T(8,128)(2,1)} %param.5) | copy-start | bytes 5111812
  17.1 55.3 %all-to-all-start = ((bf16[16,528,128]{2,1,0:T(8,128)(2,1)}), bf16[16,528,128]{2,1,0:T(8,128)(2,1)S(1)}, u32[]{:S(2)}, u32[]{:S(2)}) async-start(bf16[16,528,128]{2,1,0:T(8,128)(2,1)} %fusion.3), calls=%async_computation | async-start | bytes 4325376 | tf_op jit(solution)/shard_map/all_to_all | solution.py:75
  23.6 101.5 %all-gather.2.cloned.1.call-start = ((), (), s32[]{:S(2)}) async-start(), calls=%async_computation.1 | async-start | bytes 4526080 | tf_op jit(solution)/shard_map/all_gather | solution.py:88
  72.6 0.7 copy-start.2
  141.1 1.5 copy-start.1
Sparse Core Ops, SparseCore 0:
  75.4 49.6 all-gather.1

commit v6 on v4

--- a/solution.py
+++ b/solution.py
@@ -64,39 +64,63 @@
         send_hit.any(axis=1), jnp.sum(jnp.where(send_hit, target_label, 0), axis=1), mic_units
     )
 
+    chunks = 2
+    fields = field_width // 2
+    per_chunk = fields // chunks
     rounded = jnp.swapaxes(direction.astype(jnp.bfloat16), 1, 2)
-    both = jnp.stack([rounded, swap_halves(rounded, 1)], axis=1)
-    pair_rows = both[local_unit]
-    partial_field = jnp.einsum("tcij,tckj->tki", plant, pair_rows,
-                               preferred_element_type=jnp.float32).astype(jnp.bfloat16)
-    outgoing = jnp.take(partial_field, slot_pair, axis=0, mode="clip")
-    sent = with_header(outgoing, slot_label.reshape(devices, capacity), devices, capacity)
-    arrived, labels_in = split_header(
-        lax.all_to_all(sent, "spk", 0, 0, tiled=True), capacity, field_width, capacity)
-    labels_in = labels_in.astype(jnp.int32).reshape(slots)
-    recv_onehot = (labels_in[None, :] == jnp.arange(mic_units)[:, None]).astype(jnp.bfloat16)
-    pressure = jnp.einsum("ms,ski->mki", recv_onehot, arrived, preferred_element_type=jnp.float32)
     weights_flat = mic_weight.reshape(mic_units, block_size)
-    weighted = (weights_flat[:, None, :] * pressure).astype(jnp.bfloat16)
-
+    unit_mask = (local_unit[:, None] == jnp.arange(unit_count)[None, :]).astype(jnp.bfloat16)
     local_power = jnp.sum(jnp.square(plant.astype(jnp.float32)))
     power_hi = local_power.astype(jnp.bfloat16).astype(jnp.float32)
     power_mid = (local_power - power_hi).astype(jnp.bfloat16).astype(jnp.float32)
     power_lo = local_power - power_hi - power_mid
     power_parts = jnp.broadcast_to(jnp.stack([power_hi, power_mid, power_lo]), (devices, 3))
-    reply = jnp.take(weighted, jnp.minimum(labels_in, mic_units - 1), axis=0, mode="clip")
-    returned, powers_in = split_header(
-        lax.all_to_all(with_header(reply, power_parts, devices, capacity), "spk", 0, 0, tiled=True),
-        capacity, field_width, 3)
     source_bin = jnp.arange(devices) // groups_per_bin
-    power_of = jnp.sum(powers_in.astype(jnp.float32), axis=1)
-    bin_power = jnp.sum(jnp.where(source_bin == my_bin, power_of, 0.0))
-    tile_weighted = jnp.take(returned, position, axis=0, mode="clip")
 
-    back_rows = jnp.stack([tile_weighted, swap_halves(tile_weighted, -1)], axis=1)
-    unit_mask = (local_unit[:, None] == jnp.arange(unit_count)[None, :]).astype(jnp.bfloat16)
-    masked = back_rows[:, None] * unit_mask[:, :, None, None, None]
-    gram = jnp.einsum("tcij,tucki->ujk", plant, masked, preferred_element_type=jnp.float32)
+    labels_in = None
+    bin_power = None
+    real_parts, imag_parts = [], []
+    for chunk in range(chunks):
+        lo = chunk * per_chunk
+        cols = jnp.concatenate([rounded[:, lo:lo + per_chunk], rounded[:, fields + lo:fields + lo + per_chunk]], axis=1)
+        width = 2 * per_chunk
+        both = jnp.stack([cols, swap_halves(cols, 1)], axis=1)
+        pair_rows = both[local_unit]
+        partial_field = jnp.einsum("tcij,tckj->tki", plant, pair_rows,
+                                   preferred_element_type=jnp.float32).astype(jnp.bfloat16)
+        outgoing = jnp.take(partial_field, slot_pair, axis=0, mode="clip")
+        if chunk == 0:
+            sent = with_header(outgoing, slot_label.reshape(devices, capacity), devices, capacity)
+            arrived, header_in = split_header(
+                lax.all_to_all(sent, "spk", 0, 0, tiled=True), capacity, width, capacity)
+            labels_in = header_in.astype(jnp.int32).reshape(slots)
+        else:
+            arrived = lax.all_to_all(
+                outgoing.reshape(devices, capacity * width, block_size), "spk", 0, 0, tiled=True
+            ).reshape(slots, width, block_size)
+        recv_onehot = (labels_in[None, :] == jnp.arange(mic_units)[:, None]).astype(jnp.bfloat16)
+        pressure = jnp.einsum("ms,ski->mki", recv_onehot, arrived, preferred_element_type=jnp.float32)
+        weighted = (weights_flat[:, None, :] * pressure).astype(jnp.bfloat16)
+
+        reply = jnp.take(weighted, jnp.minimum(labels_in, mic_units - 1), axis=0, mode="clip")
+        if chunk == 0:
+            returned, powers_in = split_header(
+                lax.all_to_all(with_header(reply, power_parts, devices, capacity), "spk", 0, 0, tiled=True),
+                capacity, width, 3)
+            power_of = jnp.sum(powers_in.astype(jnp.float32), axis=1)
+            bin_power = jnp.sum(jnp.where(source_bin == my_bin, power_of, 0.0))
+        else:
+            returned = lax.all_to_all(
+                reply.reshape(devices, capacity * width, block_size), "spk", 0, 0, tiled=True
+            ).reshape(slots, width, block_size)
+        tile_weighted = jnp.take(returned, position, axis=0, mode="clip")
+
+        back_rows = jnp.stack([tile_weighted, swap_halves(tile_weighted, -1)], axis=1)
+        masked = back_rows[:, None] * unit_mask[:, :, None, None, None]
+        gram = jnp.einsum("tcij,tucki->ujk", plant, masked, preferred_element_type=jnp.float32)
+        real_parts.append(gram[..., :per_chunk])
+        imag_parts.append(gram[..., per_chunk:])
+    gram = jnp.concatenate(real_parts + imag_parts, axis=-1)
     return gram + reg_weight * bin_power / SPEAKERS * direction
 
 

time: 134 us -> 142 us (1.060)
  starting transfers between devices: 11.3 us -> 21 us
  waiting for transfers between devices: 93.3 us -> 88.3 us
  matrix products: 5.02 us -> 7.46 us
  local copies, waits for them, and re-layouts: 12.6 us -> 15 us
  other arithmetic: 8.9 us -> 7.36 us
    all_to_all x0 -> x2, waiting for transfers between devices: none -> 44.2 us  [the longest x1 24.7 us: per_device(): lax.all_to_all(outgoing.reshape(devices, capacity * width, block_size), '...]
    all_to_all x1, waiting for transfers between devices: 48.8 us -> 23.3 us  [per_device(): lax.all_to_all(with_header(reply, power_parts, devices, capacity), 'spk',...]
    all_to_all x1, waiting for transfers between devices: 44.5 us -> 20.9 us  [per_device(): lax.all_to_all(sent, 'spk', 0, 0, tiled=True)]
    all_to_all x0 -> x2, starting transfers between devices: none -> 9.65 us  [the longest x1 4.83 us: per_device(): lax.all_to_all(reply.reshape(devices, capacity * width, block_size), 'spk...]
    unnamed x8 -> x6, local copies, waits for them, and re-layouts: 2.77 us -> 1.02 us
    gather x1 -> x2, local copies, waits for them, and re-layouts: 0.95 us -> 2.45 us  [per_device(): outgoing = jnp.take(partial_field, slot_pair, axis=0, mode='clip')]
    gather x1 -> x2, local copies, waits for them, and re-layouts: 0.95 us -> 2.43 us  [per_device(): jnp.take(weighted, jnp.minimum(labels_in, mic_units - 1), axis=0, mode='c...]
    reduce_sum x1, other arithmetic: 2.93 us -> 1.47 us  [per_device(): local_power = jnp.sum(jnp.square(plant.astype(jnp.float32)))]
  transfers between devices with their start and end apart: 2 -> 4, of which waited for: 2 -> 4; matrix products, arithmetic and copies ran while one was open for 2% -> 9% of each run, Pallas kernels for 0% -> 0%
where the time goes in v6:
time: 142 us; the launch traced here: 141 us
  waiting for transfers between devices  88.3 us (62%)
  starting transfers between devices  21 us (15%)
  local copies, waits for them, and re-layouts  15 us (11%)
  matrix products  7.46 us (5%)
  other arithmetic  7.36 us (5%)
  between operations  2.25 us (2%)
    all_to_all x1, waiting for transfers between devices, per_device(): lax.all_to_all(outgoing.reshape(devices, capacity * width, block_size), '...  24.7 us
    all_to_all x1, waiting for transfers between devices, per_device(): lax.all_to_all(with_header(reply, power_parts, devices, capacity), 'spk',...  23.3 us
    all_to_all x1, waiting for transfers between devices, per_device(): lax.all_to_all(sent, 'spk', 0, 0, tiled=True)  20.9 us
    all_to_all x1, waiting for transfers between devices, per_device(): lax.all_to_all(reply.reshape(devices, capacity * width, block_size), 'spk...  19.5 us
    all_to_all x1, starting transfers between devices, per_device(): lax.all_to_all(sent, 'spk', 0, 0, tiled=True)  6.52 us
    all_to_all x1, starting transfers between devices, per_device(): lax.all_to_all(with_header(reply, power_parts, devices, capacity), 'spk',...  4.83 us
    all_to_all x1, starting transfers between devices, per_device(): lax.all_to_all(reply.reshape(devices, capacity * width, block_size), 'spk...  4.83 us
    all_to_all x1, starting transfers between devices, per_device(): lax.all_to_all(outgoing.reshape(devices, capacity * width, block_size), '...  4.82 us
  transfers between devices with their start and end apart: 4, of which 4 were waited for; matrix products, arithmetic and copies ran while one was open for 9% of the time, Pallas kernels for 0%

profile of v6, /device:TPU:13, one launch (start us, length us, event | category | flops | bytes accessed | tf_op | source)
XLA Modules:
  0.0 141.4 jit_solution(5400895164674993980)
XLA Ops:
  0.0 0.0 copy-start
  0.0 0.8 fusion.86
  0.9 0.1 fusion.47
  1.0 0.8 gather_fusion.8
  1.8 0.7 bitcast_add_fusion
  2.5 0.1 fusion.42
  2.6 0.7 fusion.78
  3.3 0.1 select_reduce_fusion
  3.4 0.1 convert_element_type.170
  3.5 1.0 copy.21
  4.6 0.2 fusion.24
  4.8 0.7 gather_fusion
  5.5 0.0 copy-done
  5.5 0.7 fusion.7
  6.2 0.8 gather_fusion.1
  7.0 1.1 fusion.23
  8.1 6.5 %all-to-all-start = ((bf16[16,272,128]{2,1,0:T(8,128)(2,1)}), bf16[16,272,128]{2,1,0:T(8,128)(2,1)S(1)}, u32[]{:S(2)}, u32[]{:S(2)}) async-start(bf16[16,272,128]{2,1,0:T(8,128)(2,1)} %fusion.23), calls=%async_computation | async-start | bytes 2228224 | tf_op jit(solution)/shard_map/all_to_all | solution.py:95
  14.6 0.2 fusion.25
  14.8 1.6 %gather_fusion.4 = bf16[26,2,64,128]{3,2,1,0:T(8,128)(2,1)} fusion(bf16[2,2,64,128]{3,2,0,1:T(8,128)(2,1)S(1)} %pad_maximum_fusion.4, s32[1024]{0:T(1024)S(1)} %pad_clamp_fusion.3), kind=kCustom, calls=%fused_computation.4 | custom fusion | bytes 1704040 | tf_op jit(solution)/shard_map/gather | solution.py:88
  16.4 1.9 %fusion.8 = bf16[26,64,128]{2,1,0:T(8,128)(2,1)S(1)} fusion(bf16[26,2,64,128]{3,2,1,0:T(8,128)(2,1)} %gather_fusion.4, bf16[26,2,128,128]{3,2,1,0:T(8,128)(2,1)S(1)} %copy-done), kind=kOutput, calls=%fused_computation.21 | convolution fusion | flops 109264896 | bytes 2981888 | tf_op jit(solution)/shard_map/tcij,tckj->tki/dot_general | solution.py:89
  18.3 0.0 copy-start.1
  18.3 1.7 %gather_fusion.5 = bf16[64,64,128]{2,1,0:T(8,128)(2,1)} fusion(bf16[26,64,128]{2,1,0:T(8,128)(2,1)S(1)} %fusion.8, s32[1024]{0:T(1024)S(1)} %pad_clamp_fusion.2), kind=kCustom, calls=%fused_computation.5 | custom fusion | bytes 2097408 | tf_op jit(solution)/shard_map/jit(_take)/gather | solution.py:91
  20.0 20.9 %all-to-all-done = bf16[16,272,128]{2,1,0:T(8,128)(2,1)S(1)} async-done(((bf16[16,272,128]{2,1,0:T(8,128)(2,1)}), bf16[16,272,128]{2,1,0:T(8,128)(2,1)S(1)}, u32[]{:S(2)}, u32[]{:S(2)}) %all-to-all-start) | async-done | bytes 1114144 | tf_op jit(solution)/shard_map/all_to_all | solution.py:95
  40.9 4.8 %all-to-all-start.2 = ((bf16[16,256,128]{2,1,0:T(8,128)(2,1)}), bf16[16,256,128]{2,1,0:T(8,128)(2,1)}, u32[]{:S(2)}, u32[]{:S(2)}) async-start(bf16[16,256,128]{2,1,0:T(8,128)(2,1)} %bitcast.116), calls=%async_computation.2 | async-start | bytes 2097152 | tf_op jit(solution)/shard_map/all_to_all | solution.py:98
  45.7 0.1 minimum_reduce_fusion
  45.7 0.1 reshape.259
  45.8 0.1 reshape.240
  45.9 24.7 %all-to-all-done.2 = bf16[16,256,128]{2,1,0:T(8,128)(2,1)} async-done(((bf16[16,256,128]{2,1,0:T(8,128)(2,1)}), bf16[16,256,128]{2,1,0:T(8,128)(2,1)}, u32[]{:S(2)}, u32[]{:S(2)}) %all-to-all-start.2) | async-done | bytes 1048608 | tf_op jit(solution)/shard_map/all_to_all | solution.py:98
  70.6 0.0 copy-done.1
  70.6 1.9 %fusion.12 = bf16[8,64,128]{2,0,1:T(8,128)(2,1)S(1)} fusion(bf16[64,64,128]{2,1,0:T(8,128)(2,1)} %bitcast.40, f32[8,128]{1,0:T(8,128)S(1)} %bitcast.123, s32[64]{0:T(128)S(1)} %reshape.240), kind=kOutput, calls=%fused_computation.29 | convolution fusion | flops 8520192 | bytes 1184000 | tf_op jit(solution)/shard_map/ms,ski->mki/dot_general | solution.py:102
  72.6 1.7 %gather_fusion.6 = bf16[64,64,128]{2,1,0:T(8,128)(2,1)} fusion(bf16[8,64,128]{2,1,0:T(8,128)(2,1)S(1)} %copy.27, s32[1024]{0:T(1024)S(1)} %pad_clamp_fusion.1), kind=kCustom, calls=%fused_computation.6 | custom fusion | bytes 2097408 | tf_op jit(solution)/shard_map/jit(_take)/gather | solution.py:105
  74.2 4.8 %all-to-all-start.3 = ((bf16[16,256,128]{2,1,0:T(8,128)(2,1)}), bf16[16,256,128]{2,1,0:T(8,128)(2,1)}, u32[]{:S(2)}, u32[]{:S(2)}) async-start(bf16[16,256,128]{2,1,0:T(8,128)(2,1)} %bitcast.115), calls=%async_computation.3 | async-start | bytes 2097152 | tf_op jit(solution)/shard_map/all_to_all | solution.py:113
  79.1 1.5 %multiply_reduce_fusion = f32[]{:T(128)} fusion(bf16[26,2,128,128]{3,2,1,0:T(8,128)(2,1)S(1)} %copy-done), kind=kLoop, calls=%fused_computation.9 | loop fusion | flops 2555903 | bytes 1703940 | tf_op jit(solution)/shard_map/reduce_sum | solution.py:73
  81.8 0.1 fusion.66
  81.9 0.1 slice.77
  82.0 0.7 fusion.11
  82.7 0.7 gather_fusion.2
  83.5 1.1 pad_maximum_fusion
  84.6 19.5 %all-to-all-done.3 = bf16[16,256,128]{2,1,0:T(8,128)(2,1)} async-done(((bf16[16,256,128]{2,1,0:T(8,128)(2,1)}), bf16[16,256,128]{2,1,0:T(8,128)(2,1)}, u32[]{:S(2)}, u32[]{:S(2)}) %all-to-all-start.3) | async-done | bytes 1048608 | tf_op jit(solution)/shard_map/all_to_all | solution.py:113
  104.0 4.8 %all-to-all-start.1 = ((bf16[16,272,128]{2,1,0:T(8,128)(2,1)}), bf16[16,272,128]{2,1,0:T(8,128)(2,1)S(1)}, u32[]{:S(2)}, u32[]{:S(2)}) async-start(bf16[16,272,128]{2,1,0:T(8,128)(2,1)} %pad_maximum_fusion), calls=%async_computation.1 | async-start | bytes 2228224 | tf_op jit(solution)/shard_map/all_to_all | solution.py:108
  108.9 1.9 %gather_fusion.7 = bf16[26,64,128]{2,1,0:T(8,128)(2,1)S(1)} fusion(bf16[64,64,128]{2,1,0:T(8,128)(2,1)} %bitcast.42, s32[1024]{0:T(1024)S(1)} %pad_clamp_fusion), kind=kCustom, calls=%fused_computation.7 | custom fusion | bytes 852072 | tf_op jit(solution)/shard_map/jit(_take)/gather | solution.py:116
  110.7 0.3 fusion.10
  111.1 0.1 pad_maximum_fusion.2
  111.2 0.7 fusion.18
  111.8 23.3 %all-to-all-done.1 = bf16[16,272,128]{2,1,0:T(8,128)(2,1)S(1)} async-done(((bf16[16,272,128]{2,1,0:T(8,128)(2,1)}), bf16[16,272,128]{2,1,0:T(8,128)(2,1)S(1)}, u32[]{:S(2)}, u32[]{:S(2)}) %all-to-all-start.1) | async-done | bytes 1114144 | tf_op jit(solution)/shard_map/all_to_all | solution.py:108
  135.1 0.2 fusion.48
  135.3 0.6 fusion.74
  135.9 1.1 slice.78
  137.0 1.9 %gather_fusion.3 = bf16[26,64,128]{2,1,0:T(8,128)(2,1)S(1)} fusion(bf16[64,64,128]{2,1,0:T(8,128)(2,1)} %bitcast.122, s32[1024]{0:T(1024)S(1)} %pad_clamp_fusion), kind=kCustom, calls=%fused_computation.3 | custom fusion | bytes 852072 | tf_op jit(solution)/shard_map/jit(_take)/gather | solution.py:116
  138.9 0.3 fusion.9
  139.2 0.1 pad_maximum_fusion.1
  139.3 0.6 fusion.13
  140.6 0.8 copy.30
  (24 shorter events, 0.3 us)
Async XLA Ops:
  0.0 5.5 %copy-start = (bf16[26,2,128,128]{3,2,1,0:T(8,128)(2,1)S(1)}, bf16[26,2,128,128]{3,2,1,0:T(8,128)(2,1)}, u32[]{:S(2)}) copy-start(bf16[26,2,128,128]{3,2,1,0:T(8,128)(2,1)} %param.5) | copy-start | bytes 5111812
  8.1 32.8 %all-to-all-start = ((bf16[16,272,128]{2,1,0:T(8,128)(2,1)}), bf16[16,272,128]{2,1,0:T(8,128)(2,1)S(1)}, u32[]{:S(2)}, u32[]{:S(2)}) async-start(bf16[16,272,128]{2,1,0:T(8,128)(2,1)} %fusion.23), calls=%async_computation | async-start | bytes 2228224 | tf_op jit(solution)/shard_map/all_to_all | solution.py:95
  18.3 52.4 %copy-start.1 = (f32[1,8,128]{2,1,0:T(8,128)S(1)}, f32[1,8,128]{2,1,0:T(8,128)}, u32[]{:S(2)}) copy-start(f32[1,8,128]{2,1,0:T(8,128)} %param.7) | copy-start | bytes 12292
  40.9 29.8 %all-to-all-start.2 = ((bf16[16,256,128]{2,1,0:T(8,128)(2,1)}), bf16[16,256,128]{2,1,0:T(8,128)(2,1)}, u32[]{:S(2)}, u32[]{:S(2)}) async-start(bf16[16,256,128]{2,1,0:T(8,128)(2,1)} %bitcast.116), calls=%async_computation.2 | async-start | bytes 2097152 | tf_op jit(solution)/shard_map/all_to_all | solution.py:98
  74.2 29.8 %all-to-all-start.3 = ((bf16[16,256,128]{2,1,0:T(8,128)(2,1)}), bf16[16,256,128]{2,1,0:T(8,128)(2,1)}, u32[]{:S(2)}, u32[]{:S(2)}) async-start(bf16[16,256,128]{2,1,0:T(8,128)(2,1)} %bitcast.115), calls=%async_computation.3 | async-start | bytes 2097152 | tf_op jit(solution)/shard_map/all_to_all | solution.py:113
  104.0 31.1 %all-to-all-start.1 = ((bf16[16,272,128]{2,1,0:T(8,128)(2,1)}), bf16[16,272,128]{2,1,0:T(8,128)(2,1)S(1)}, u32[]{:S(2)}, u32[]{:S(2)}) async-start(bf16[16,272,128]{2,1,0:T(8,128)(2,1)} %pad_maximum_fusion), calls=%async_computation.1 | async-start | bytes 2228224 | tf_op jit(solution)/shard_map/all_to_all | solution.py:108

commit v7 on v4

--- a/solution.py
+++ b/solution.py
@@ -70,27 +70,29 @@
     partial_field = jnp.einsum("tcij,tckj->tki", plant, pair_rows,
                                preferred_element_type=jnp.float32).astype(jnp.bfloat16)
     outgoing = jnp.take(partial_field, slot_pair, axis=0, mode="clip")
-    sent = with_header(outgoing, slot_label.reshape(devices, capacity), devices, capacity)
-    arrived, labels_in = split_header(
-        lax.all_to_all(sent, "spk", 0, 0, tiled=True), capacity, field_width, capacity)
-    labels_in = labels_in.astype(jnp.int32).reshape(slots)
+    squares = jnp.square(plant.astype(jnp.float32)).reshape(-1, block_size)
+    local_power = jnp.sum(jnp.sum(squares, axis=0))
+    power_hi = local_power.astype(jnp.bfloat16).astype(jnp.float32)
+    power_mid = (local_power - power_hi).astype(jnp.bfloat16).astype(jnp.float32)
+    power_lo = local_power - power_hi - power_mid
+    power_parts = jnp.broadcast_to(jnp.stack([power_hi, power_mid, power_lo]), (devices, 3))
+    header = jnp.concatenate([slot_label.reshape(devices, capacity).astype(jnp.float32), power_parts], axis=1)
+    sent = with_header(outgoing, header, devices, capacity)
+    arrived, header_in = split_header(
+        lax.all_to_all(sent, "spk", 0, 0, tiled=True), capacity, field_width, capacity + 3)
+    labels_in = header_in[:, :capacity].astype(jnp.int32).reshape(slots)
+    source_bin = jnp.arange(devices) // groups_per_bin
+    power_of = jnp.sum(header_in[:, capacity:].astype(jnp.float32), axis=1)
+    bin_power = jnp.sum(jnp.where(source_bin == my_bin, power_of, 0.0))
     recv_onehot = (labels_in[None, :] == jnp.arange(mic_units)[:, None]).astype(jnp.bfloat16)
     pressure = jnp.einsum("ms,ski->mki", recv_onehot, arrived, preferred_element_type=jnp.float32)
     weights_flat = mic_weight.reshape(mic_units, block_size)
     weighted = (weights_flat[:, None, :] * pressure).astype(jnp.bfloat16)
 
-    local_power = jnp.sum(jnp.square(plant.astype(jnp.float32)))
-    power_hi = local_power.astype(jnp.bfloat16).astype(jnp.float32)
-    power_mid = (local_power - power_hi).astype(jnp.bfloat16).astype(jnp.float32)
-    power_lo = local_power - power_hi - power_mid
-    power_parts = jnp.broadcast_to(jnp.stack([power_hi, power_mid, power_lo]), (devices, 3))
     reply = jnp.take(weighted, jnp.minimum(labels_in, mic_units - 1), axis=0, mode="clip")
-    returned, powers_in = split_header(
-        lax.all_to_all(with_header(reply, power_parts, devices, capacity), "spk", 0, 0, tiled=True),
-        capacity, field_width, 3)
-    source_bin = jnp.arange(devices) // groups_per_bin
-    power_of = jnp.sum(powers_in.astype(jnp.float32), axis=1)
-    bin_power = jnp.sum(jnp.where(source_bin == my_bin, power_of, 0.0))
+    returned = lax.all_to_all(
+        reply.reshape(devices, capacity * field_width, block_size), "spk", 0, 0, tiled=True
+    ).reshape(slots, field_width, block_size)
     tile_weighted = jnp.take(returned, position, axis=0, mode="clip")
 
     back_rows = jnp.stack([tile_weighted, swap_halves(tile_weighted, -1)], axis=1)

time: 134 us -> 131 us (0.978)
  blocking collectives: 0 us -> 55.1 us
  waiting for transfers between devices: 93.3 us -> 46.1 us
  starting transfers between devices: 11.3 us -> 5.78 us
  other arithmetic: 8.9 us -> 5.86 us
  local copies, waits for them, and re-layouts: 12.6 us -> 10.1 us
    all_to_all x0 -> x1, blocking collectives: none -> 55.1 us  [per_device(): lax.all_to_all(sent, 'spk', 0, 0, tiled=True)]
    all_to_all x2 -> x1, waiting for transfers between devices: 93.3 us -> 46.1 us  [per_device(): lax.all_to_all(reply.reshape(devices, capacity * field_width, block_size)...]
    all_to_all x2 -> x1, starting transfers between devices: 11.3 us -> 5.78 us  [per_device(): lax.all_to_all(reply.reshape(devices, capacity * field_width, block_size)...]
    concatenate x2 -> x1, other arithmetic: 2.99 us -> 0.15 us  [with_header(): return jnp.concatenate([body, head], axis=1)]
    gather x1, local copies, waits for them, and re-layouts: 2.3 us -> 0.71 us  [per_device(): tile_weighted = jnp.take(returned, position, axis=0, mode='clip')]
    slice x2 -> x1, local copies, waits for them, and re-layouts: 1.77 us -> 0.21 us  [split_header(): body = buffer[:, :capacity * rows].reshape(-1, rows, buffer.shape[2])]
    unnamed x8 -> x12, local copies, waits for them, and re-layouts: 2.77 us -> 1.96 us
  transfers between devices with their start and end apart: 2 -> 1, of which waited for: 2 -> 1; matrix products, arithmetic and copies ran while one was open for 2% -> 0% of each run, Pallas kernels for 0% -> 0%
where the time goes in v7:
time: 131 us; the launch traced here: 130 us
  blocking collectives  55.1 us (42%)
  waiting for transfers between devices  46.1 us (35%)
  local copies, waits for them, and re-layouts  10.1 us (8%)
  other arithmetic  5.86 us (4%)
  starting transfers between devices  5.78 us (4%)
  matrix products  5.02 us (4%)
  between operations  2.17 us (2%)
    all_to_all x1, blocking collectives, per_device(): lax.all_to_all(sent, 'spk', 0, 0, tiled=True)  55.1 us
    all_to_all x1, waiting for transfers between devices, per_device(): lax.all_to_all(reply.reshape(devices, capacity * field_width, block_size)...  46.1 us
    all_to_all x1, starting transfers between devices, per_device(): lax.all_to_all(reply.reshape(devices, capacity * field_width, block_size)...  5.78 us
    reduce_sum x1, other arithmetic, per_device(): local_power = jnp.sum(jnp.sum(squares, axis=0))  2.95 us
  transfers between devices with their start and end apart: 1, of which 1 were waited for; matrix products, arithmetic and copies ran while one was open for 0% of the time, Pallas kernels for 0%

profile of v7, /device:TPU:13, one launch (start us, length us, event | category | flops | bytes accessed | tf_op | source)
XLA Modules:
  0.0 130.2 jit_solution(3223129042737353984)
XLA Ops:
  0.0 0.0 copy-start.2
  0.0 0.8 fusion.56
  0.8 0.1 fusion.42
  0.9 0.8 gather_fusion.4
  1.7 0.7 fusion.52
  2.4 0.1 fusion.38
  2.5 0.1 select_reduce_fusion.1
  2.6 0.1 concatenate.16
  2.7 2.9 %multiply_reduce_fusion = f32[]{:T(128)} fusion(bf16[26,2,128,128]{3,2,1,0:T(8,128)(2,1)} %param.5), kind=kLoop, calls=%fused_computation.9 | loop fusion | flops 2555903 | bytes 1703940 | tf_op jit(solution)/shard_map/reduce_sum | solution.py:74
  7.0 0.1 maximum_convert_fusion
  7.1 0.1 pad.10.clone
  7.2 0.0 copy-done.2
  7.2 0.1 copy.34
  7.3 0.0 copy-start
  7.3 0.2 fusion.26
  7.6 2.0 %gather_fusion = bf16[26,2,128,128]{3,2,1,0:T(8,128)(2,1)} fusion(bf16[2,2,128,128]{3,2,0,1:T(8,128)(2,1)S(1)} %pad_maximum_fusion.1, s32[1024]{0:T(1024)S(1)} %pad_clamp_fusion.3), kind=kCustom, calls=%fused_computation | custom fusion | bytes 3407976 | tf_op jit(solution)/shard_map/gather | solution.py:69
  9.5 0.0 copy-done
  9.6 2.1 %bitcast_convert_fusion = bf16[26,128,128]{2,1,0:T(8,128)(2,1)S(1)} fusion(bf16[26,2,128,128]{3,2,1,0:T(8,128)(2,1)} %gather_fusion, bf16[26,2,128,128]{3,2,1,0:T(8,128)(2,1)S(1)} %copy-done), kind=kOutput, calls=%fused_computation.15 | convolution fusion | flops 218529792 | bytes 4259840 | tf_op jit(solution)/shard_map/tcij,tckj->tki/dot_general | solution.py:70
  11.6 1.0 gather_fusion.1
  12.6 0.2 fusion.3
  12.7 55.1 %all_to_all.10 = bf16[16,528,128]{2,1,0:T(8,128)(2,1)S(1)} all-to-all(bf16[16,528,128]{2,1,0:T(8,128)(2,1)S(1)} %fusion.3), channel_id=1, replica_groups=mesh['band'=2,'spk'=16] {'spk'}, dimensions={0} | all-to-all | bytes 4325376 | tf_op jit(solution)/shard_map/all_to_all | solution.py:82
  67.9 0.1 copy.49
  68.0 0.1 copy.37
  68.1 0.1 eq.107
  68.2 0.0 copy-start.3
  68.2 0.2 slice.35
  68.4 0.5 copy-done.3
  68.8 1.2 fusion.13
  70.1 0.1 copy.39
  70.2 0.1 reshape.213
  70.3 2.2 %gather_fusion.2 = bf16[64,128,128]{2,1,0:T(8,128)(2,1)} fusion(bf16[8,128,128]{2,1,0:T(8,128)(2,1)S(1)} %copy.40, s32[1024]{0:T(1024)S(1)} %pad_clamp_fusion.1), kind=kCustom, calls=%fused_computation.2 | custom fusion | bytes 4194560 | tf_op jit(solution)/shard_map/jit(_take)/gather | solution.py:92
  72.5 5.8 %all-to-all-start.1 = ((bf16[16,512,128]{2,1,0:T(8,128)(2,1)}), bf16[16,512,128]{2,1,0:T(8,128)(2,1)S(1)}, u32[]{:S(2)}, u32[]{:S(2)}) async-start(bf16[16,512,128]{2,1,0:T(8,128)(2,1)} %bitcast.23), calls=%async_computation.1 | async-start | bytes 4194304 | tf_op jit(solution)/shard_map/all_to_all | solution.py:93
  78.3 0.6 fusion.48
  79.6 46.1 %all-to-all-done.1 = bf16[16,512,128]{2,1,0:T(8,128)(2,1)S(1)} async-done(((bf16[16,512,128]{2,1,0:T(8,128)(2,1)}), bf16[16,512,128]{2,1,0:T(8,128)(2,1)S(1)}, u32[]{:S(2)}, u32[]{:S(2)}) %all-to-all-start.1) | async-done | bytes 2097184 | tf_op jit(solution)/shard_map/all_to_all | solution.py:93
  125.7 0.7 gather_fusion.3
  126.4 0.4 fusion.9
  126.8 0.0 copy-start.1
  126.8 0.2 pad_maximum_fusion
  127.0 1.3 copy-done.1
  128.3 1.1 fusion.21
  129.4 0.8 copy.43
  (23 shorter events, 0.3 us)
Async XLA Ops:
  0.0 7.2 %copy-start.2 = (f32[2,128,128]{2,1,0:T(8,128)S(1)}, f32[2,128,128]{2,1,0:T(8,128)}, u32[]{:S(2)}) copy-start(f32[2,128,128]{2,1,0:T(8,128)} %param.4) | copy-start | bytes 393220
  7.3 2.3 %copy-start = (bf16[26,2,128,128]{3,2,1,0:T(8,128)(2,1)S(1)}, bf16[26,2,128,128]{3,2,1,0:T(8,128)(2,1)}, u32[]{:S(2)}) copy-start(bf16[26,2,128,128]{3,2,1,0:T(8,128)(2,1)} %param.5) | copy-start | bytes 5111812
  68.2 0.7 copy-start.3
  72.5 53.2 %all-to-all-start.1 = ((bf16[16,512,128]{2,1,0:T(8,128)(2,1)}), bf16[16,512,128]{2,1,0:T(8,128)(2,1)S(1)}, u32[]{:S(2)}, u32[]{:S(2)}) async-start(bf16[16,512,128]{2,1,0:T(8,128)(2,1)} %bitcast.23), calls=%async_computation.1 | async-start | bytes 4194304 | tf_op jit(solution)/shard_map/all_to_all | solution.py:93
  126.8 1.5 %copy-start.1 = (bf16[26,2,128,128]{3,2,1,0:T(8,128)(2,1)S(1)}, bf16[26,2,128,128]{3,2,1,0:T(8,128)(2,1)}, u32[]{:S(2)}) copy-start(bf16[26,2,128,128]{3,2,1,0:T(8,128)(2,1)} %param.5) | copy-start | bytes 5111812

commit v8 on v7

--- a/solution.py
+++ b/solution.py
@@ -70,8 +70,9 @@
     partial_field = jnp.einsum("tcij,tckj->tki", plant, pair_rows,
                                preferred_element_type=jnp.float32).astype(jnp.bfloat16)
     outgoing = jnp.take(partial_field, slot_pair, axis=0, mode="clip")
-    squares = jnp.square(plant.astype(jnp.float32)).reshape(-1, block_size)
-    local_power = jnp.sum(jnp.sum(squares, axis=0))
+    plant_rows = plant.reshape(-1, block_size)
+    local_power = jnp.trace(jnp.einsum("mj,mk->jk", plant_rows, plant_rows,
+                                       preferred_element_type=jnp.float32))
     power_hi = local_power.astype(jnp.bfloat16).astype(jnp.float32)
     power_mid = (local_power - power_hi).astype(jnp.bfloat16).astype(jnp.float32)
     power_lo = local_power - power_hi - power_mid
@@ -84,12 +85,13 @@
     source_bin = jnp.arange(devices) // groups_per_bin
     power_of = jnp.sum(header_in[:, capacity:].astype(jnp.float32), axis=1)
     bin_power = jnp.sum(jnp.where(source_bin == my_bin, power_of, 0.0))
-    recv_onehot = (labels_in[None, :] == jnp.arange(mic_units)[:, None]).astype(jnp.bfloat16)
-    pressure = jnp.einsum("ms,ski->mki", recv_onehot, arrived, preferred_element_type=jnp.float32)
+    valid = labels_in < mic_units
+    same_unit = ((labels_in[:, None] == labels_in[None, :]) & valid[None, :]).astype(jnp.bfloat16)
+    pressure = jnp.einsum("rs,ski->rki", same_unit, arrived, preferred_element_type=jnp.float32)
     weights_flat = mic_weight.reshape(mic_units, block_size)
-    weighted = (weights_flat[:, None, :] * pressure).astype(jnp.bfloat16)
+    slot_weights = jnp.take(weights_flat, jnp.minimum(labels_in, mic_units - 1), axis=0)
 
-    reply = jnp.take(weighted, jnp.minimum(labels_in, mic_units - 1), axis=0, mode="clip")
+    reply = (slot_weights[:, None, :] * pressure).astype(jnp.bfloat16)
     returned = lax.all_to_all(
         reply.reshape(devices, capacity * field_width, block_size), "spk", 0, 0, tiled=True
     ).reshape(slots, field_width, block_size)

time: 131 us -> 137 us (1.046)
  local copies, waits for them, and re-layouts: 10.1 us -> 14.9 us
  matrix products: 5.02 us -> 6.85 us
    reduce_sum x1 -> x0, other arithmetic: 2.95 us -> none  [per_device(): local_power = jnp.sum(jnp.sum(squares, axis=0))]
    convert_element_type x1, local copies, waits for them, and re-layouts: 0.04 us -> 2.65 us  [per_device(): reply = (slot_weights[:, None, :] * pressure).astype(jnp.bfloat16)]
    dot_general x1 -> x2, matrix products: 1.22 us -> 3.04 us  [the longest x1 1.79 us: per_device(): jnp.einsum('rs,ski->rki', same_unit, arrived, preferred_element_type=jnp....]
    gather x1, local copies, waits for them, and re-layouts: 0.71 us -> 2.3 us  [per_device(): tile_weighted = jnp.take(returned, position, axis=0, mode='clip')]
    concatenate x1, other arithmetic: 0.15 us -> 1.74 us  [with_header(): return jnp.concatenate([body, head], axis=1)]
    gather x1, local copies, waits for them, and re-layouts: 2.17 us -> 0.6 us  [per_device(): jnp.take(weights_flat, jnp.minimum(labels_in, mic_units - 1), axis=0)]
    slice x1 -> x2, local copies, waits for them, and re-layouts: 0.21 us -> 1.59 us  [split_header(): body = buffer[:, :capacity * rows].reshape(-1, rows, buffer.shape[2])]
where the time goes in v8:
time: 137 us; the launch traced here: 136 us
  blocking collectives  55.1 us (40%)
  waiting for transfers between devices  46.2 us (34%)
  local copies, waits for them, and re-layouts  14.9 us (11%)
  matrix products  6.85 us (5%)
  starting transfers between devices  6.42 us (5%)
  other arithmetic  4.66 us (3%)
  between operations  2.17 us (2%)
    all_to_all x1, blocking collectives, per_device(): lax.all_to_all(sent, 'spk', 0, 0, tiled=True)  55.1 us
    all_to_all x1, waiting for transfers between devices, per_device(): lax.all_to_all(reply.reshape(devices, capacity * field_width, block_size)...  46.2 us
    all_to_all x1, starting transfers between devices, per_device(): lax.all_to_all(reply.reshape(devices, capacity * field_width, block_size)...  6.42 us
  transfers between devices with their start and end apart: 1, of which 1 were waited for; matrix products, arithmetic and copies ran while one was open for 0% of the time, Pallas kernels for 0%

profile of v8, /device:TPU:13, one launch (start us, length us, event | category | flops | bytes accessed | tf_op | source)
XLA Modules:
  0.0 136.4 jit_solution(4317163642355778300)
XLA Ops:
  0.0 0.0 copy-start
  0.0 0.0 copy-start.3
  0.0 0.8 fusion.55
  0.9 0.1 fusion.42
  1.0 0.8 gather_fusion.4
  1.8 0.7 fusion.51
  2.5 0.1 fusion.37
  2.6 0.1 select_reduce_fusion.1
  2.7 0.1 concatenate.16
  2.8 0.0 copy-done
  2.8 1.3 fusion.21
  5.4 0.1 maximum_convert_fusion
  5.5 0.1 pad.10.clone
  5.6 0.0 copy-done.3
  5.6 0.1 copy.37
  5.7 0.2 fusion.19
  5.9 2.0 %gather_fusion = bf16[26,2,128,128]{3,2,1,0:T(8,128)(2,1)} fusion(bf16[2,2,128,128]{3,2,0,1:T(8,128)(2,1)S(1)} %pad_maximum_fusion.1, s32[1024]{0:T(1024)S(1)} %pad_clamp_fusion.3), kind=kCustom, calls=%fused_computation | custom fusion | bytes 3407976 | tf_op jit(solution)/shard_map/gather | solution.py:69
  7.9 2.1 %bitcast_convert_fusion = bf16[26,128,128]{2,1,0:T(8,128)(2,1)S(1)} fusion(bf16[26,2,128,128]{3,2,1,0:T(8,128)(2,1)} %gather_fusion, bf16[26,2,128,128]{3,2,1,0:T(8,128)(2,1)S(1)} %copy-done), kind=kOutput, calls=%fused_computation.14 | convolution fusion | flops 218529792 | bytes 4259840 | tf_op jit(solution)/shard_map/tcij,tckj->tki/dot_general | solution.py:70
  10.0 2.2 %gather_fusion.1 = bf16[64,128,128]{2,1,0:T(8,128)(2,1)} fusion(bf16[26,128,128]{2,1,0:T(8,128)(2,1)S(1)} %bitcast_convert_fusion, s32[1024]{0:T(1024)S(1)} %pad_clamp_fusion.2), kind=kCustom, calls=%fused_computation.1 | custom fusion | bytes 4194560 | tf_op jit(solution)/shard_map/jit(_take)/gather | solution.py:72
  12.2 1.7 %fusion.3 = bf16[16,528,128]{2,1,0:T(8,128)(2,1)S(1)} fusion(bf16[16,1,7]{2,1,0:T(2,128)(2,1)S(1)} %copy.56, bf16[16,512,128]{2,1,0:T(8,128)(2,1)} %bitcast.97), kind=kLoop, calls=%fused_computation.10 | loop fusion | flops 6488064 | bytes 4260064 | tf_op jit(solution)/shard_map/concatenate | solution.py:33
  13.9 0.0 copy-start.1
  13.9 55.1 %all_to_all.10 = bf16[16,528,128]{2,1,0:T(8,128)(2,1)S(1)} all-to-all(bf16[16,528,128]{2,1,0:T(8,128)(2,1)S(1)} %fusion.3), channel_id=1, replica_groups=mesh['band'=2,'spk'=16] {'spk'}, dimensions={0} | all-to-all | bytes 4325376 | tf_op jit(solution)/shard_map/all_to_all | solution.py:83
  69.0 0.0 copy-start.2
  69.1 1.3 copy-done.2
  70.4 0.1 copy.55
  70.5 0.1 copy.42
  70.6 0.1 min.26
  70.7 0.1 copy.41
  70.8 0.1 reshape.229
  70.9 0.0 copy-done.1
  70.9 0.6 gather_fusion.2
  71.5 0.1 broadcast_select_fusion
  71.6 0.0 slice-start
  71.6 1.6 %slice-done = bf16[16,512,128]{2,1,0:T(8,128)(2,1)S(1)} async-done(((bf16[16,528,128]{2,1,0:T(8,128)(2,1)}), bf16[16,512,128]{2,1,0:T(8,128)(2,1)S(1)}, s32[]{:S(2)}) %slice-start) | async-done | bytes 2097176 | tf_op jit(solution)/shard_map/slice | solution.py:37
  73.2 1.8 %multiply_convert_fusion = bf16[64,128,128]{2,0,1:T(8,128)(2,1)S(1)} fusion(bf16[64,128,128]{2,1,0:T(8,128)(2,1)S(1)} %bitcast.95, f32[64,128]{1,0:T(8,128)S(1)} %broadcast_select_fusion, s32[64]{0:T(128)S(1)} %reshape.229, pred[64]{0:T(512)(128)(4,1)S(1)} %get-tuple-element.17), kind=kOutput, calls=%fused_computation.7 | convolution fusion | flops 136323072 | bytes 4227392 | tf_op jit(solution)/shard_map/rs,ski->rki/dot_general | solution.py:90
  75.0 2.7 %copy.44 = bf16[64,128,128]{2,1,0:T(8,128)(2,1)} copy(bf16[64,128,128]{2,0,1:T(8,128)(2,1)S(1)} %multiply_convert_fusion) | data formatting | bytes 4194304 | tf_op jit(solution)/shard_map/convert_element_type | solution.py:94
  77.6 6.4 %all-to-all-start.1 = ((bf16[16,512,128]{2,1,0:T(8,128)(2,1)}), bf16[16,512,128]{2,1,0:T(8,128)(2,1)}, u32[]{:S(2)}, u32[]{:S(2)}) async-start(bf16[16,512,128]{2,1,0:T(8,128)(2,1)} %bitcast.96), calls=%async_computation.1 | async-start | bytes 4194304 | tf_op jit(solution)/shard_map/all_to_all | solution.py:95
  84.1 0.6 fusion.46
  85.4 46.2 %all-to-all-done.1 = bf16[16,512,128]{2,1,0:T(8,128)(2,1)} async-done(((bf16[16,512,128]{2,1,0:T(8,128)(2,1)}), bf16[16,512,128]{2,1,0:T(8,128)(2,1)}, u32[]{:S(2)}, u32[]{:S(2)}) %all-to-all-start.1) | async-done | bytes 2097184 | tf_op jit(solution)/shard_map/all_to_all | solution.py:95
  131.6 2.3 %gather_fusion.3 = bf16[26,128,128]{2,1,0:T(8,128)(2,1)S(1)} fusion(bf16[64,128,128]{2,1,0:T(8,128)(2,1)} %bitcast.27, s32[1024]{0:T(1024)S(1)} %pad_clamp_fusion), kind=kCustom, calls=%fused_computation.3 | custom fusion | bytes 1704040 | tf_op jit(solution)/shard_map/jit(_take)/gather | solution.py:98
  133.9 0.4 fusion.8
  134.3 0.2 pad_maximum_fusion
  134.5 1.1 fusion.14
  135.6 0.8 copy.47
  (24 shorter events, 0.2 us)
Async XLA Ops:
  0.0 2.8 %copy-start = (bf16[26,2,128,128]{3,2,1,0:T(8,128)(2,1)S(1)}, bf16[26,2,128,128]{3,2,1,0:T(8,128)(2,1)}, u32[]{:S(2)}) copy-start(bf16[26,2,128,128]{3,2,1,0:T(8,128)(2,1)} %param.5) | copy-start | bytes 5111812
  0.0 5.6 %copy-start.3 = (f32[2,128,128]{2,1,0:T(8,128)S(1)}, f32[2,128,128]{2,1,0:T(8,128)}, u32[]{:S(2)}) copy-start(f32[2,128,128]{2,1,0:T(8,128)} %param.4) | copy-start | bytes 393220
  13.9 57.0 %copy-start.1 = (f32[1,8,128]{2,1,0:T(8,128)S(1)}, f32[1,8,128]{2,1,0:T(8,128)}, u32[]{:S(2)}) copy-start(f32[1,8,128]{2,1,0:T(8,128)} %param.7) | copy-start | bytes 12292
  69.0 1.4 copy-start.2
  71.6 1.6 %slice-start = ((bf16[16,528,128]{2,1,0:T(8,128)(2,1)}), bf16[16,512,128]{2,1,0:T(8,128)(2,1)S(1)}, s32[]{:S(2)}) async-start(bf16[16,528,128]{2,1,0:T(8,128)(2,1)} %copy-done.2), calls=%async_computation.2 | async-start | bytes 4194304 | tf_op jit(solution)/shard_map/slice | solution.py:37
  77.6 54.0 %all-to-all-start.1 = ((bf16[16,512,128]{2,1,0:T(8,128)(2,1)}), bf16[16,512,128]{2,1,0:T(8,128)(2,1)}, u32[]{:S(2)}, u32[]{:S(2)}) async-start(bf16[16,512,128]{2,1,0:T(8,128)(2,1)} %bitcast.96), calls=%async_computation.1 | async-start | bytes 4194304 | tf_op jit(solution)/shard_map/all_to_all | solution.py:95

commit v9 on v7

--- a/solution.py
+++ b/solution.py
@@ -70,8 +70,9 @@
     partial_field = jnp.einsum("tcij,tckj->tki", plant, pair_rows,
                                preferred_element_type=jnp.float32).astype(jnp.bfloat16)
     outgoing = jnp.take(partial_field, slot_pair, axis=0, mode="clip")
-    squares = jnp.square(plant.astype(jnp.float32)).reshape(-1, block_size)
-    local_power = jnp.sum(jnp.sum(squares, axis=0))
+    plant_rows = plant.reshape(-1, block_size)
+    local_power = jnp.trace(jnp.einsum("mj,mk->jk", plant_rows, plant_rows,
+                                       preferred_element_type=jnp.float32))
     power_hi = local_power.astype(jnp.bfloat16).astype(jnp.float32)
     power_mid = (local_power - power_hi).astype(jnp.bfloat16).astype(jnp.float32)
     power_lo = local_power - power_hi - power_mid

time: 131 us -> 135 us (1.031)
  local copies, waits for them, and re-layouts: 10.1 us -> 13.8 us
    reduce_sum x1 -> x0, other arithmetic: 2.95 us -> none  [per_device(): local_power = jnp.sum(jnp.sum(squares, axis=0))]
    gather x1, local copies, waits for them, and re-layouts: 0.71 us -> 2.3 us  [per_device(): tile_weighted = jnp.take(returned, position, axis=0, mode='clip')]
    concatenate x1, other arithmetic: 0.15 us -> 1.74 us  [with_header(): return jnp.concatenate([body, head], axis=1)]
    slice x1 -> x2, local copies, waits for them, and re-layouts: 0.21 us -> 1.58 us  [split_header(): body = buffer[:, :capacity * rows].reshape(-1, rows, buffer.shape[2])]
where the time goes in v9:
time: 135 us
  blocking collectives  55.1 us (41%)
  waiting for transfers between devices  46.2 us (34%)
  local copies, waits for them, and re-layouts  13.8 us (10%)
  starting transfers between devices  6.42 us (5%)
  matrix products  6.28 us (5%)
  other arithmetic  4.57 us (3%)
  between operations  2.15 us (2%)
    all_to_all x1, blocking collectives, per_device(): lax.all_to_all(sent, 'spk', 0, 0, tiled=True)  55.1 us
    all_to_all x1, waiting for transfers between devices, per_device(): lax.all_to_all(reply.reshape(devices, capacity * field_width, block_size)...  46.2 us
    all_to_all x1, starting transfers between devices, per_device(): lax.all_to_all(reply.reshape(devices, capacity * field_width, block_size)...  6.42 us
  transfers between devices with their start and end apart: 1, of which 1 were waited for; matrix products, arithmetic and copies ran while one was open for 0% of the time, Pallas kernels for 0%

profile of v9, /device:TPU:13, one launch (start us, length us, event | category | flops | bytes accessed | tf_op | source)
XLA Modules:
  0.0 134.6 jit_solution(14577162332832159590)
XLA Ops:
  0.0 0.0 copy-start
  0.0 0.0 copy-start.2
  0.0 0.8 fusion.58
  0.9 0.1 fusion.44
  1.0 0.8 gather_fusion.4
  1.8 0.7 fusion.54
  2.5 0.1 fusion.40
  2.6 0.1 select_reduce_fusion.1
  2.7 0.1 concatenate.16
  2.8 0.0 copy-done
  2.8 1.3 fusion.28
  5.4 0.1 maximum_convert_fusion
  5.5 0.1 pad.10.clone
  5.6 0.0 copy-done.2
  5.6 0.1 copy.37
  5.7 0.2 fusion.26
  5.9 2.0 %gather_fusion = bf16[26,2,128,128]{3,2,1,0:T(8,128)(2,1)} fusion(bf16[2,2,128,128]{3,2,0,1:T(8,128)(2,1)S(1)} %pad_maximum_fusion.1, s32[1024]{0:T(1024)S(1)} %pad_clamp_fusion.3), kind=kCustom, calls=%fused_computation | custom fusion | bytes 3407976 | tf_op jit(solution)/shard_map/gather | solution.py:69
  7.9 2.1 %bitcast_convert_fusion = bf16[26,128,128]{2,1,0:T(8,128)(2,1)S(1)} fusion(bf16[26,2,128,128]{3,2,1,0:T(8,128)(2,1)} %gather_fusion, bf16[26,2,128,128]{3,2,1,0:T(8,128)(2,1)S(1)} %copy-done), kind=kOutput, calls=%fused_computation.14 | convolution fusion | flops 218529792 | bytes 4259840 | tf_op jit(solution)/shard_map/tcij,tckj->tki/dot_general | solution.py:70
  10.0 2.2 %gather_fusion.1 = bf16[64,128,128]{2,1,0:T(8,128)(2,1)} fusion(bf16[26,128,128]{2,1,0:T(8,128)(2,1)S(1)} %bitcast_convert_fusion, s32[1024]{0:T(1024)S(1)} %pad_clamp_fusion.2), kind=kCustom, calls=%fused_computation.1 | custom fusion | bytes 4194560 | tf_op jit(solution)/shard_map/jit(_take)/gather | solution.py:72
  12.2 1.7 %fusion.3 = bf16[16,528,128]{2,1,0:T(8,128)(2,1)S(1)} fusion(bf16[16,1,7]{2,1,0:T(2,128)(2,1)S(1)} %copy.56, bf16[16,512,128]{2,1,0:T(8,128)(2,1)} %bitcast.94), kind=kLoop, calls=%fused_computation.9 | loop fusion | flops 6488064 | bytes 4260064 | tf_op jit(solution)/shard_map/concatenate | solution.py:33
  13.9 55.1 %all_to_all.10 = bf16[16,528,128]{2,1,0:T(8,128)(2,1)S(1)} all-to-all(bf16[16,528,128]{2,1,0:T(8,128)(2,1)S(1)} %fusion.3), channel_id=1, replica_groups=mesh['band'=2,'spk'=16] {'spk'}, dimensions={0} | all-to-all | bytes 4325376 | tf_op jit(solution)/shard_map/all_to_all | solution.py:83
  69.0 0.0 copy-start.1
  69.0 1.3 %copy-done.1 = bf16[16,528,128]{2,1,0:T(8,128)(2,1)} copy-done((bf16[16,528,128]{2,1,0:T(8,128)(2,1)}, bf16[16,528,128]{2,1,0:T(8,128)(2,1)S(1)}, u32[]{:S(2)}) %copy-start.1) | copy-done | bytes 2162712
  70.4 0.1 copy.55
  70.5 0.1 copy.41
  70.6 0.1 eq.112
  70.7 0.0 slice-start
  70.7 0.0 copy-start.3
  70.7 1.6 %slice-done = bf16[16,512,128]{2,1,0:T(8,128)(2,1)S(1)} async-done(((bf16[16,528,128]{2,1,0:T(8,128)(2,1)}), bf16[16,512,128]{2,1,0:T(8,128)(2,1)S(1)}, s32[]{:S(2)}) %slice-start) | async-done | bytes 2097176 | tf_op jit(solution)/shard_map/slice | solution.py:37
  72.3 0.0 copy-done.3
  72.3 1.2 fusion.13
  73.5 0.1 copy.43
  73.6 0.1 reshape.213
  73.7 2.1 %gather_fusion.2 = bf16[64,128,128]{2,1,0:T(8,128)(2,1)} fusion(bf16[8,128,128]{2,1,0:T(8,128)(2,1)S(1)} %copy.44, s32[1024]{0:T(1024)S(1)} %pad_clamp_fusion.1), kind=kCustom, calls=%fused_computation.2 | custom fusion | bytes 4194560 | tf_op jit(solution)/shard_map/jit(_take)/gather | solution.py:93
  75.8 6.4 %all-to-all-start.1 = ((bf16[16,512,128]{2,1,0:T(8,128)(2,1)}), bf16[16,512,128]{2,1,0:T(8,128)(2,1)}, u32[]{:S(2)}, u32[]{:S(2)}) async-start(bf16[16,512,128]{2,1,0:T(8,128)(2,1)} %bitcast.93), calls=%async_computation.1 | async-start | bytes 4194304 | tf_op jit(solution)/shard_map/all_to_all | solution.py:94
  82.3 0.6 fusion.50
  83.6 46.2 %all-to-all-done.1 = bf16[16,512,128]{2,1,0:T(8,128)(2,1)} async-done(((bf16[16,512,128]{2,1,0:T(8,128)(2,1)}), bf16[16,512,128]{2,1,0:T(8,128)(2,1)}, u32[]{:S(2)}, u32[]{:S(2)}) %all-to-all-start.1) | async-done | bytes 2097184 | tf_op jit(solution)/shard_map/all_to_all | solution.py:94
  129.8 2.3 %gather_fusion.3 = bf16[26,128,128]{2,1,0:T(8,128)(2,1)S(1)} fusion(bf16[64,128,128]{2,1,0:T(8,128)(2,1)} %bitcast.26, s32[1024]{0:T(1024)S(1)} %pad_clamp_fusion), kind=kCustom, calls=%fused_computation.3 | custom fusion | bytes 1704040 | tf_op jit(solution)/shard_map/jit(_take)/gather | solution.py:97
  132.1 0.4 fusion.9
  132.6 0.2 pad_maximum_fusion
  132.7 1.1 fusion.21
  133.8 0.8 copy.47
  (23 shorter events, 0.3 us)
Async XLA Ops:
  0.0 2.8 %copy-start = (bf16[26,2,128,128]{3,2,1,0:T(8,128)(2,1)S(1)}, bf16[26,2,128,128]{3,2,1,0:T(8,128)(2,1)}, u32[]{:S(2)}) copy-start(bf16[26,2,128,128]{3,2,1,0:T(8,128)(2,1)} %param.5) | copy-start | bytes 5111812
  0.0 5.6 %copy-start.2 = (f32[2,128,128]{2,1,0:T(8,128)S(1)}, f32[2,128,128]{2,1,0:T(8,128)}, u32[]{:S(2)}) copy-start(f32[2,128,128]{2,1,0:T(8,128)} %param.4) | copy-start | bytes 393220
  69.0 1.4 %copy-start.1 = (bf16[16,528,128]{2,1,0:T(8,128)(2,1)}, bf16[16,528,128]{2,1,0:T(8,128)(2,1)S(1)}, u32[]{:S(2)}) copy-start(bf16[16,528,128]{2,1,0:T(8,128)(2,1)S(1)} %all_to_all.10) | copy-start | bytes 6488068
  70.7 1.6 %slice-start = ((bf16[16,528,128]{2,1,0:T(8,128)(2,1)}), bf16[16,512,128]{2,1,0:T(8,128)(2,1)S(1)}, s32[]{:S(2)}) async-start(bf16[16,528,128]{2,1,0:T(8,128)(2,1)} %copy-done.1), calls=%async_computation.2 | async-start | bytes 4194304 | tf_op jit(solution)/shard_map/slice | solution.py:37
  70.7 1.6 %copy-start.3 = (f32[1,8,128]{2,1,0:T(8,128)S(1)}, f32[1,8,128]{2,1,0:T(8,128)}, u32[]{:S(2)}) copy-start(f32[1,8,128]{2,1,0:T(8,128)} %param.7) | copy-start | bytes 12292
  75.8 54.0 %all-to-all-start.1 = ((bf16[16,512,128]{2,1,0:T(8,128)(2,1)}), bf16[16,512,128]{2,1,0:T(8,128)(2,1)}, u32[]{:S(2)}, u32[]{:S(2)}) async-start(bf16[16,512,128]{2,1,0:T(8,128)(2,1)} %bitcast.93), calls=%async_computation.1 | async-start | bytes 4194304 | tf_op jit(solution)/shard_map/all_to_all | solution.py:94

commit v10 on v9

--- a/solution.py
+++ b/solution.py
@@ -70,8 +70,7 @@
     partial_field = jnp.einsum("tcij,tckj->tki", plant, pair_rows,
                                preferred_element_type=jnp.float32).astype(jnp.bfloat16)
     outgoing = jnp.take(partial_field, slot_pair, axis=0, mode="clip")
-    plant_rows = plant.reshape(-1, block_size)
-    local_power = jnp.trace(jnp.einsum("mj,mk->jk", plant_rows, plant_rows,
+    local_power = jnp.trace(jnp.einsum("tcij,tcik->jk", plant, plant,
                                        preferred_element_type=jnp.float32))
     power_hi = local_power.astype(jnp.bfloat16).astype(jnp.float32)
     power_mid = (local_power - power_hi).astype(jnp.bfloat16).astype(jnp.float32)

time: 135 us -> 130 us (0.963)
  local copies, waits for them, and re-layouts: 13.8 us -> 8.97 us
  matrix products: 6.28 us -> 8.39 us
  other arithmetic: 4.57 us -> 2.91 us
    dot_general x1, matrix products: 1.25 us -> 3.36 us  [per_device(): jnp.einsum('tcij,tcik->jk', plant, plant, preferred_element_type=jnp.floa...]
    gather x1, local copies, waits for them, and re-layouts: 2.3 us -> 0.71 us  [per_device(): tile_weighted = jnp.take(returned, position, axis=0, mode='clip')]
    concatenate x1, other arithmetic: 1.74 us -> 0.15 us  [with_header(): return jnp.concatenate([body, head], axis=1)]
    slice x2 -> x1, local copies, waits for them, and re-layouts: 1.58 us -> 0.21 us  [split_header(): body = buffer[:, :capacity * rows].reshape(-1, rows, buffer.shape[2])]
where the time goes in v10:
time: 130 us; the launch traced here: 129 us
  blocking collectives  55.1 us (42%)
  waiting for transfers between devices  46.1 us (35%)
  local copies, waits for them, and re-layouts  8.97 us (7%)
  matrix products  8.39 us (6%)
  starting transfers between devices  5.78 us (4%)
  other arithmetic  2.91 us (2%)
  between operations  2.17 us (2%)
    all_to_all x1, blocking collectives, per_device(): lax.all_to_all(sent, 'spk', 0, 0, tiled=True)  55.1 us
    all_to_all x1, waiting for transfers between devices, per_device(): lax.all_to_all(reply.reshape(devices, capacity * field_width, block_size)...  46.1 us
    all_to_all x1, starting transfers between devices, per_device(): lax.all_to_all(reply.reshape(devices, capacity * field_width, block_size)...  5.78 us
    dot_general x1, matrix products, per_device(): jnp.einsum('tcij,tcik->jk', plant, plant, preferred_element_type=jnp.floa...  3.36 us
  transfers between devices with their start and end apart: 1, of which 1 were waited for; matrix products, arithmetic and copies ran while one was open for 0% of the time, Pallas kernels for 0%

profile of v10, /device:TPU:13, one launch (start us, length us, event | category | flops | bytes accessed | tf_op | source)
XLA Modules:
  0.0 129.5 jit_solution(16423141099259190976)
XLA Ops:
  0.0 0.0 copy-start.1
  0.0 0.8 fusion.67
  0.8 0.1 fusion.53
  0.9 0.8 gather_fusion.4
  1.7 0.7 fusion.63
  2.4 0.1 fusion.49
  2.5 0.1 select_reduce_fusion.1
  2.6 0.1 concatenate.16
  2.7 3.4 %fusion.35 = f32[]{:T(128)} fusion(bf16[26,2,128,128]{3,2,1,0:T(8,128)(2,1)} %param.5), kind=kOutput, calls=%fused_computation.29 | convolution fusion | flops 218152960 | bytes 1703940 | tf_op jit(solution)/shard_map/tcij,tcik->jk/dot_general | solution.py:73
  7.4 0.1 maximum_convert_fusion
  7.5 0.1 pad.10.clone
  7.6 0.0 copy-done.1
  7.6 0.1 copy.40
  7.7 0.2 fusion.28
  8.0 0.9 gather_fusion
  8.8 2.1 %bitcast_convert_fusion = bf16[26,128,128]{2,1,0:T(8,128)(2,1)S(1)} fusion(bf16[26,2,128,128]{3,2,1,0:T(8,128)(2,1)S(1)} %gather_fusion, bf16[26,2,128,128]{3,2,1,0:T(8,128)(2,1)} %param.5), kind=kOutput, calls=%fused_computation.16 | convolution fusion | flops 218529792 | bytes 4259840 | tf_op jit(solution)/shard_map/tcij,tckj->tki/dot_general | solution.py:70
  10.9 1.0 gather_fusion.1
  11.9 0.2 fusion.3
  12.0 55.1 %all_to_all.10 = bf16[16,528,128]{2,1,0:T(8,128)(2,1)S(1)} all-to-all(bf16[16,528,128]{2,1,0:T(8,128)(2,1)S(1)} %fusion.3), channel_id=1, replica_groups=mesh['band'=2,'spk'=16] {'spk'}, dimensions={0} | all-to-all | bytes 4325376 | tf_op jit(solution)/shard_map/all_to_all | solution.py:82
  67.2 0.1 copy.60
  67.3 0.1 copy.45
  67.4 0.1 eq.112
  67.5 0.0 copy-start.2
  67.5 0.2 slice.35
  67.7 0.5 copy-done.2
  68.1 1.2 fusion.15
  69.4 0.1 copy.47
  69.5 0.1 reshape.212
  69.6 2.2 %gather_fusion.2 = bf16[64,128,128]{2,1,0:T(8,128)(2,1)} fusion(bf16[8,128,128]{2,1,0:T(8,128)(2,1)S(1)} %copy.48, s32[1024]{0:T(1024)S(1)} %pad_clamp_fusion.1), kind=kCustom, calls=%fused_computation.2 | custom fusion | bytes 4194560 | tf_op jit(solution)/shard_map/jit(_take)/gather | solution.py:92
  71.8 5.8 %all-to-all-start.1 = ((bf16[16,512,128]{2,1,0:T(8,128)(2,1)}), bf16[16,512,128]{2,1,0:T(8,128)(2,1)S(1)}, u32[]{:S(2)}, u32[]{:S(2)}) async-start(bf16[16,512,128]{2,1,0:T(8,128)(2,1)} %bitcast.25), calls=%async_computation.1 | async-start | bytes 4194304 | tf_op jit(solution)/shard_map/all_to_all | solution.py:93
  77.6 0.6 fusion.59
  78.8 46.1 %all-to-all-done.1 = bf16[16,512,128]{2,1,0:T(8,128)(2,1)S(1)} async-done(((bf16[16,512,128]{2,1,0:T(8,128)(2,1)}), bf16[16,512,128]{2,1,0:T(8,128)(2,1)S(1)}, u32[]{:S(2)}, u32[]{:S(2)}) %all-to-all-start.1) | async-done | bytes 2097184 | tf_op jit(solution)/shard_map/all_to_all | solution.py:93
  125.0 0.7 gather_fusion.3
  125.7 0.4 fusion.11
  126.1 0.0 copy-start
  126.1 0.2 pad_maximum_fusion
  126.3 1.3 copy-done
  127.6 1.1 fusion.23
  128.7 0.8 copy.51
  (23 shorter events, 0.3 us)
Async XLA Ops:
  0.0 7.6 %copy-start.1 = (f32[2,128,128]{2,1,0:T(8,128)S(1)}, f32[2,128,128]{2,1,0:T(8,128)}, u32[]{:S(2)}) copy-start(f32[2,128,128]{2,1,0:T(8,128)} %param.4) | copy-start | bytes 393220
  67.5 0.7 copy-start.2
  71.8 53.2 %all-to-all-start.1 = ((bf16[16,512,128]{2,1,0:T(8,128)(2,1)}), bf16[16,512,128]{2,1,0:T(8,128)(2,1)S(1)}, u32[]{:S(2)}, u32[]{:S(2)}) async-start(bf16[16,512,128]{2,1,0:T(8,128)(2,1)} %bitcast.25), calls=%async_computation.1 | async-start | bytes 4194304 | tf_op jit(solution)/shard_map/all_to_all | solution.py:93
  126.1 1.5 %copy-start = (bf16[26,2,128,128]{3,2,1,0:T(8,128)(2,1)S(1)}, bf16[26,2,128,128]{3,2,1,0:T(8,128)(2,1)}, u32[]{:S(2)}) copy-start(bf16[26,2,128,128]{3,2,1,0:T(8,128)(2,1)} %param.5) | copy-start | bytes 5111812

commit v11 on v10

--- a/solution.py
+++ b/solution.py
@@ -70,8 +70,8 @@
     partial_field = jnp.einsum("tcij,tckj->tki", plant, pair_rows,
                                preferred_element_type=jnp.float32).astype(jnp.bfloat16)
     outgoing = jnp.take(partial_field, slot_pair, axis=0, mode="clip")
-    local_power = jnp.trace(jnp.einsum("tcij,tcik->jk", plant, plant,
-                                       preferred_element_type=jnp.float32))
+    squares = jnp.square(plant.astype(jnp.float32)).reshape(-1, 8, block_size)
+    local_power = jnp.sum(lax.optimization_barrier(jnp.sum(squares, axis=0)))
     power_hi = local_power.astype(jnp.bfloat16).astype(jnp.float32)
     power_mid = (local_power - power_hi).astype(jnp.bfloat16).astype(jnp.float32)
     power_lo = local_power - power_hi - power_mid

time: 130 us -> 134 us (1.031)
  other arithmetic: 2.91 us -> 8.64 us
  matrix products: 8.39 us -> 5.68 us
    dot_general x1 -> x0, matrix products: 3.36 us -> none  [per_device(): jnp.einsum('tcij,tcik->jk', plant, plant, preferred_element_type=jnp.floa...]
    square x0 -> x1, other arithmetic: none -> 1.88 us  [per_device(): squares = jnp.square(plant.astype(jnp.float32)).reshape(-1, 8, block_size)]
    reduce_sum x0 -> x2, other arithmetic: none -> 1.45 us  [per_device(): local_power = jnp.sum(lax.optimization_barrier(jnp.sum(squares, axis=0)))]
where the time goes in v11:
time: 134 us
  blocking collectives  55.1 us (41%)
  waiting for transfers between devices  46.1 us (34%)
  local copies, waits for them, and re-layouts  10.1 us (8%)
  other arithmetic  8.64 us (6%)
  starting transfers between devices  5.91 us (4%)
  matrix products  5.68 us (4%)
  between operations  2 us (1%)
    all_to_all x1, blocking collectives, per_device(): lax.all_to_all(sent, 'spk', 0, 0, tiled=True)  55.1 us
    all_to_all x1, waiting for transfers between devices, per_device(): lax.all_to_all(reply.reshape(devices, capacity * field_width, block_size)...  46.1 us
    all_to_all x1, starting transfers between devices, per_device(): lax.all_to_all(reply.reshape(devices, capacity * field_width, block_size)...  5.91 us
  transfers between devices with their start and end apart: 1, of which 1 were waited for; matrix products, arithmetic and copies ran while one was open for 0% of the time, Pallas kernels for 0%

profile of v11, /device:TPU:13, one launch (start us, length us, event | category | flops | bytes accessed | tf_op | source)
XLA Modules:
  0.0 133.6 jit_solution(3933075566568039302)
XLA Ops:
  0.0 0.6 and_select_fusion.5
  0.6 1.3 fusion.56
  1.9 0.1 fusion.42
  2.0 0.8 gather_fusion.4
  2.8 0.7 fusion.52
  3.5 0.1 fusion.38
  3.6 0.6 select_reduce_fusion.1
  4.2 0.1 concatenate.16
  4.3 1.9 %convert_multiply_fusion = f32[26,2,128,128]{3,2,1,0:T(8,128)S(1)} fusion(bf16[26,2,128,128]{3,2,1,0:T(8,128)(2,1)} %param.5), kind=kLoop, calls=%fused_computation.9 | loop fusion | flops 1703936 | bytes 5111808 | tf_op jit(solution)/shard_map/square | solution.py:73
  6.2 0.0 copy-start.2
  6.2 0.9 reduce_sum.56
  7.1 0.6 reduce_sum.57
  8.8 0.1 maximum_convert_fusion
  8.9 0.1 pad.10.clone
  9.0 0.0 copy-done.2
  9.0 0.1 copy.34
  9.1 0.0 copy-start
  9.1 0.8 pad_clamp_fusion.3
  9.9 0.9 fusion.26
  10.8 2.0 %gather_fusion = bf16[26,2,128,128]{3,2,1,0:T(8,128)(2,1)} fusion(bf16[2,2,128,128]{3,2,0,1:T(8,128)(2,1)S(1)} %pad_maximum_fusion.1, s32[1024]{0:T(1024)S(1)} %pad_clamp_fusion.3), kind=kCustom, calls=%fused_computation | custom fusion | bytes 3407976 | tf_op jit(solution)/shard_map/gather | solution.py:69
  12.8 0.0 copy-done
  12.8 0.0 copy-start.4
  12.8 2.1 %bitcast_convert_fusion = bf16[26,128,128]{2,1,0:T(8,128)(2,1)S(1)} fusion(bf16[26,2,128,128]{3,2,1,0:T(8,128)(2,1)} %gather_fusion, bf16[26,2,128,128]{3,2,1,0:T(8,128)(2,1)S(1)} %copy-done), kind=kOutput, calls=%fused_computation.15 | convolution fusion | flops 218529792 | bytes 4259840 | tf_op jit(solution)/shard_map/tcij,tckj->tki/dot_general | solution.py:70
  14.9 0.0 copy-done.4
  14.9 1.0 gather_fusion.1
  15.9 0.2 fusion.3
  16.0 55.1 %all_to_all.10 = bf16[16,528,128]{2,1,0:T(8,128)(2,1)S(1)} all-to-all(bf16[16,528,128]{2,1,0:T(8,128)(2,1)S(1)} %fusion.3), channel_id=1, replica_groups=mesh['band'=2,'spk'=16] {'spk'}, dimensions={0} | all-to-all | bytes 4325376 | tf_op jit(solution)/shard_map/all_to_all | solution.py:82
  71.1 0.1 copy.49
  71.3 0.1 copy.37
  71.3 0.1 eq.107
  71.4 0.0 copy-start.3
  71.4 0.2 slice.35
  71.7 0.5 copy-done.3
  72.1 1.2 fusion.13
  73.4 0.1 copy.39
  73.5 0.1 reshape.216
  73.6 2.2 %gather_fusion.2 = bf16[64,128,128]{2,1,0:T(8,128)(2,1)} fusion(bf16[8,128,128]{2,1,0:T(8,128)(2,1)S(1)} %copy.40, s32[1024]{0:T(1024)S(1)} %pad_clamp_fusion.1), kind=kCustom, calls=%fused_computation.2 | custom fusion | bytes 4194560 | tf_op jit(solution)/shard_map/jit(_take)/gather | solution.py:92
  75.7 0.0 copy-start.5
  75.7 5.9 %all-to-all-start.1 = ((bf16[16,512,128]{2,1,0:T(8,128)(2,1)}), bf16[16,512,128]{2,1,0:T(8,128)(2,1)S(1)}, u32[]{:S(2)}, u32[]{:S(2)}) async-start(bf16[16,512,128]{2,1,0:T(8,128)(2,1)} %bitcast.24), calls=%async_computation.1 | async-start | bytes 4194304 | tf_op jit(solution)/shard_map/all_to_all | solution.py:93
  81.7 0.0 copy-done.5
  81.7 0.6 fusion.48
  83.0 46.1 %all-to-all-done.1 = bf16[16,512,128]{2,1,0:T(8,128)(2,1)S(1)} async-done(((bf16[16,512,128]{2,1,0:T(8,128)(2,1)}), bf16[16,512,128]{2,1,0:T(8,128)(2,1)S(1)}, u32[]{:S(2)}, u32[]{:S(2)}) %all-to-all-start.1) | async-done | bytes 2097184 | tf_op jit(solution)/shard_map/all_to_all | solution.py:93
  129.1 0.7 gather_fusion.3
  129.8 0.4 fusion.9
  130.2 0.0 copy-start.1
  130.3 0.2 pad_maximum_fusion
  130.4 1.3 copy-done.1
  131.7 1.1 fusion.21
  132.8 0.8 copy.43
  (21 shorter events, 0.2 us)
Async XLA Ops:
  6.2 2.8 %copy-start.2 = (f32[2,128,128]{2,1,0:T(8,128)S(1)}, f32[2,128,128]{2,1,0:T(8,128)}, u32[]{:S(2)}) copy-start(f32[2,128,128]{2,1,0:T(8,128)} %param.4) | copy-start | bytes 393220
  9.1 3.7 %copy-start = (bf16[26,2,128,128]{3,2,1,0:T(8,128)(2,1)S(1)}, bf16[26,2,128,128]{3,2,1,0:T(8,128)(2,1)}, u32[]{:S(2)}) copy-start(bf16[26,2,128,128]{3,2,1,0:T(8,128)(2,1)} %param.5) | copy-start | bytes 5111812
  12.8 2.1 %copy-start.4 = (s32[64]{0:T(128)S(1)}, s32[64]{0:T(128)}, u32[]{:S(2)}) copy-start(s32[64]{0:T(128)} %get-tuple-element.5) | copy-start | bytes 772
  71.4 0.7 copy-start.3
  75.7 5.9 %copy-start.5 = (s32[26,1]{0,1:T(1,128)S(1)}, s32[26,1]{0,1:T(1,128)}, u32[]{:S(2)}) copy-start(s32[26,1]{0,1:T(1,128)} %get-tuple-element.16) | copy-start | bytes 316
  75.7 53.3 %all-to-all-start.1 = ((bf16[16,512,128]{2,1,0:T(8,128)(2,1)}), bf16[16,512,128]{2,1,0:T(8,128)(2,1)S(1)}, u32[]{:S(2)}, u32[]{:S(2)}) async-start(bf16[16,512,128]{2,1,0:T(8,128)(2,1)} %bitcast.24), calls=%async_computation.1 | async-start | bytes 4194304 | tf_op jit(solution)/shard_map/all_to_all | solution.py:93
  130.2 1.5 %copy-start.1 = (bf16[26,2,128,128]{3,2,1,0:T(8,128)(2,1)S(1)}, bf16[26,2,128,128]{3,2,1,0:T(8,128)(2,1)}, u32[]{:S(2)}) copy-start(bf16[26,2,128,128]{3,2,1,0:T(8,128)(2,1)} %param.5) | copy-start | bytes 5111812

commit v12 on v10

--- a/solution.py
+++ b/solution.py
@@ -21,9 +21,10 @@
 
 
 def slot_ranks(target_peer, devices):
-    onehot = (target_peer[..., :, None] == jnp.arange(devices)).astype(jnp.int32)
-    running = jnp.cumsum(onehot, axis=-2)
-    return jnp.take_along_axis(running, target_peer[..., None], axis=-1)[..., 0] - 1
+    count = target_peer.shape[-1]
+    earlier = jnp.arange(count)[None, :] < jnp.arange(count)[:, None]
+    same = target_peer[:, None] == target_peer[None, :]
+    return jnp.sum((earlier & same).astype(jnp.int32), axis=1)
 
 
 def with_header(blocks, values, devices, capacity):

time: 130 us -> 129 us (level)
  transfers between devices with their start and end apart: 1 -> 1, of which waited for: 1 -> 1; matrix products, arithmetic and copies ran while one was open for 0% -> 1% of each run, Pallas kernels for 0% -> 0%
where the time goes in v12:
time: 129 us
  blocking collectives  55.1 us (43%)
  waiting for transfers between devices  46.1 us (36%)
  matrix products  8.38 us (6%)
  local copies, waits for them, and re-layouts  8.17 us (6%)
  starting transfers between devices  5.78 us (4%)
  other arithmetic  2.95 us (2%)
  between operations  2.18 us (2%)
    all_to_all x1, blocking collectives, per_device(): lax.all_to_all(sent, 'spk', 0, 0, tiled=True)  55.1 us
    all_to_all x1, waiting for transfers between devices, per_device(): lax.all_to_all(reply.reshape(devices, capacity * field_width, block_size)...  46.1 us
    all_to_all x1, starting transfers between devices, per_device(): lax.all_to_all(reply.reshape(devices, capacity * field_width, block_size)...  5.78 us
    dot_general x1, matrix products, per_device(): jnp.einsum('tcij,tcik->jk', plant, plant, preferred_element_type=jnp.floa...  3.36 us
  transfers between devices with their start and end apart: 1, of which 1 were waited for; matrix products, arithmetic and copies ran while one was open for 1% of the time, Pallas kernels for 0%

profile of v12, /device:TPU:13, one launch (start us, length us, event | category | flops | bytes accessed | tf_op | source)
XLA Modules:
  0.0 128.7 jit_solution(13048939207325613440)
XLA Ops:
  0.0 0.0 copy-start.1
  0.0 0.8 fusion.62
  0.8 0.7 fusion.64
  1.5 0.2 convert_reduce_fusion
  1.7 0.1 fusion.49
  1.8 0.1 select_reduce_fusion.1
  1.9 0.1 concatenate.16
  2.0 3.4 %fusion.35 = f32[]{:T(128)} fusion(bf16[26,2,128,128]{3,2,1,0:T(8,128)(2,1)} %param.5), kind=kOutput, calls=%fused_computation.28 | convolution fusion | flops 218152960 | bytes 1703940 | tf_op jit(solution)/shard_map/tcij,tcik->jk/dot_general | solution.py:74
  6.6 0.1 maximum_convert_fusion
  6.7 0.1 pad.10.clone
  6.8 0.0 copy-done.1
  6.8 0.1 copy.40
  7.0 0.2 fusion.28
  7.2 0.9 gather_fusion
  8.1 2.1 %bitcast_convert_fusion = bf16[26,128,128]{2,1,0:T(8,128)(2,1)S(1)} fusion(bf16[26,2,128,128]{3,2,1,0:T(8,128)(2,1)S(1)} %gather_fusion, bf16[26,2,128,128]{3,2,1,0:T(8,128)(2,1)} %param.5), kind=kOutput, calls=%fused_computation.15 | convolution fusion | flops 218529792 | bytes 4259840 | tf_op jit(solution)/shard_map/tcij,tckj->tki/dot_general | solution.py:71
  10.2 1.0 gather_fusion.1
  11.1 0.2 fusion.3
  11.3 55.1 %all_to_all.10 = bf16[16,528,128]{2,1,0:T(8,128)(2,1)S(1)} all-to-all(bf16[16,528,128]{2,1,0:T(8,128)(2,1)S(1)} %fusion.3), channel_id=1, replica_groups=mesh['band'=2,'spk'=16] {'spk'}, dimensions={0} | all-to-all | bytes 4325376 | tf_op jit(solution)/shard_map/all_to_all | solution.py:83
  66.4 0.1 copy.60
  66.5 0.1 copy.45
  66.6 0.1 eq.112
  66.7 0.0 copy-start.2
  66.7 0.2 slice.33
  66.9 0.5 copy-done.2
  67.4 1.2 fusion.15
  68.6 0.1 copy.47
  68.7 0.1 reshape.196
  68.8 2.2 %gather_fusion.2 = bf16[64,128,128]{2,1,0:T(8,128)(2,1)} fusion(bf16[8,128,128]{2,1,0:T(8,128)(2,1)S(1)} %copy.48, s32[1024]{0:T(1024)S(1)} %pad_clamp_fusion.1), kind=kCustom, calls=%fused_computation.2 | custom fusion | bytes 4194560 | tf_op jit(solution)/shard_map/jit(_take)/gather | solution.py:93
  71.0 5.8 %all-to-all-start.1 = ((bf16[16,512,128]{2,1,0:T(8,128)(2,1)}), bf16[16,512,128]{2,1,0:T(8,128)(2,1)S(1)}, u32[]{:S(2)}, u32[]{:S(2)}) async-start(bf16[16,512,128]{2,1,0:T(8,128)(2,1)} %bitcast.20), calls=%async_computation.1 | async-start | bytes 4194304 | tf_op jit(solution)/shard_map/all_to_all | solution.py:94
  76.8 0.6 fusion.59
  78.1 46.1 %all-to-all-done.1 = bf16[16,512,128]{2,1,0:T(8,128)(2,1)S(1)} async-done(((bf16[16,512,128]{2,1,0:T(8,128)(2,1)}), bf16[16,512,128]{2,1,0:T(8,128)(2,1)S(1)}, u32[]{:S(2)}, u32[]{:S(2)}) %all-to-all-start.1) | async-done | bytes 2097184 | tf_op jit(solution)/shard_map/all_to_all | solution.py:94
  124.2 0.7 gather_fusion.3
  124.9 0.4 fusion.11
  125.4 0.0 copy-start
  125.4 0.2 pad_maximum_fusion
  125.5 1.3 copy-done
  126.8 1.1 fusion.23
  127.9 0.8 copy.51
  (19 shorter events, 0.2 us)
Async XLA Ops:
  0.0 6.8 %copy-start.1 = (f32[2,128,128]{2,1,0:T(8,128)S(1)}, f32[2,128,128]{2,1,0:T(8,128)}, u32[]{:S(2)}) copy-start(f32[2,128,128]{2,1,0:T(8,128)} %param.4) | copy-start | bytes 393220
  66.7 0.7 copy-start.2
  71.0 53.2 %all-to-all-start.1 = ((bf16[16,512,128]{2,1,0:T(8,128)(2,1)}), bf16[16,512,128]{2,1,0:T(8,128)(2,1)S(1)}, u32[]{:S(2)}, u32[]{:S(2)}) async-start(bf16[16,512,128]{2,1,0:T(8,128)(2,1)} %bitcast.20), calls=%async_computation.1 | async-start | bytes 4194304 | tf_op jit(solution)/shard_map/all_to_all | solution.py:94
  125.4 1.5 %copy-start = (bf16[26,2,128,128]{3,2,1,0:T(8,128)(2,1)S(1)}, bf16[26,2,128,128]{3,2,1,0:T(8,128)(2,1)}, u32[]{:S(2)}) copy-start(bf16[26,2,128,128]{3,2,1,0:T(8,128)(2,1)} %param.5) | copy-start | bytes 5111812

commit v13 on v12

--- a/solution.py
+++ b/solution.py
@@ -2,6 +2,8 @@
 import jax.numpy as jnp
 from jax import lax
 from jax.sharding import PartitionSpec as P
+from jax.experimental import pallas as pl
+from jax.experimental.pallas import tpu as pltpu
 
 SBLK = 32
 MBLK = 128
@@ -19,6 +21,44 @@
     flip = flip * jnp.where(col[None, :] < half, -sign, sign).astype(rows.dtype)
     return jnp.einsum("...ki,kl->...li", rows, flip, preferred_element_type=jnp.float32).astype(rows.dtype)
 
+
+def _forward_kernel(unit_ref, plant_ref, rows_ref, out_ref, power_ref):
+    pair = pl.program_id(0)
+    dims = (((1,), (1,)), ((), ()))
+    acc = lax.dot_general(rows_ref[0, 0], plant_ref[0, 0], dims, preferred_element_type=jnp.float32)
+    acc = acc + lax.dot_general(rows_ref[0, 1], plant_ref[0, 1], dims, preferred_element_type=jnp.float32)
+    out_ref[0] = acc.astype(out_ref.dtype)
+
+    @pl.when(pair == 0)
+    def _():
+        power_ref[...] = jnp.zeros_like(power_ref)
+
+    wide = plant_ref[0].astype(jnp.float32)
+    sq = wide * wide
+    power_ref[...] += jnp.sum(sq.reshape(-1, 8, sq.shape[-1]), axis=0)
+
+def forward_and_power(plant, rows, unit, interpret=False):
+    tiles, _, block, width = plant.shape
+    fw = rows.shape[2]
+    grid_spec = pltpu.PrefetchScalarGridSpec(
+        num_scalar_prefetch=1,
+        grid=(tiles,),
+        in_specs=[
+            pl.BlockSpec((1, 2, block, width), lambda t, u: (t, 0, 0, 0)),
+            pl.BlockSpec((1, 2, fw, width), lambda t, u: (u[t], 0, 0, 0)),
+        ],
+        out_specs=[
+            pl.BlockSpec((1, fw, block), lambda t, u: (t, 0, 0)),
+            pl.BlockSpec((8, width), lambda t, u: (0, 0)),
+        ],
+    )
+    return pl.pallas_call(
+        _forward_kernel,
+        grid_spec=grid_spec,
+        out_shape=[jax.ShapeDtypeStruct((tiles, fw, block), jnp.bfloat16),
+                   jax.ShapeDtypeStruct((8, width), jnp.float32)],
+        interpret=interpret,
+    )(unit, plant, rows)
 
 def slot_ranks(target_peer, devices):
     count = target_peer.shape[-1]
@@ -67,12 +107,9 @@
 
     rounded = jnp.swapaxes(direction.astype(jnp.bfloat16), 1, 2)
     both = jnp.stack([rounded, swap_halves(rounded, 1)], axis=1)
-    pair_rows = both[local_unit]
-    partial_field = jnp.einsum("tcij,tckj->tki", plant, pair_rows,
-                               preferred_element_type=jnp.float32).astype(jnp.bfloat16)
+    partial_field, power_tile = forward_and_power(plant, both, local_unit)
     outgoing = jnp.take(partial_field, slot_pair, axis=0, mode="clip")
-    local_power = jnp.trace(jnp.einsum("tcij,tcik->jk", plant, plant,
-                                       preferred_element_type=jnp.float32))
+    local_power = jnp.sum(power_tile)
     power_hi = local_power.astype(jnp.bfloat16).astype(jnp.float32)
     power_mid = (local_power - power_hi).astype(jnp.bfloat16).astype(jnp.float32)
     power_lo = local_power - power_hi - power_mid

time: 129 us -> 144 us (1.12)
  Pallas kernels: 0 us -> 16 us
  matrix products: 8.38 us -> 2.96 us
  other arithmetic: 2.95 us -> 5.51 us
    pallas_call x0 -> x1, Pallas kernels: none -> 16 us  [forward_and_power(): pl.pallas_call(_forward_kernel, grid_spec=grid_spec, out_shape=[jax.Shape...]
    dot_general x2 -> x0, matrix products: 5.42 us -> none  [the longest x1 3.36 us: per_device(): jnp.einsum('tcij,tcik->jk', plant, plant, preferred_element_type=jnp.floa...]
  transfers between devices with their start and end apart: 1 -> 1, of which waited for: 1 -> 1; matrix products, arithmetic and copies ran while one was open for 1% -> 0% of each run, Pallas kernels for 0% -> 0%
where the time goes in v13:
time: 144 us; the launch traced here: 143 us
  blocking collectives  55.1 us (38%)
  waiting for transfers between devices  46.1 us (32%)
  Pallas kernels  16 us (11%)
  local copies, waits for them, and re-layouts  9.36 us (6%)
  starting transfers between devices  5.78 us (4%)
  other arithmetic  5.51 us (4%)
  matrix products  2.96 us (2%)
  between operations  2.14 us (1%)
    all_to_all x1, blocking collectives, per_device(): lax.all_to_all(sent, 'spk', 0, 0, tiled=True)  55.1 us
    all_to_all x1, waiting for transfers between devices, per_device(): lax.all_to_all(reply.reshape(devices, capacity * field_width, block_size)...  46.1 us
    pallas_call x1, Pallas kernels, forward_and_power(): pl.pallas_call(_forward_kernel, grid_spec=grid_spec, out_shape=[jax.Shape...  16 us
    all_to_all x1, starting transfers between devices, per_device(): lax.all_to_all(reply.reshape(devices, capacity * field_width, block_size)...  5.78 us
  transfers between devices with their start and end apart: 1, of which 1 were waited for; matrix products, arithmetic and copies ran while one was open for 0% of the time, Pallas kernels for 0%

profile of v13, /device:TPU:13, one launch (start us, length us, event | category | flops | bytes accessed | tf_op | source)
XLA Modules:
  0.0 142.9 jit_solution(7307862537906901994)
XLA Ops:
  0.0 0.8 and_select_fusion.2
  0.8 1.3 fusion.54
  2.1 0.2 convert_reduce_fusion
  2.3 0.1 fusion.38
  2.4 0.1 select_reduce_fusion.1
  2.5 0.1 concatenate.16
  2.6 1.0 copy.34
  3.6 0.2 fusion.26
  3.8 0.7 pad_maximum_fusion.1.rows_ref
  4.5 16.0 %shard_map.46 = (bf16[26,128,128]{2,1,0:T(8,128)(2,1)}, f32[8,128]{1,0:T(8,128)}) custom-call(s32[26]{0:T(128)} %get-tuple-element.13.unit_ref, bf16[26,2,128,128]{3,2,1,0:T(8,128)(2,1)} %plant_ref.1, bf16[2,2,128,128]{3,2,1,0:T(8,128)(2,1)} %pad_maximum_fusion.1.rows_ref), custom_call_target="tpu_custom_call" | custom-call | tf_op jit(solution)/shard_map/pallas_call | solution.py:55
  20.5 1.3 reduce_sum.59
  23.1 0.1 maximum_convert_fusion
  23.2 0.1 pad.10.clone
  23.3 2.1 %gather_fusion = bf16[64,128,128]{2,1,0:T(8,128)(2,1)S(1)} fusion(bf16[26,128,128]{2,1,0:T(8,128)(2,1)} %get-tuple-element.7, s32[1024]{0:T(1024)S(1)} %pad_clamp_fusion.2), kind=kCustom, calls=%fused_computation | custom fusion | bytes 4194560 | tf_op jit(solution)/shard_map/jit(_take)/gather | solution.py:111
  25.4 0.2 fusion.3
  25.6 55.1 %all_to_all.10 = bf16[16,528,128]{2,1,0:T(8,128)(2,1)S(1)} all-to-all(bf16[16,528,128]{2,1,0:T(8,128)(2,1)S(1)} %fusion.3), channel_id=1, replica_groups=mesh['band'=2,'spk'=16] {'spk'}, dimensions={0} | all-to-all | bytes 4325376 | tf_op jit(solution)/shard_map/all_to_all | solution.py:120
  80.6 0.1 copy.48
  80.8 0.1 copy.37
  80.8 0.1 eq.107
  80.9 0.0 copy-start.1
  80.9 0.2 slice.31
  81.2 0.5 copy-done.1
  81.6 1.2 fusion.13
  82.9 0.1 copy.39
  83.0 0.1 reshape.188
  83.1 2.2 %gather_fusion.1 = bf16[64,128,128]{2,1,0:T(8,128)(2,1)} fusion(bf16[8,128,128]{2,1,0:T(8,128)(2,1)S(1)} %copy.40, s32[1024]{0:T(1024)S(1)} %pad_clamp_fusion.1), kind=kCustom, calls=%fused_computation.1 | custom fusion | bytes 4194560 | tf_op jit(solution)/shard_map/jit(_take)/gather | solution.py:130
  85.2 5.8 %all-to-all-start.1 = ((bf16[16,512,128]{2,1,0:T(8,128)(2,1)}), bf16[16,512,128]{2,1,0:T(8,128)(2,1)S(1)}, u32[]{:S(2)}, u32[]{:S(2)}) async-start(bf16[16,512,128]{2,1,0:T(8,128)(2,1)} %bitcast.16), calls=%async_computation.1 | async-start | bytes 4194304 | tf_op jit(solution)/shard_map/all_to_all | solution.py:131
  91.1 0.6 fusion.49
  92.3 46.1 %all-to-all-done.1 = bf16[16,512,128]{2,1,0:T(8,128)(2,1)S(1)} async-done(((bf16[16,512,128]{2,1,0:T(8,128)(2,1)}), bf16[16,512,128]{2,1,0:T(8,128)(2,1)S(1)}, u32[]{:S(2)}, u32[]{:S(2)}) %all-to-all-start.1) | async-done | bytes 2097184 | tf_op jit(solution)/shard_map/all_to_all | solution.py:131
  138.4 0.7 gather_fusion.2
  139.2 0.4 fusion.9
  139.6 0.0 copy-start
  139.6 0.2 pad_maximum_fusion
  139.8 1.3 copy-done
  141.1 1.1 fusion.21
  142.2 0.8 copy.43
  (17 shorter events, 0.2 us)
Async XLA Ops:
  80.9 0.7 copy-start.1
  85.2 53.2 %all-to-all-start.1 = ((bf16[16,512,128]{2,1,0:T(8,128)(2,1)}), bf16[16,512,128]{2,1,0:T(8,128)(2,1)S(1)}, u32[]{:S(2)}, u32[]{:S(2)}) async-start(bf16[16,512,128]{2,1,0:T(8,128)(2,1)} %bitcast.16), calls=%async_computation.1 | async-start | bytes 4194304 | tf_op jit(solution)/shard_map/all_to_all | solution.py:131
  139.6 1.5 %copy-start = (bf16[26,2,128,128]{3,2,1,0:T(8,128)(2,1)S(1)}, bf16[26,2,128,128]{3,2,1,0:T(8,128)(2,1)}, u32[]{:S(2)}) copy-start(bf16[26,2,128,128]{3,2,1,0:T(8,128)(2,1)} %plant_ref.1) | copy-start | bytes 5111812

commit v14 on v13

--- a/solution.py
+++ b/solution.py
@@ -23,33 +23,32 @@
 
 
 def _forward_kernel(unit_ref, plant_ref, rows_ref, out_ref, power_ref):
-    pair = pl.program_id(0)
     dims = (((1,), (1,)), ((), ()))
-    acc = lax.dot_general(rows_ref[0, 0], plant_ref[0, 0], dims, preferred_element_type=jnp.float32)
-    acc = acc + lax.dot_general(rows_ref[0, 1], plant_ref[0, 1], dims, preferred_element_type=jnp.float32)
-    out_ref[0] = acc.astype(out_ref.dtype)
+    lanes = plant_ref.shape[-1]
 
-    @pl.when(pair == 0)
-    def _():
-        power_ref[...] = jnp.zeros_like(power_ref)
+    def body(pair, power):
+        unit = unit_ref[pair]
+        acc = lax.dot_general(rows_ref[unit, 0], plant_ref[pair, 0], dims, preferred_element_type=jnp.float32)
+        acc = acc + lax.dot_general(rows_ref[unit, 1], plant_ref[pair, 1], dims, preferred_element_type=jnp.float32)
+        out_ref[pair] = acc.astype(out_ref.dtype)
+        wide = plant_ref[pair].astype(jnp.float32)
+        return power + jnp.sum((wide * wide).reshape(-1, 8, lanes), axis=0)
 
-    wide = plant_ref[0].astype(jnp.float32)
-    sq = wide * wide
-    power_ref[...] += jnp.sum(sq.reshape(-1, 8, sq.shape[-1]), axis=0)
+    power_ref[...] = lax.fori_loop(0, plant_ref.shape[0], body, jnp.zeros((8, lanes), jnp.float32))
 
 def forward_and_power(plant, rows, unit, interpret=False):
     tiles, _, block, width = plant.shape
     fw = rows.shape[2]
     grid_spec = pltpu.PrefetchScalarGridSpec(
         num_scalar_prefetch=1,
-        grid=(tiles,),
+        grid=(1,),
         in_specs=[
-            pl.BlockSpec((1, 2, block, width), lambda t, u: (t, 0, 0, 0)),
-            pl.BlockSpec((1, 2, fw, width), lambda t, u: (u[t], 0, 0, 0)),
+            pl.BlockSpec(plant.shape, lambda i, u: (0, 0, 0, 0)),
+            pl.BlockSpec(rows.shape, lambda i, u: (0, 0, 0, 0)),
         ],
         out_specs=[
-            pl.BlockSpec((1, fw, block), lambda t, u: (t, 0, 0)),
-            pl.BlockSpec((8, width), lambda t, u: (0, 0)),
+            pl.BlockSpec((tiles, fw, block), lambda i, u: (0, 0, 0)),
+            pl.BlockSpec((8, width), lambda i, u: (0, 0)),
         ],
     )
     return pl.pallas_call(

time: 144 us -> 135 us (0.938)
  Pallas kernels: 16 us -> 7.58 us
    pallas_call x1, Pallas kernels: 16 us -> 7.58 us  [forward_and_power(): pl.pallas_call(_forward_kernel, grid_spec=grid_spec, out_shape=[jax.Shape...]
where the time goes in v14:
time: 135 us
  blocking collectives  55.1 us (41%)
  waiting for transfers between devices  46.1 us (34%)
  local copies, waits for them, and re-layouts  9.36 us (7%)
  Pallas kernels  7.58 us (6%)
  starting transfers between devices  5.78 us (4%)
  other arithmetic  5.51 us (4%)
  matrix products  2.96 us (2%)
  between operations  2.14 us (2%)
    all_to_all x1, blocking collectives, per_device(): lax.all_to_all(sent, 'spk', 0, 0, tiled=True)  55.1 us
    all_to_all x1, waiting for transfers between devices, per_device(): lax.all_to_all(reply.reshape(devices, capacity * field_width, block_size)...  46.1 us
    pallas_call x1, Pallas kernels, forward_and_power(): pl.pallas_call(_forward_kernel, grid_spec=grid_spec, out_shape=[jax.Shape...  7.58 us
    all_to_all x1, starting transfers between devices, per_device(): lax.all_to_all(reply.reshape(devices, capacity * field_width, block_size)...  5.78 us
    unnamed x7, local copies, waits for them, and re-layouts  2.86 us
  transfers between devices with their start and end apart: 1, of which 1 were waited for; matrix products, arithmetic and copies ran while one was open for 0% of the time, Pallas kernels for 0%

profile of v14, /device:TPU:13, one launch (start us, length us, event | category | flops | bytes accessed | tf_op | source)
XLA Modules:
  0.0 134.6 jit_solution(13718187736532197349)
XLA Ops:
  0.0 0.8 and_select_fusion.2
  0.8 1.3 fusion.54
  2.1 0.2 convert_reduce_fusion
  2.3 0.1 fusion.38
  2.4 0.1 select_reduce_fusion.1
  2.5 0.1 concatenate.16
  2.6 1.0 copy.34
  3.6 0.2 fusion.26
  3.8 0.7 pad_maximum_fusion.1.rows_ref
  4.5 7.6 %shard_map.46 = (bf16[26,128,128]{2,1,0:T(8,128)(2,1)}, f32[8,128]{1,0:T(8,128)}) custom-call(s32[26]{0:T(128)} %get-tuple-element.13.unit_ref, bf16[26,2,128,128]{3,2,1,0:T(8,128)(2,1)} %plant_ref.1, bf16[2,2,128,128]{3,2,1,0:T(8,128)(2,1)} %pad_maximum_fusion.1.rows_ref), custom_call_target="tpu_custom_call" | custom-call | tf_op jit(solution)/shard_map/pallas_call | solution.py:54
  12.1 1.3 reduce_sum.59
  14.7 0.1 maximum_convert_fusion
  14.8 0.1 pad.10.clone
  14.9 2.1 %gather_fusion = bf16[64,128,128]{2,1,0:T(8,128)(2,1)S(1)} fusion(bf16[26,128,128]{2,1,0:T(8,128)(2,1)} %get-tuple-element.7, s32[1024]{0:T(1024)S(1)} %pad_clamp_fusion.2), kind=kCustom, calls=%fused_computation | custom fusion | bytes 4194560 | tf_op jit(solution)/shard_map/jit(_take)/gather | solution.py:110
  17.0 0.2 fusion.3
  17.2 55.1 %all_to_all.10 = bf16[16,528,128]{2,1,0:T(8,128)(2,1)S(1)} all-to-all(bf16[16,528,128]{2,1,0:T(8,128)(2,1)S(1)} %fusion.3), channel_id=1, replica_groups=mesh['band'=2,'spk'=16] {'spk'}, dimensions={0} | all-to-all | bytes 4325376 | tf_op jit(solution)/shard_map/all_to_all | solution.py:119
  72.3 0.1 copy.48
  72.4 0.1 copy.37
  72.5 0.1 eq.107
  72.6 0.0 copy-start.1
  72.6 0.2 slice.31
  72.8 0.5 copy-done.1
  73.3 1.2 fusion.13
  74.5 0.1 copy.39
  74.6 0.1 reshape.188
  74.7 2.2 %gather_fusion.1 = bf16[64,128,128]{2,1,0:T(8,128)(2,1)} fusion(bf16[8,128,128]{2,1,0:T(8,128)(2,1)S(1)} %copy.40, s32[1024]{0:T(1024)S(1)} %pad_clamp_fusion.1), kind=kCustom, calls=%fused_computation.1 | custom fusion | bytes 4194560 | tf_op jit(solution)/shard_map/jit(_take)/gather | solution.py:129
  76.9 5.8 %all-to-all-start.1 = ((bf16[16,512,128]{2,1,0:T(8,128)(2,1)}), bf16[16,512,128]{2,1,0:T(8,128)(2,1)S(1)}, u32[]{:S(2)}, u32[]{:S(2)}) async-start(bf16[16,512,128]{2,1,0:T(8,128)(2,1)} %bitcast.16), calls=%async_computation.1 | async-start | bytes 4194304 | tf_op jit(solution)/shard_map/all_to_all | solution.py:130
  82.7 0.6 fusion.49
  84.0 46.1 %all-to-all-done.1 = bf16[16,512,128]{2,1,0:T(8,128)(2,1)S(1)} async-done(((bf16[16,512,128]{2,1,0:T(8,128)(2,1)}), bf16[16,512,128]{2,1,0:T(8,128)(2,1)S(1)}, u32[]{:S(2)}, u32[]{:S(2)}) %all-to-all-start.1) | async-done | bytes 2097184 | tf_op jit(solution)/shard_map/all_to_all | solution.py:130
  130.1 0.7 gather_fusion.2
  130.8 0.4 fusion.9
  131.2 0.0 copy-start
  131.3 0.2 pad_maximum_fusion
  131.4 1.3 copy-done
  132.7 1.1 fusion.21
  133.8 0.8 copy.43
  (17 shorter events, 0.2 us)
Async XLA Ops:
  72.6 0.7 copy-start.1
  76.9 53.2 %all-to-all-start.1 = ((bf16[16,512,128]{2,1,0:T(8,128)(2,1)}), bf16[16,512,128]{2,1,0:T(8,128)(2,1)S(1)}, u32[]{:S(2)}, u32[]{:S(2)}) async-start(bf16[16,512,128]{2,1,0:T(8,128)(2,1)} %bitcast.16), calls=%async_computation.1 | async-start | bytes 4194304 | tf_op jit(solution)/shard_map/all_to_all | solution.py:130
  131.2 1.5 %copy-start = (bf16[26,2,128,128]{3,2,1,0:T(8,128)(2,1)S(1)}, bf16[26,2,128,128]{3,2,1,0:T(8,128)(2,1)}, u32[]{:S(2)}) copy-start(bf16[26,2,128,128]{3,2,1,0:T(8,128)(2,1)} %plant_ref.1) | copy-start | bytes 5111812

commit v15 on v5

--- a/solution.py
+++ b/solution.py
@@ -21,9 +21,10 @@
 
 
 def slot_ranks(target_peer, devices):
-    onehot = (target_peer[..., :, None] == jnp.arange(devices)).astype(jnp.int32)
-    running = jnp.cumsum(onehot, axis=-2)
-    return jnp.take_along_axis(running, target_peer[..., None], axis=-1)[..., 0] - 1
+    count = target_peer.shape[-1]
+    earlier = jnp.arange(count)[None, :] < jnp.arange(count)[:, None]
+    same = target_peer[:, None] == target_peer[None, :]
+    return jnp.sum((earlier & same).astype(jnp.int32), axis=1)
 
 
 def with_header(blocks, values, devices, capacity):
@@ -71,27 +72,39 @@
                                preferred_element_type=jnp.float32).astype(jnp.bfloat16)
     outgoing = jnp.take(partial_field, slot_pair, axis=0, mode="clip")
     sent = with_header(outgoing, slot_label.reshape(devices, capacity), devices, capacity)
-    arrived, labels_in = split_header(
+    arrived, header_in = split_header(
         lax.all_to_all(sent, "spk", 0, 0, tiled=True), capacity, field_width, capacity)
-    labels_in = labels_in.astype(jnp.int32).reshape(slots)
+    labels_in = header_in.astype(jnp.int32).reshape(slots)
     recv_onehot = (labels_in[None, :] == jnp.arange(mic_units)[:, None]).astype(jnp.bfloat16)
     pressure = jnp.einsum("ms,ski->mki", recv_onehot, arrived, preferred_element_type=jnp.float32)
     weights_flat = mic_weight.reshape(mic_units, block_size)
     weighted = (weights_flat[:, None, :] * pressure).astype(jnp.bfloat16)
 
-    local_power = jnp.sum(jnp.square(plant.astype(jnp.float32)))
+    local_power = jnp.trace(jnp.einsum("tcij,tcik->jk", plant, plant,
+                                       preferred_element_type=jnp.float32))
     power_hi = local_power.astype(jnp.bfloat16).astype(jnp.float32)
     power_mid = (local_power - power_hi).astype(jnp.bfloat16).astype(jnp.float32)
     power_lo = local_power - power_hi - power_mid
-    power_parts = jnp.stack([power_hi, power_mid, power_lo])[None, :]
-    shared = with_header(weighted, power_parts, 1, mic_units)[0]
-    gathered = lax.all_gather(shared, "spk")
+    power_row = jnp.zeros((16, block_size), jnp.float32).at[0, :3].set(
+        jnp.stack([power_hi, power_mid, power_lo])).astype(jnp.bfloat16)
+    groups = field_width // 16
+    per_peer = capacity * groups + 1
+    source_rows = jnp.concatenate(
+        [weighted.reshape(mic_units * groups, 16, block_size), power_row[None]], axis=0)
+    reply_group = (jnp.minimum(labels_in, mic_units - 1) * groups)[:, None] + jnp.arange(groups)
+    reply_index = jnp.concatenate(
+        [reply_group.reshape(devices, capacity * groups),
+         jnp.full((devices, 1), mic_units * groups, jnp.int32)], axis=1)
+    reply = jnp.take(source_rows, reply_index.reshape(-1), axis=0, mode="clip")
+    returned = lax.all_to_all(
+        reply.reshape(devices, per_peer * 16, block_size), "spk", 0, 0, tiled=True)
     source_bin = jnp.arange(devices) // groups_per_bin
-    power_of = jnp.sum(gathered[:, mic_units * field_width, :3].astype(jnp.float32), axis=1)
+    power_of = jnp.sum(returned[:, capacity * field_width, :3].astype(jnp.float32), axis=1)
     bin_power = jnp.sum(jnp.where(source_bin == my_bin, power_of, 0.0))
-    tile_weighted = jax.vmap(
-        lambda peer, row: lax.dynamic_slice(gathered, (peer, row, 0), (1, field_width, block_size))[0]
-    )(target_peer, target_label * field_width)
+    rank = position - target_peer * capacity
+    pick = (target_peer * per_peer + rank * groups)[:, None] + jnp.arange(groups)
+    tile_weighted = jnp.take(returned.reshape(devices * per_peer, 16, block_size), pick.reshape(-1),
+                             axis=0, mode="clip").reshape(tile_count, field_width, block_size)
 
     back_rows = jnp.stack([tile_weighted, swap_halves(tile_weighted, -1)], axis=1)
     unit_mask = (local_unit[:, None] == jnp.arange(unit_count)[None, :]).astype(jnp.bfloat16)

time: 154 us -> 130 us (0.84); the launches traced: 151 us -> 129 us
  between operations: 15.7 us -> 2.18 us
  local copies, waits for them, and re-layouts: 20.9 us -> 10.3 us
  starting transfers between devices: 6.56 us -> 11.3 us
  other arithmetic: 8.86 us -> 4.64 us
  matrix products: 5.07 us -> 8.38 us
  waiting for transfers between devices: 94.3 us -> 92.6 us
    all_gather x1 -> x0, waiting for transfers between devices: 49.8 us -> none  [per_device(): gathered = lax.all_gather(shared, 'spk')]
    all_to_all x0 -> x1, waiting for transfers between devices: none -> 48.6 us  [per_device(): lax.all_to_all(reply.reshape(devices, per_peer * 16, block_size), 'spk',...]
    all_gather x1 -> x0, local copies, waits for them, and re-layouts: 8.72 us -> none  [per_device(): gathered = lax.all_gather(shared, 'spk')]
    all_to_all x0 -> x1, starting transfers between devices: none -> 4.78 us  [per_device(): lax.all_to_all(reply.reshape(devices, per_peer * 16, block_size), 'spk',...]
    reduce_sum x2, other arithmetic: 3.9 us -> 0.38 us  [the longest x1 0.2 us: per_device(): jnp.sum(returned[:, capacity * field_width, :3].astype(jnp.float32), axis=1)]
    dot_general x0 -> x1, matrix products: none -> 3.35 us  [per_device(): jnp.einsum('tcij,tcik->jk', plant, plant, preferred_element_type=jnp.floa...]
    gather x3 -> x2, local copies, waits for them, and re-layouts: 6.03 us -> 3.96 us  [the longest x1 3.17 us: per_device(): reply = jnp.take(source_rows, reply_index.reshape(-1), axis=0, mode='clip')]
  transfers between devices with their start and end apart: 2 -> 2, of which waited for: 2 -> 2; matrix products, arithmetic and copies ran while one was open for 2% -> 3% of each run, Pallas kernels for 0% -> 0%
where the time goes in v15:
time: 130 us; the launch traced here: 129 us
  waiting for transfers between devices  92.6 us (71%)
  starting transfers between devices  11.3 us (9%)
  local copies, waits for them, and re-layouts  10.3 us (8%)
  matrix products  8.38 us (6%)
  other arithmetic  4.64 us (4%)
  between operations  2.18 us (2%)
    all_to_all x1, waiting for transfers between devices, per_device(): lax.all_to_all(reply.reshape(devices, per_peer * 16, block_size), 'spk',...  48.6 us
    all_to_all x1, waiting for transfers between devices, per_device(): lax.all_to_all(sent, 'spk', 0, 0, tiled=True)  44 us
    all_to_all x1, starting transfers between devices, per_device(): lax.all_to_all(sent, 'spk', 0, 0, tiled=True)  6.52 us
    all_to_all x1, starting transfers between devices, per_device(): lax.all_to_all(reply.reshape(devices, per_peer * 16, block_size), 'spk',...  4.78 us
    dot_general x1, matrix products, per_device(): jnp.einsum('tcij,tcik->jk', plant, plant, preferred_element_type=jnp.floa...  3.35 us
    gather x1, local copies, waits for them, and re-layouts, per_device(): reply = jnp.take(source_rows, reply_index.reshape(-1), axis=0, mode='clip')  3.17 us
    unnamed x7, local copies, waits for them, and re-layouts  2.92 us
  transfers between devices with their start and end apart: 2, of which 2 were waited for; matrix products, arithmetic and copies ran while one was open for 3% of the time, Pallas kernels for 0%

profile of v15, /device:TPU:13, one launch (start us, length us, event | category | flops | bytes accessed | tf_op | source)
XLA Modules:
  0.0 129.4 jit_solution(907460203609287291)
XLA Ops:
  0.0 0.8 fusion.63
  0.8 0.7 fusion.65
  1.5 0.2 convert_reduce_fusion
  1.7 0.1 fusion.49
  1.8 0.1 select_reduce_fusion.1
  1.9 0.1 convert_element_type.122
  2.0 1.0 copy.72
  3.0 0.2 fusion.28
  3.3 0.9 gather_fusion
  4.1 2.1 %bitcast_convert_fusion = bf16[26,128,128]{2,1,0:T(8,128)(2,1)S(1)} fusion(bf16[26,2,128,128]{3,2,1,0:T(8,128)(2,1)S(1)} %gather_fusion, bf16[26,2,128,128]{3,2,1,0:T(8,128)(2,1)} %param.7), kind=kOutput, calls=%fused_computation.15 | convolution fusion | flops 218529792 | bytes 4259840 | tf_op jit(solution)/shard_map/tcij,tckj->tki/dot_general | solution.py:71
  6.2 1.0 gather_fusion.1
  7.2 1.5 %fusion.3 = bf16[16,528,128]{2,1,0:T(8,128)(2,1)} fusion(bf16[16,1,4]{2,1,0:T(2,128)(2,1)S(1)} %convert_element_type.122, bf16[16,512,128]{2,1,0:T(8,128)(2,1)S(1)} %bitcast.92), kind=kLoop, calls=%fused_computation.8 | loop fusion | flops 6488064 | bytes 4259968 | tf_op jit(solution)/shard_map/concatenate | solution.py:34
  8.7 6.5 %all-to-all-start = ((bf16[16,528,128]{2,1,0:T(8,128)(2,1)}), bf16[16,528,128]{2,1,0:T(8,128)(2,1)S(1)}, u32[]{:S(2)}, u32[]{:S(2)}) async-start(bf16[16,528,128]{2,1,0:T(8,128)(2,1)} %fusion.3), calls=%async_computation | async-start | bytes 4325376 | tf_op jit(solution)/shard_map/all_to_all | solution.py:76
  15.2 3.3 %fusion.35 = f32[]{:T(128)} fusion(bf16[26,2,128,128]{3,2,1,0:T(8,128)(2,1)} %param.7), kind=kOutput, calls=%fused_computation.28 | convolution fusion | flops 218152960 | bytes 1703940 | tf_op jit(solution)/shard_map/tcij,tcik->jk/dot_general | solution.py:83
  19.9 0.1 add.133
  19.9 0.1 maximum_bitcast_fusion
  20.0 44.0 %all-to-all-done = bf16[16,528,128]{2,1,0:T(8,128)(2,1)S(1)} async-done(((bf16[16,528,128]{2,1,0:T(8,128)(2,1)}), bf16[16,528,128]{2,1,0:T(8,128)(2,1)S(1)}, u32[]{:S(2)}, u32[]{:S(2)}) %all-to-all-start) | async-done | bytes 2162720 | tf_op jit(solution)/shard_map/all_to_all | solution.py:76
  64.0 0.1 copy.92
  64.1 0.1 copy.75
  64.2 0.1 reshape.246
  64.3 0.0 copy-start.1
  64.3 0.2 slice.45
  64.5 0.5 copy-done.1
  65.0 1.2 fusion.15
  66.3 0.1 bitcast_add_fusion
  66.3 0.1 copy.94
  66.4 0.1 reshape.265
  66.6 3.2 %gather_fusion.2 = bf16[528,16,128]{2,1,0:T(8,128)(2,1)} fusion(bf16[65,16,128]{2,1,0:T(8,128)(2,1)S(1)} %pad_maximum_fusion.1, s32[1024]{0:T(1024)S(1)} %pad_clamp_fusion.1), kind=kCustom, calls=%fused_computation.2 | custom fusion | bytes 4327488 | tf_op jit(solution)/shard_map/jit(_take)/gather | solution.py:98
  69.7 4.8 %all-to-all-start.1 = ((bf16[16,528,128]{2,1,0:T(8,128)(2,1)}), bf16[16,528,128]{2,1,0:T(8,128)(2,1)S(1)}, u32[]{:S(2)}, u32[]{:S(2)}) async-start(bf16[16,528,128]{2,1,0:T(8,128)(2,1)} %bitcast.24), calls=%async_computation.1 | async-start | bytes 4325376 | tf_op jit(solution)/shard_map/all_to_all | solution.py:99
  74.5 0.1 iota_add_fusion
  74.6 0.1 reshape.273
  74.7 48.6 %all-to-all-done.1 = bf16[16,528,128]{2,1,0:T(8,128)(2,1)S(1)} async-done(((bf16[16,528,128]{2,1,0:T(8,128)(2,1)}), bf16[16,528,128]{2,1,0:T(8,128)(2,1)S(1)}, u32[]{:S(2)}, u32[]{:S(2)}) %all-to-all-start.1) | async-done | bytes 2162720 | tf_op jit(solution)/shard_map/all_to_all | solution.py:99
  123.3 0.2 fusion.54
  123.5 0.6 fusion.60
  124.8 0.8 gather_fusion.3
  125.6 0.4 fusion.11
  126.0 0.0 copy-start
  126.0 0.2 pad_maximum_fusion
  126.2 1.3 copy-done
  127.5 1.1 fusion.23
  128.6 0.8 copy.83
  (20 shorter events, 0.2 us)
Async XLA Ops:
  8.7 55.3 %all-to-all-start = ((bf16[16,528,128]{2,1,0:T(8,128)(2,1)}), bf16[16,528,128]{2,1,0:T(8,128)(2,1)S(1)}, u32[]{:S(2)}, u32[]{:S(2)}) async-start(bf16[16,528,128]{2,1,0:T(8,128)(2,1)} %fusion.3), calls=%async_computation | async-start | bytes 4325376 | tf_op jit(solution)/shard_map/all_to_all | solution.py:76
  64.3 0.7 copy-start.1
  69.7 53.6 %all-to-all-start.1 = ((bf16[16,528,128]{2,1,0:T(8,128)(2,1)}), bf16[16,528,128]{2,1,0:T(8,128)(2,1)S(1)}, u32[]{:S(2)}, u32[]{:S(2)}) async-start(bf16[16,528,128]{2,1,0:T(8,128)(2,1)} %bitcast.24), calls=%async_computation.1 | async-start | bytes 4325376 | tf_op jit(solution)/shard_map/all_to_all | solution.py:99
  126.0 1.5 %copy-start = (bf16[26,2,128,128]{3,2,1,0:T(8,128)(2,1)S(1)}, bf16[26,2,128,128]{3,2,1,0:T(8,128)(2,1)}, u32[]{:S(2)}) copy-start(bf16[26,2,128,128]{3,2,1,0:T(8,128)(2,1)} %param.7) | copy-start | bytes 5111812

commit v16 on v12

--- a/solution.py
+++ b/solution.py
@@ -39,6 +39,14 @@
     return body, buffer[:, capacity * rows, :width]
 
 
+def exchange(blocks, devices, direction):
+    received = [blocks[0]]
+    for shift in range(1, devices):
+        pairs = [(i, (i + direction * shift) % devices) for i in range(devices)]
+        received.append(lax.ppermute(blocks[shift], "spk", pairs))
+    return jnp.stack(received)
+
+
 def per_device(direction, plant, tile_pairs, mic_weight):
     devices = lax.axis_size("spk")
     device_id = lax.axis_index("spk")
@@ -57,7 +65,8 @@
     local_unit = tile_pairs[:, 0] % unit_count
     mic_block = tile_pairs[:, 1]
     target_peer = mic_block // peer_blocks
-    position = target_peer * capacity + slot_ranks(target_peer, devices)
+    shift_of = (target_peer - device_id) % devices
+    position = shift_of * capacity + slot_ranks(target_peer, devices)
     send_hit = position[None, :] == jnp.arange(slots)[:, None]
     slot_pair = jnp.sum(jnp.where(send_hit, jnp.arange(tile_count), 0), axis=1)
     target_label = my_bin * peer_blocks + mic_block - target_peer * peer_blocks
@@ -79,10 +88,9 @@
     power_parts = jnp.broadcast_to(jnp.stack([power_hi, power_mid, power_lo]), (devices, 3))
     header = jnp.concatenate([slot_label.reshape(devices, capacity).astype(jnp.float32), power_parts], axis=1)
     sent = with_header(outgoing, header, devices, capacity)
-    arrived, header_in = split_header(
-        lax.all_to_all(sent, "spk", 0, 0, tiled=True), capacity, field_width, capacity + 3)
+    arrived, header_in = split_header(exchange(sent, devices, 1), capacity, field_width, capacity + 3)
     labels_in = header_in[:, :capacity].astype(jnp.int32).reshape(slots)
-    source_bin = jnp.arange(devices) // groups_per_bin
+    source_bin = ((device_id - jnp.arange(devices)) % devices) // groups_per_bin
     power_of = jnp.sum(header_in[:, capacity:].astype(jnp.float32), axis=1)
     bin_power = jnp.sum(jnp.where(source_bin == my_bin, power_of, 0.0))
     recv_onehot = (labels_in[None, :] == jnp.arange(mic_units)[:, None]).astype(jnp.bfloat16)
@@ -91,9 +99,8 @@
     weighted = (weights_flat[:, None, :] * pressure).astype(jnp.bfloat16)
 
     reply = jnp.take(weighted, jnp.minimum(labels_in, mic_units - 1), axis=0, mode="clip")
-    returned = lax.all_to_all(
-        reply.reshape(devices, capacity * field_width, block_size), "spk", 0, 0, tiled=True
-    ).reshape(slots, field_width, block_size)
+    returned = exchange(reply.reshape(devices, capacity * field_width, block_size), devices, -1
+                        ).reshape(slots, field_width, block_size)
     tile_weighted = jnp.take(returned, position, axis=0, mode="clip")
 
     back_rows = jnp.stack([tile_weighted, swap_halves(tile_weighted, -1)], axis=1)

time: 129 us -> 134 us (1.039)
  the two profiles are of different devices: /device:TPU:13 before, /device:TPU:0 now
where the time goes in v16:
time: 134 us
  starting transfers between devices  65.1 us (49%)
  waiting for transfers between devices  42.1 us (31%)
  local copies, waits for them, and re-layouts  12.4 us (9%)
  matrix products  8.38 us (6%)
  other arithmetic  3.04 us (2%)
  between operations  2.56 us (2%)
    ppermute x30, starting transfers between devices, exchange(): received.append(lax.ppermute(blocks[shift], 'spk', pairs))  65.1 us
    ppermute x30, waiting for transfers between devices, exchange(): received.append(lax.ppermute(blocks[shift], 'spk', pairs))  42.1 us
    unnamed x41, local copies, waits for them, and re-layouts  6.07 us
    dot_general x1, matrix products, per_device(): jnp.einsum('tcij,tcik->jk', plant, plant, preferred_element_type=jnp.floa...  3.36 us
  transfers between devices with their start and end apart: 30, of which 11 were waited for; matrix products, arithmetic and copies ran while one was open for 3% of the time, Pallas kernels for 0%

profile of v16, /device:TPU:0, one launch (start us, length us, event | category | flops | bytes accessed | tf_op | source)
XLA Modules:
  0.0 133.7 jit_solution(5725872817229459236)
XLA Ops:
  0.0 0.8 fusion.69
  0.8 0.7 fusion.70
  1.5 0.2 convert_reduce_fusion
  1.7 0.1 fusion.49
  2.0 3.4 %fusion.35 = f32[]{:T(128)} fusion(bf16[26,2,128,128]{3,2,1,0:T(8,128)(2,1)} %param.5), kind=kOutput, calls=%fused_computation.28 | convolution fusion | flops 218152960 | bytes 1703940 | tf_op jit(solution)/shard_map/tcij,tcik->jk/dot_general | solution.py:83
  6.8 0.1 copy.41
  7.0 0.2 fusion.28
  7.2 0.9 gather_fusion
  8.1 2.1 %bitcast_convert_fusion = bf16[26,128,128]{2,1,0:T(8,128)(2,1)S(1)} fusion(bf16[26,2,128,128]{3,2,1,0:T(8,128)(2,1)S(1)} %gather_fusion, bf16[26,2,128,128]{3,2,1,0:T(8,128)(2,1)} %param.5), kind=kOutput, calls=%fused_computation.15 | convolution fusion | flops 218529792 | bytes 4259840 | tf_op jit(solution)/shard_map/tcij,tckj->tki/dot_general | solution.py:80
  10.2 1.0 gather_fusion.1
  11.1 0.1 fusion.3
  11.3 0.1 slice_bitcast_fusion
  11.4 0.6 collective-permute-start
  12.0 2.6 %collective-permute-start.1 = (bf16[528,128]{1,0:T(8,128)(2,1)S(1)}, bf16[528,128]{1,0:T(8,128)(2,1)S(1)}, u32[]{:S(2)}, u32[]{:S(2)}) collective-permute-start(bf16[528,128]{1,0:T(8,128)(2,1)S(1)} %get-tuple-element.24), channel_id=1, source_target_pairs={{0,2},{1,3},{2,4},{3,5},{4,6},{5,7},{6,8},{7,9},{8,10},{9,11},{10,... | collective-permute-start | bytes 405512 | tf_op jit(solution)/shard_map/ppermute | solution.py:46
  14.5 2.4 %collective-permute-start.2 = (bf16[528,128]{1,0:T(8,128)(2,1)S(1)}, bf16[528,128]{1,0:T(8,128)(2,1)S(1)}, u32[]{:S(2)}, u32[]{:S(2)}) collective-permute-start(bf16[528,128]{1,0:T(8,128)(2,1)S(1)} %get-tuple-element.23), channel_id=1, source_target_pairs={{0,3},{1,4},{2,5},{3,6},{4,7},{5,8},{6,9},{7,10},{8,11},{9,12},{10... | collective-permute-start | bytes 405512 | tf_op jit(solution)/shard_map/ppermute | solution.py:46
  17.0 1.6 %collective-permute-start.3 = (bf16[528,128]{1,0:T(8,128)(2,1)S(1)}, bf16[528,128]{1,0:T(8,128)(2,1)S(1)}, u32[]{:S(2)}, u32[]{:S(2)}) collective-permute-start(bf16[528,128]{1,0:T(8,128)(2,1)S(1)} %get-tuple-element.22), channel_id=1, source_target_pairs={{0,4},{1,5},{2,6},{3,7},{4,8},{5,9},{6,10},{7,11},{8,12},{9,13},{1... | collective-permute-start | bytes 405512 | tf_op jit(solution)/shard_map/ppermute | solution.py:46
  18.5 0.2 collective-permute-start.4
  18.8 1.4 %collective-permute-done = bf16[528,128]{1,0:T(8,128)(2,1)S(1)} collective-permute-done((bf16[528,128]{1,0:T(8,128)(2,1)S(1)}, bf16[528,128]{1,0:T(8,128)(2,1)S(1)}, u32[]{:S(2)}, u32[]{:S(2)}) %collective-permute-start) | collective-permute-done | bytes 135200 | tf_op jit(solution)/shard_map/ppermute | solution.py:46
  20.2 0.6 collective-permute-start.5
  20.8 1.3 collective-permute-done.1
  22.0 2.4 %collective-permute-start.6 = (bf16[528,128]{1,0:T(8,128)(2,1)S(1)}, bf16[528,128]{1,0:T(8,128)(2,1)S(1)}, u32[]{:S(2)}, u32[]{:S(2)}) collective-permute-start(bf16[528,128]{1,0:T(8,128)(2,1)S(1)} %get-tuple-element.19), channel_id=1, source_target_pairs={{0,7},{1,8},{2,9},{3,10},{4,11},{5,12},{6,13},{7,14},{8,15},{9,0},... | collective-permute-start | bytes 405512 | tf_op jit(solution)/shard_map/ppermute | solution.py:46
  24.4 1.6 %collective-permute-start.7 = (bf16[528,128]{1,0:T(8,128)(2,1)S(1)}, bf16[528,128]{1,0:T(8,128)(2,1)S(1)}, u32[]{:S(2)}, u32[]{:S(2)}) collective-permute-start(bf16[528,128]{1,0:T(8,128)(2,1)S(1)} %get-tuple-element.18), channel_id=1, source_target_pairs={{0,8},{1,9},{2,10},{3,11},{4,12},{5,13},{6,14},{7,15},{8,0},{9,1},... | collective-permute-start | bytes 405512 | tf_op jit(solution)/shard_map/ppermute | solution.py:46
  26.1 1.1 collective-permute-start.8
  27.2 17.0 %collective-permute-done.4 = bf16[528,128]{1,0:T(8,128)(2,1)S(1)} collective-permute-done((bf16[528,128]{1,0:T(8,128)(2,1)S(1)}, bf16[528,128]{1,0:T(8,128)(2,1)S(1)}, u32[]{:S(2)}, u32[]{:S(2)}) %collective-permute-start.4) | collective-permute-done | bytes 135200 | tf_op jit(solution)/shard_map/ppermute | solution.py:46
  44.2 0.2 collective-permute-done.5
  44.4 3.0 %collective-permute-start.10 = (bf16[528,128]{1,0:T(8,128)(2,1)S(1)}, bf16[528,128]{1,0:T(8,128)(2,1)S(1)}, u32[]{:S(2)}, u32[]{:S(2)}) collective-permute-start(bf16[528,128]{1,0:T(8,128)(2,1)S(1)} %get-tuple-element.15), channel_id=1, source_target_pairs={{0,11},{1,12},{2,13},{3,14},{4,15},{5,0},{6,1},{7,2},{8,3},{9,4},{... | collective-permute-start | bytes 405512 | tf_op jit(solution)/shard_map/ppermute | solution.py:46
  47.4 6.4 %collective-permute-start.11 = (bf16[528,128]{1,0:T(8,128)(2,1)S(1)}, bf16[528,128]{1,0:T(8,128)(2,1)S(1)}, u32[]{:S(2)}, u32[]{:S(2)}) collective-permute-start(bf16[528,128]{1,0:T(8,128)(2,1)S(1)} %get-tuple-element.14), channel_id=1, source_target_pairs={{0,12},{1,13},{2,14},{3,15},{4,0},{5,1},{6,2},{7,3},{8,4},{9,5},{1... | collective-permute-start | bytes 405512 | tf_op jit(solution)/shard_map/ppermute | solution.py:46
  53.8 1.4 %collective-permute-start.12 = (bf16[528,128]{1,0:T(8,128)(2,1)S(1)}, bf16[528,128]{1,0:T(8,128)(2,1)S(1)}, u32[]{:S(2)}, u32[]{:S(2)}) collective-permute-start(bf16[528,128]{1,0:T(8,128)(2,1)S(1)} %get-tuple-element.13), channel_id=1, source_target_pairs={{0,13},{1,14},{2,15},{3,0},{4,1},{5,2},{6,3},{7,4},{8,5},{9,6},{10... | collective-permute-start | bytes 405512 | tf_op jit(solution)/shard_map/ppermute | solution.py:46
  55.3 4.9 %collective-permute-start.13 = (bf16[528,128]{1,0:T(8,128)(2,1)S(1)}, bf16[528,128]{1,0:T(8,128)(2,1)S(1)}, u32[]{:S(2)}, u32[]{:S(2)}) collective-permute-start(bf16[528,128]{1,0:T(8,128)(2,1)S(1)} %get-tuple-element.12), channel_id=1, source_target_pairs={{0,14},{1,15},{2,0},{3,1},{4,2},{5,3},{6,4},{7,5},{8,6},{9,7},{10,... | collective-permute-start | bytes 405512 | tf_op jit(solution)/shard_map/ppermute | solution.py:46
  60.2 4.5 %collective-permute-start.14 = (bf16[528,128]{1,0:T(8,128)(2,1)S(1)}, bf16[528,128]{1,0:T(8,128)(2,1)S(1)}, u32[]{:S(2)}, u32[]{:S(2)}) collective-permute-start(bf16[528,128]{1,0:T(8,128)(2,1)S(1)} %get-tuple-element.11), channel_id=1, source_target_pairs={{0,15},{1,0},{2,1},{3,2},{4,3},{5,4},{6,5},{7,6},{8,7},{9,8},{10,9... | collective-permute-start | bytes 405512 | tf_op jit(solution)/shard_map/ppermute | solution.py:46
  64.9 2.8 %collective-permute-done.13 = bf16[528,128]{1,0:T(8,128)(2,1)S(1)} collective-permute-done((bf16[528,128]{1,0:T(8,128)(2,1)S(1)}, bf16[528,128]{1,0:T(8,128)(2,1)S(1)}, u32[]{:S(2)}, u32[]{:S(2)}) %collective-permute-start.13) | collective-permute-done | bytes 135200 | tf_op jit(solution)/shard_map/ppermute | solution.py:46
  67.7 0.4 collective-permute-done.14
  68.1 0.2 slice.196
  68.3 0.1 copy.45
  68.6 0.2 copy-done.4
  68.8 1.2 fusion.15
  70.2 1.0 gather_fusion.2
  71.2 1.1 fusion.74
  72.3 4.6 %collective-permute-start.15 = (bf16[512,128]{1,0:T(8,128)(2,1)}, bf16[512,128]{1,0:T(8,128)(2,1)S(1)}, u32[]{:S(2)}, u32[]{:S(2)}) collective-permute-start(bf16[512,128]{1,0:T(8,128)(2,1)} %bitcast.51), channel_id=1, source_target_pairs={{0,15},{1,0},{2,1},{3,2},{4,3},{5,4},{6,5},{7,6},{8,7},{9,8},{10,9... | collective-permute-start | bytes 393224 | tf_op jit(solution)/shard_map/ppermute | solution.py:46
  76.9 2.6 %collective-permute-start.19 = (bf16[512,128]{1,0:T(8,128)(2,1)}, bf16[512,128]{1,0:T(8,128)(2,1)S(1)}, u32[]{:S(2)}, u32[]{:S(2)}) collective-permute-start(bf16[512,128]{1,0:T(8,128)(2,1)} %bitcast.59), channel_id=1, source_target_pairs={{0,11},{1,12},{2,13},{3,14},{4,15},{5,0},{6,1},{7,2},{8,3},{9,4},{... | collective-permute-start | bytes 393224 | tf_op jit(solution)/shard_map/ppermute | solution.py:46
  79.5 0.7 fusion.63
  80.9 0.2 collective-permute-done.15
  81.1 0.6 copy-done.3
  81.8 2.8 %collective-permute-start.20 = (bf16[512,128]{1,0:T(8,128)(2,1)}, bf16[512,128]{1,0:T(8,128)(2,1)S(1)}, u32[]{:S(2)}, u32[]{:S(2)}) collective-permute-start(bf16[512,128]{1,0:T(8,128)(2,1)} %bitcast.202), channel_id=1, source_target_pairs={{0,10},{1,11},{2,12},{3,13},{4,14},{5,15},{6,0},{7,1},{8,2},{9,3},... | collective-permute-start | bytes 393224 | tf_op jit(solution)/shard_map/ppermute | solution.py:46
  84.5 0.9 bitcast_dynamic-update-slice_fusion.29
  85.5 0.6 copy-done.2
  86.1 0.2 collective-permute-start.21
  86.3 0.9 bitcast_dynamic-update-slice_fusion.28
  87.2 2.2 %collective-permute-start.22 = (bf16[512,128]{1,0:T(8,128)(2,1)}, bf16[512,128]{1,0:T(8,128)(2,1)S(1)}, u32[]{:S(2)}, u32[]{:S(2)}) collective-permute-start(bf16[512,128]{1,0:T(8,128)(2,1)} %bitcast.200), channel_id=1, source_target_pairs={{0,8},{1,9},{2,10},{3,11},{4,12},{5,13},{6,14},{7,15},{8,0},{9,1},... | collective-permute-start | bytes 393224 | tf_op jit(solution)/shard_map/ppermute | solution.py:46
  89.4 0.9 bitcast_dynamic-update-slice_fusion.27
  90.4 2.4 %collective-permute-start.23 = (bf16[512,128]{1,0:T(8,128)(2,1)}, bf16[512,128]{1,0:T(8,128)(2,1)S(1)}, u32[]{:S(2)}, u32[]{:S(2)}) collective-permute-start(bf16[512,128]{1,0:T(8,128)(2,1)} %bitcast.199), channel_id=1, source_target_pairs={{0,7},{1,8},{2,9},{3,10},{4,11},{5,12},{6,13},{7,14},{8,15},{9,0},... | collective-permute-start | bytes 393224 | tf_op jit(solution)/shard_map/ppermute | solution.py:46
  92.8 2.8 %collective-permute-start.24 = (bf16[512,128]{1,0:T(8,128)(2,1)}, bf16[512,128]{1,0:T(8,128)(2,1)S(1)}, u32[]{:S(2)}, u32[]{:S(2)}) collective-permute-start(bf16[512,128]{1,0:T(8,128)(2,1)} %bitcast.198), channel_id=1, source_target_pairs={{0,6},{1,7},{2,8},{3,9},{4,10},{5,11},{6,12},{7,13},{8,14},{9,15},... | collective-permute-start | bytes 393224 | tf_op jit(solution)/shard_map/ppermute | solution.py:46
  95.6 8.6 %collective-permute-start.25 = (bf16[512,128]{1,0:T(8,128)(2,1)}, bf16[512,128]{1,0:T(8,128)(2,1)S(1)}, u32[]{:S(2)}, u32[]{:S(2)}) collective-permute-start(bf16[512,128]{1,0:T(8,128)(2,1)} %bitcast.197), channel_id=1, source_target_pairs={{0,5},{1,6},{2,7},{3,8},{4,9},{5,10},{6,11},{7,12},{8,13},{9,14},{... | collective-permute-start | bytes 393224 | tf_op jit(solution)/shard_map/ppermute | solution.py:46
  104.3 5.7 %collective-permute-start.26 = (bf16[512,128]{1,0:T(8,128)(2,1)S(1)}, bf16[512,128]{1,0:T(8,128)(2,1)S(1)}, u32[]{:S(2)}, u32[]{:S(2)}) collective-permute-start(bf16[512,128]{1,0:T(8,128)(2,1)S(1)} %bitcast.196), channel_id=1, source_target_pairs={{0,4},{1,5},{2,6},{3,7},{4,8},{5,9},{6,10},{7,11},{8,12},{9,13},{1... | collective-permute-start | bytes 393224 | tf_op jit(solution)/shard_map/ppermute | solution.py:46
  110.0 5.8 %collective-permute-done.22 = bf16[512,128]{1,0:T(8,128)(2,1)S(1)} collective-permute-done((bf16[512,128]{1,0:T(8,128)(2,1)}, bf16[512,128]{1,0:T(8,128)(2,1)S(1)}, u32[]{:S(2)}, u32[]{:S(2)}) %collective-permute-start.22) | collective-permute-done | bytes 131104 | tf_op jit(solution)/shard_map/ppermute | solution.py:46
  115.8 3.7 %collective-permute-done.23 = bf16[512,128]{1,0:T(8,128)(2,1)S(1)} collective-permute-done((bf16[512,128]{1,0:T(8,128)(2,1)}, bf16[512,128]{1,0:T(8,128)(2,1)S(1)}, u32[]{:S(2)}, u32[]{:S(2)}) %collective-permute-start.23) | collective-permute-done | bytes 131104 | tf_op jit(solution)/shard_map/ppermute | solution.py:46
  119.8 2.2 %collective-permute-done.27 = bf16[512,128]{1,0:T(8,128)(2,1)S(1)} collective-permute-done((bf16[512,128]{1,0:T(8,128)(2,1)S(1)}, bf16[512,128]{1,0:T(8,128)(2,1)S(1)}, u32[]{:S(2)}, u32[]{:S(2)}) %collective-permute-start.27) | collective-permute-done | bytes 131104 | tf_op jit(solution)/shard_map/ppermute | solution.py:46
  122.0 7.1 %collective-permute-done.28 = bf16[512,128]{1,0:T(8,128)(2,1)S(1)} collective-permute-done((bf16[512,128]{1,0:T(8,128)(2,1)S(1)}, bf16[512,128]{1,0:T(8,128)(2,1)S(1)}, u32[]{:S(2)}, u32[]{:S(2)}) %collective-permute-start.28) | collective-permute-done | bytes 131104 | tf_op jit(solution)/shard_map/ppermute | solution.py:46
  129.2 0.7 gather_fusion.3
  129.9 0.4 fusion.11
  130.3 0.2 pad_maximum_fusion
  130.5 1.3 copy-done
  131.8 1.1 fusion.23
  132.9 0.8 copy.52
  (86 shorter events, 1.5 us)
Async XLA Ops:
  0.0 6.8 %copy-start.1 = (f32[2,128,128]{2,1,0:T(8,128)S(1)}, f32[2,128,128]{2,1,0:T(8,128)}, u32[]{:S(2)}) copy-start(f32[2,128,128]{2,1,0:T(8,128)} %param.4) | copy-start | bytes 393220
  11.4 8.8 %collective-permute-start = (bf16[528,128]{1,0:T(8,128)(2,1)S(1)}, bf16[528,128]{1,0:T(8,128)(2,1)S(1)}, u32[]{:S(2)}, u32[]{:S(2)}) collective-permute-start(bf16[528,128]{1,0:T(8,128)(2,1)S(1)} %get-tuple-element.25), channel_id=1, source_target_pairs={{0,1},{1,2},{2,3},{3,4},{4,5},{5,6},{6,7},{7,8},{8,9},{9,10},{10,1... | collective-permute-start | bytes 405512 | tf_op jit(solution)/shard_map/ppermute | solution.py:46
  12.0 10.0 %collective-permute-start.1 = (bf16[528,128]{1,0:T(8,128)(2,1)S(1)}, bf16[528,128]{1,0:T(8,128)(2,1)S(1)}, u32[]{:S(2)}, u32[]{:S(2)}) collective-permute-start(bf16[528,128]{1,0:T(8,128)(2,1)S(1)} %get-tuple-element.24), channel_id=1, source_target_pairs={{0,2},{1,3},{2,4},{3,5},{4,6},{5,7},{6,8},{7,9},{8,10},{9,11},{10,... | collective-permute-start | bytes 405512 | tf_op jit(solution)/shard_map/ppermute | solution.py:46
  14.5 9.9 %collective-permute-start.2 = (bf16[528,128]{1,0:T(8,128)(2,1)S(1)}, bf16[528,128]{1,0:T(8,128)(2,1)S(1)}, u32[]{:S(2)}, u32[]{:S(2)}) collective-permute-start(bf16[528,128]{1,0:T(8,128)(2,1)S(1)} %get-tuple-element.23), channel_id=1, source_target_pairs={{0,3},{1,4},{2,5},{3,6},{4,7},{5,8},{6,9},{7,10},{8,11},{9,12},{10... | collective-permute-start | bytes 405512 | tf_op jit(solution)/shard_map/ppermute | solution.py:46
  17.0 9.1 %collective-permute-start.3 = (bf16[528,128]{1,0:T(8,128)(2,1)S(1)}, bf16[528,128]{1,0:T(8,128)(2,1)S(1)}, u32[]{:S(2)}, u32[]{:S(2)}) collective-permute-start(bf16[528,128]{1,0:T(8,128)(2,1)S(1)} %get-tuple-element.22), channel_id=1, source_target_pairs={{0,4},{1,5},{2,6},{3,7},{4,8},{5,9},{6,10},{7,11},{8,12},{9,13},{1... | collective-permute-start | bytes 405512 | tf_op jit(solution)/shard_map/ppermute | solution.py:46
  18.5 25.6 %collective-permute-start.4 = (bf16[528,128]{1,0:T(8,128)(2,1)S(1)}, bf16[528,128]{1,0:T(8,128)(2,1)S(1)}, u32[]{:S(2)}, u32[]{:S(2)}) collective-permute-start(bf16[528,128]{1,0:T(8,128)(2,1)S(1)} %get-tuple-element.21), channel_id=1, source_target_pairs={{0,5},{1,6},{2,7},{3,8},{4,9},{5,10},{6,11},{7,12},{8,13},{9,14},{... | collective-permute-start | bytes 405512 | tf_op jit(solution)/shard_map/ppermute | solution.py:46
  20.2 24.2 %collective-permute-start.5 = (bf16[528,128]{1,0:T(8,128)(2,1)S(1)}, bf16[528,128]{1,0:T(8,128)(2,1)S(1)}, u32[]{:S(2)}, u32[]{:S(2)}) collective-permute-start(bf16[528,128]{1,0:T(8,128)(2,1)S(1)} %get-tuple-element.20), channel_id=1, source_target_pairs={{0,6},{1,7},{2,8},{3,9},{4,10},{5,11},{6,12},{7,13},{8,14},{9,15},... | collective-permute-start | bytes 405512 | tf_op jit(solution)/shard_map/ppermute | solution.py:46
  22.0 25.4 %collective-permute-start.6 = (bf16[528,128]{1,0:T(8,128)(2,1)S(1)}, bf16[528,128]{1,0:T(8,128)(2,1)S(1)}, u32[]{:S(2)}, u32[]{:S(2)}) collective-permute-start(bf16[528,128]{1,0:T(8,128)(2,1)S(1)} %get-tuple-element.19), channel_id=1, source_target_pairs={{0,7},{1,8},{2,9},{3,10},{4,11},{5,12},{6,13},{7,14},{8,15},{9,0},... | collective-permute-start | bytes 405512 | tf_op jit(solution)/shard_map/ppermute | solution.py:46
  24.4 29.4 %collective-permute-start.7 = (bf16[528,128]{1,0:T(8,128)(2,1)S(1)}, bf16[528,128]{1,0:T(8,128)(2,1)S(1)}, u32[]{:S(2)}, u32[]{:S(2)}) collective-permute-start(bf16[528,128]{1,0:T(8,128)(2,1)S(1)} %get-tuple-element.18), channel_id=1, source_target_pairs={{0,8},{1,9},{2,10},{3,11},{4,12},{5,13},{6,14},{7,15},{8,0},{9,1},... | collective-permute-start | bytes 405512 | tf_op jit(solution)/shard_map/ppermute | solution.py:46
  26.1 29.2 %collective-permute-start.8 = (bf16[528,128]{1,0:T(8,128)(2,1)S(1)}, bf16[528,128]{1,0:T(8,128)(2,1)S(1)}, u32[]{:S(2)}, u32[]{:S(2)}) collective-permute-start(bf16[528,128]{1,0:T(8,128)(2,1)S(1)} %get-tuple-element.17), channel_id=1, source_target_pairs={{0,9},{1,10},{2,11},{3,12},{4,13},{5,14},{6,15},{7,0},{8,1},{9,2},... | collective-permute-start | bytes 405512 | tf_op jit(solution)/shard_map/ppermute | solution.py:46
  44.2 16.0 %collective-permute-start.9 = (bf16[528,128]{1,0:T(8,128)(2,1)S(1)}, bf16[528,128]{1,0:T(8,128)(2,1)S(1)}, u32[]{:S(2)}, u32[]{:S(2)}) collective-permute-start(bf16[528,128]{1,0:T(8,128)(2,1)S(1)} %get-tuple-element.16), channel_id=1, source_target_pairs={{0,10},{1,11},{2,12},{3,13},{4,14},{5,15},{6,0},{7,1},{8,2},{9,3},... | collective-permute-start | bytes 405512 | tf_op jit(solution)/shard_map/ppermute | solution.py:46
  44.4 20.4 %collective-permute-start.10 = (bf16[528,128]{1,0:T(8,128)(2,1)S(1)}, bf16[528,128]{1,0:T(8,128)(2,1)S(1)}, u32[]{:S(2)}, u32[]{:S(2)}) collective-permute-start(bf16[528,128]{1,0:T(8,128)(2,1)S(1)} %get-tuple-element.15), channel_id=1, source_target_pairs={{0,11},{1,12},{2,13},{3,14},{4,15},{5,0},{6,1},{7,2},{8,3},{9,4},{... | collective-permute-start | bytes 405512 | tf_op jit(solution)/shard_map/ppermute | solution.py:46
  47.4 17.4 %collective-permute-start.11 = (bf16[528,128]{1,0:T(8,128)(2,1)S(1)}, bf16[528,128]{1,0:T(8,128)(2,1)S(1)}, u32[]{:S(2)}, u32[]{:S(2)}) collective-permute-start(bf16[528,128]{1,0:T(8,128)(2,1)S(1)} %get-tuple-element.14), channel_id=1, source_target_pairs={{0,12},{1,13},{2,14},{3,15},{4,0},{5,1},{6,2},{7,3},{8,4},{9,5},{1... | collective-permute-start | bytes 405512 | tf_op jit(solution)/shard_map/ppermute | solution.py:46
  53.8 11.0 %collective-permute-start.12 = (bf16[528,128]{1,0:T(8,128)(2,1)S(1)}, bf16[528,128]{1,0:T(8,128)(2,1)S(1)}, u32[]{:S(2)}, u32[]{:S(2)}) collective-permute-start(bf16[528,128]{1,0:T(8,128)(2,1)S(1)} %get-tuple-element.13), channel_id=1, source_target_pairs={{0,13},{1,14},{2,15},{3,0},{4,1},{5,2},{6,3},{7,4},{8,5},{9,6},{10... | collective-permute-start | bytes 405512 | tf_op jit(solution)/shard_map/ppermute | solution.py:46
  55.3 12.4 %collective-permute-start.13 = (bf16[528,128]{1,0:T(8,128)(2,1)S(1)}, bf16[528,128]{1,0:T(8,128)(2,1)S(1)}, u32[]{:S(2)}, u32[]{:S(2)}) collective-permute-start(bf16[528,128]{1,0:T(8,128)(2,1)S(1)} %get-tuple-element.12), channel_id=1, source_target_pairs={{0,14},{1,15},{2,0},{3,1},{4,2},{5,3},{6,4},{7,5},{8,6},{9,7},{10,... | collective-permute-start | bytes 405512 | tf_op jit(solution)/shard_map/ppermute | solution.py:46
  60.2 7.9 %collective-permute-start.14 = (bf16[528,128]{1,0:T(8,128)(2,1)S(1)}, bf16[528,128]{1,0:T(8,128)(2,1)S(1)}, u32[]{:S(2)}, u32[]{:S(2)}) collective-permute-start(bf16[528,128]{1,0:T(8,128)(2,1)S(1)} %get-tuple-element.11), channel_id=1, source_target_pairs={{0,15},{1,0},{2,1},{3,2},{4,3},{5,4},{6,5},{7,6},{8,7},{9,8},{10,9... | collective-permute-start | bytes 405512 | tf_op jit(solution)/shard_map/ppermute | solution.py:46
  68.1 0.7 copy-start.4
  72.3 8.9 %collective-permute-start.15 = (bf16[512,128]{1,0:T(8,128)(2,1)}, bf16[512,128]{1,0:T(8,128)(2,1)S(1)}, u32[]{:S(2)}, u32[]{:S(2)}) collective-permute-start(bf16[512,128]{1,0:T(8,128)(2,1)} %bitcast.51), channel_id=1, source_target_pairs={{0,15},{1,0},{2,1},{3,2},{4,3},{5,4},{6,5},{7,6},{8,7},{9,8},{10,9... | collective-permute-start | bytes 393224 | tf_op jit(solution)/shard_map/ppermute | solution.py:46
  76.9 8.6 %collective-permute-start.16 = (bf16[512,128]{1,0:T(8,128)(2,1)}, bf16[512,128]{1,0:T(8,128)(2,1)S(1)}, u32[]{:S(2)}, u32[]{:S(2)}) collective-permute-start(bf16[512,128]{1,0:T(8,128)(2,1)} %bitcast.53), channel_id=1, source_target_pairs={{0,14},{1,15},{2,0},{3,1},{4,2},{5,3},{6,4},{7,5},{8,6},{9,7},{10,... | collective-permute-start | bytes 393224 | tf_op jit(solution)/shard_map/ppermute | solution.py:46
  76.9 10.4 %collective-permute-start.17 = (bf16[512,128]{1,0:T(8,128)(2,1)}, bf16[512,128]{1,0:T(8,128)(2,1)}, u32[]{:S(2)}, u32[]{:S(2)}) collective-permute-start(bf16[512,128]{1,0:T(8,128)(2,1)} %bitcast.55), channel_id=1, source_target_pairs={{0,13},{1,14},{2,15},{3,0},{4,1},{5,2},{6,3},{7,4},{8,5},{9,6},{10... | collective-permute-start | bytes 393224 | tf_op jit(solution)/shard_map/ppermute | solution.py:46
  76.9 13.5 %collective-permute-start.18 = (bf16[512,128]{1,0:T(8,128)(2,1)}, bf16[512,128]{1,0:T(8,128)(2,1)S(1)}, u32[]{:S(2)}, u32[]{:S(2)}) collective-permute-start(bf16[512,128]{1,0:T(8,128)(2,1)} %bitcast.57), channel_id=1, source_target_pairs={{0,12},{1,13},{2,14},{3,15},{4,0},{5,1},{6,2},{7,3},{8,4},{9,5},{1... | collective-permute-start | bytes 393224 | tf_op jit(solution)/shard_map/ppermute | solution.py:46
  76.9 15.9 %collective-permute-start.19 = (bf16[512,128]{1,0:T(8,128)(2,1)}, bf16[512,128]{1,0:T(8,128)(2,1)S(1)}, u32[]{:S(2)}, u32[]{:S(2)}) collective-permute-start(bf16[512,128]{1,0:T(8,128)(2,1)} %bitcast.59), channel_id=1, source_target_pairs={{0,11},{1,12},{2,13},{3,14},{4,15},{5,0},{6,1},{7,2},{8,3},{9,4},{... | collective-permute-start | bytes 393224 | tf_op jit(solution)/shard_map/ppermute | solution.py:46
  81.1 0.6 copy-start.3
  81.8 13.9 %collective-permute-start.20 = (bf16[512,128]{1,0:T(8,128)(2,1)}, bf16[512,128]{1,0:T(8,128)(2,1)S(1)}, u32[]{:S(2)}, u32[]{:S(2)}) collective-permute-start(bf16[512,128]{1,0:T(8,128)(2,1)} %bitcast.202), channel_id=1, source_target_pairs={{0,10},{1,11},{2,12},{3,13},{4,14},{5,15},{6,0},{7,1},{8,2},{9,3},... | collective-permute-start | bytes 393224 | tf_op jit(solution)/shard_map/ppermute | solution.py:46
  85.4 0.7 copy-start.2
  86.1 18.2 %collective-permute-start.21 = (bf16[512,128]{1,0:T(8,128)(2,1)}, bf16[512,128]{1,0:T(8,128)(2,1)S(1)}, u32[]{:S(2)}, u32[]{:S(2)}) collective-permute-start(bf16[512,128]{1,0:T(8,128)(2,1)} %bitcast.201), channel_id=1, source_target_pairs={{0,9},{1,10},{2,11},{3,12},{4,13},{5,14},{6,15},{7,0},{8,1},{9,2},... | collective-permute-start | bytes 393224 | tf_op jit(solution)/shard_map/ppermute | solution.py:46
  87.2 28.6 %collective-permute-start.22 = (bf16[512,128]{1,0:T(8,128)(2,1)}, bf16[512,128]{1,0:T(8,128)(2,1)S(1)}, u32[]{:S(2)}, u32[]{:S(2)}) collective-permute-start(bf16[512,128]{1,0:T(8,128)(2,1)} %bitcast.200), channel_id=1, source_target_pairs={{0,8},{1,9},{2,10},{3,11},{4,12},{5,13},{6,14},{7,15},{8,0},{9,1},... | collective-permute-start | bytes 393224 | tf_op jit(solution)/shard_map/ppermute | solution.py:46
  90.4 29.2 %collective-permute-start.23 = (bf16[512,128]{1,0:T(8,128)(2,1)}, bf16[512,128]{1,0:T(8,128)(2,1)S(1)}, u32[]{:S(2)}, u32[]{:S(2)}) collective-permute-start(bf16[512,128]{1,0:T(8,128)(2,1)} %bitcast.199), channel_id=1, source_target_pairs={{0,7},{1,8},{2,9},{3,10},{4,11},{5,12},{6,13},{7,14},{8,15},{9,0},... | collective-permute-start | bytes 393224 | tf_op jit(solution)/shard_map/ppermute | solution.py:46
  92.8 26.8 %collective-permute-start.24 = (bf16[512,128]{1,0:T(8,128)(2,1)}, bf16[512,128]{1,0:T(8,128)(2,1)S(1)}, u32[]{:S(2)}, u32[]{:S(2)}) collective-permute-start(bf16[512,128]{1,0:T(8,128)(2,1)} %bitcast.198), channel_id=1, source_target_pairs={{0,6},{1,7},{2,8},{3,9},{4,10},{5,11},{6,12},{7,13},{8,14},{9,15},... | collective-permute-start | bytes 393224 | tf_op jit(solution)/shard_map/ppermute | solution.py:46
  95.6 24.1 %collective-permute-start.25 = (bf16[512,128]{1,0:T(8,128)(2,1)}, bf16[512,128]{1,0:T(8,128)(2,1)S(1)}, u32[]{:S(2)}, u32[]{:S(2)}) collective-permute-start(bf16[512,128]{1,0:T(8,128)(2,1)} %bitcast.197), channel_id=1, source_target_pairs={{0,5},{1,6},{2,7},{3,8},{4,9},{5,10},{6,11},{7,12},{8,13},{9,14},{... | collective-permute-start | bytes 393224 | tf_op jit(solution)/shard_map/ppermute | solution.py:46
  104.3 15.5 %collective-permute-start.26 = (bf16[512,128]{1,0:T(8,128)(2,1)S(1)}, bf16[512,128]{1,0:T(8,128)(2,1)S(1)}, u32[]{:S(2)}, u32[]{:S(2)}) collective-permute-start(bf16[512,128]{1,0:T(8,128)(2,1)S(1)} %bitcast.196), channel_id=1, source_target_pairs={{0,4},{1,5},{2,6},{3,7},{4,8},{5,9},{6,10},{7,11},{8,12},{9,13},{1... | collective-permute-start | bytes 393224 | tf_op jit(solution)/shard_map/ppermute | solution.py:46
  115.8 6.2 %collective-permute-start.27 = (bf16[512,128]{1,0:T(8,128)(2,1)S(1)}, bf16[512,128]{1,0:T(8,128)(2,1)S(1)}, u32[]{:S(2)}, u32[]{:S(2)}) collective-permute-start(bf16[512,128]{1,0:T(8,128)(2,1)S(1)} %bitcast.195), channel_id=1, source_target_pairs={{0,3},{1,4},{2,5},{3,6},{4,7},{5,8},{6,9},{7,10},{8,11},{9,12},{10... | collective-permute-start | bytes 393224 | tf_op jit(solution)/shard_map/ppermute | solution.py:46
  119.6 9.5 %collective-permute-start.28 = (bf16[512,128]{1,0:T(8,128)(2,1)S(1)}, bf16[512,128]{1,0:T(8,128)(2,1)S(1)}, u32[]{:S(2)}, u32[]{:S(2)}) collective-permute-start(bf16[512,128]{1,0:T(8,128)(2,1)S(1)} %bitcast.194), channel_id=1, source_target_pairs={{0,2},{1,3},{2,4},{3,5},{4,6},{5,7},{6,8},{7,9},{8,10},{9,11},{10,... | collective-permute-start | bytes 393224 | tf_op jit(solution)/shard_map/ppermute | solution.py:46
  119.6 9.5 %collective-permute-start.29 = (bf16[512,128]{1,0:T(8,128)(2,1)S(1)}, bf16[512,128]{1,0:T(8,128)(2,1)S(1)}, u32[]{:S(2)}, u32[]{:S(2)}) collective-permute-start(bf16[512,128]{1,0:T(8,128)(2,1)S(1)} %bitcast.193), channel_id=1, source_target_pairs={{0,1},{1,2},{2,3},{3,4},{4,5},{5,6},{6,7},{7,8},{8,9},{9,10},{10,1... | collective-permute-start | bytes 393224 | tf_op jit(solution)/shard_map/ppermute | solution.py:46
  130.3 1.5 %copy-start = (bf16[26,2,128,128]{3,2,1,0:T(8,128)(2,1)S(1)}, bf16[26,2,128,128]{3,2,1,0:T(8,128)(2,1)}, u32[]{:S(2)}) copy-start(bf16[26,2,128,128]{3,2,1,0:T(8,128)(2,1)} %param.5) | copy-start | bytes 5111812
